TPU v7x, 512 devices: a whole 4x4x16 slice. The times are simulated.
512 devices in a mesh: dp: 32 (over y, x, core), tensor: 16 (over z).
Axes of the slice: x: 4, y: 4, z: 16, core: 2. Of those that a mesh axis runs over, the one named last changes fastest.
Arguments:
- activations: bfloat16 [32768, 4096], P('dp', 'tensor'), may hold values from -40 to 40
- labels: int32 [32768], P('dp'), may hold values from 0 to 7, as said below
Outputs:
- covariance: float32 [4096, 4096], P('tensor', 'dp')
- cross_covariance: float32 [8, 4096], P(None, 'tensor')
Inputs may be any that keep to these rules, and one draw needn't show every extreme that they name: Every one of the 8 classes labels at least one token.
All inputs are finite; a program needn't handle non-finite values.
Results may differ from a plain program's by a relative error of at most 0.0003.
Values may be sent and summed in bfloat16 or wider, within the bound.
No kernel may reach another device: no remote copies, remote signals or barrier semaphores. Data moves between devices by JAX's collectives and lax.ppermute only.
A program may use at most 64 MiB of HBM per device.

v0:
```python
import jax
import jax.numpy as jnp
from jax import lax
from jax.sharding import PartitionSpec as P

D = 4096
CLASSES = 8


def body(activations, labels):
    tok_rows, slice_width = activations.shape
    token_total = tok_rows * lax.axis_size("dp")
    col_width = D // lax.axis_size("dp")
    classes = jnp.arange(CLASSES, dtype=jnp.int32)
    matches = labels[None, :] == classes[:, None]
    onehot = matches.astype(jnp.bfloat16)
    local_counts = jnp.sum(matches.astype(jnp.float32), axis=1)
    gathered = lax.all_gather(activations, "tensor", axis=1, tiled=True)
    gram_cols = lax.psum_scatter(
        lax.dot_general(
            gathered, activations, (((0,), (0,)), ((), ())), preferred_element_type=jnp.float32
        ),
        "dp",
        scatter_dimension=0,
        tiled=True,
    )
    slice_start = lax.axis_index("tensor") * slice_width
    wide_local = jnp.dot(onehot, gathered, preferred_element_type=jnp.float32)
    class_sums, class_counts = lax.psum((wide_local, local_counts), "dp")
    own_sums = lax.dynamic_slice_in_dim(class_sums, slice_start, slice_width, 1)
    overall_mean = jnp.sum(class_sums, axis=0) / token_total
    mean_rows = lax.dynamic_slice_in_dim(overall_mean, slice_start, slice_width, 0)
    mean_cols = lax.dynamic_slice_in_dim(
        overall_mean, lax.axis_index("dp") * col_width, col_width, 0
    )
    covariance = gram_cols.T / token_total - mean_rows[:, None] * mean_cols[None, :]
    cross_covariance = (own_sums - class_counts[:, None] * mean_rows[None, :]) / token_total
    return (covariance, cross_covariance)


def solution(mesh):
    in_specs = (P("dp", "tensor"), P("dp"))
    out_specs = (P("tensor", "dp"), P(None, "tensor"))
    return jax.shard_map(body, mesh=mesh, in_specs=in_specs, out_specs=out_specs, check_vma=False)
```

profile of v0, /device:TPU:6, one launch (start us, length us, event | category | flops | bytes accessed | tf_op | source)
XLA Modules:
  0.0 394.6 jit_solution(16058188507503878054)
XLA Ops:
  7.2 0.0 copy-start
  7.2 0.0 all-gather.2.cloned.1.call-start
  7.2 0.7 all-gather.2.cloned.1.call-update
  7.9 0.0 all-reduce.2.cloned.1.call-start
  8.0 135.1 %all-gather.2.cloned.1.call-done = bf16[1024,4096]{1,0:T(8,128)(2,1)} async-done(((bf16[1024,256]{1,0:T(8,128)(2,1)}), bf16[1024,4096]{1,0:T(8,128)(2,1)}) %all-gather.2.cloned.1.call-update) | async-done | bytes 8388624 | tf_op jit(solution)/shard_map/all_gather | solution.py:18
  143.0 5.2 %fusion = f32[8,4096]{1,0:T(8,128)} fusion(bf16[1024,4096]{1,0:T(8,128)(2,1)} %all-gather.2.cloned.1.call-done, s32[1024]{0:T(1024)} %param.3), kind=kOutput, calls=%fused_computation.3 | convolution fusion | flops 67117056 | bytes 8523776 | tf_op jit(solution)/shard_map/dot_general | solution.py:28
  148.3 0.0 all-reduce.2.cloned.1.call-update
  148.3 0.0 copy-start.1
  148.3 0.0 reduce-scatter.2.cloned.1.call-start
  148.4 0.0 copy-done
  148.4 7.8 %fusion.2 = f32[4096,256]{1,0:T(8,128)} fusion(bf16[1024,4096]{1,0:T(8,128)(2,1)} %all-gather.2.cloned.1.call-done, bf16[1024,256]{1,0:T(8,128)(2,1)S(1)} %copy-done), kind=kOutput, calls=%fused_computation.7 | convolution fusion | flops 2147483648 | bytes 13107200 | tf_op jit(solution)/shard_map/dot_general | solution.py:20
  156.2 0.0 reduce-scatter.2.cloned.1.call-update
  156.2 0.0 copy-done.1
  156.2 0.1 convert_reduce_fusion
  156.4 49.6 %psum.15 = f32[8]{0:T(128)S(1)} all-reduce(f32[8]{0:T(128)S(1)} %convert_reduce_fusion), channel_id=1, replica_groups=mesh['dp'=32,'tensor'=16] {'dp'}, use_global_device_ids=true, to_apply=%region_4.0 | all-reduce | flops 8 | bytes 64 | tf_op jit(solution)/shard_map/psum | solution.py:29
  206.0 71.6 %all-reduce.2.cloned.1.call-done = f32[8,4096]{1,0:T(8,128)} async-done(((f32[8,4096]{1,0:T(8,128)}), f32[8,4096]{1,0:T(8,128)}) %all-reduce.2.cloned.1.call-update) | async-done | bytes 131088 | tf_op jit(solution)/shard_map/psum | solution.py:29
  277.6 0.9 reduce_sum.18
  278.6 0.1 dynamic_slice.10
  278.7 0.1 dynamic_slice.9
  278.7 1.4 subtract_multiply_fusion
  280.1 106.2 %reduce-scatter.2.cloned.1.call-done = f32[128,256]{1,0:T(8,128)} async-done(((f32[4096,256]{1,0:T(8,128)}), f32[128,256]{1,0:T(8,128)}) %reduce-scatter.2.cloned.1.call-update) | async-done | bytes 131088 | tf_op jit(solution)/shard_map/reduce_scatter | solution.py:19
  386.3 1.0 bitcast_subtract_fusion
  387.3 0.8 copy.5
  (1 shorter events, 0.0 us)
Async XLA Ops:
  7.2 141.2 %copy-start = (bf16[1024,256]{1,0:T(8,128)(2,1)S(1)}, bf16[1024,256]{1,0:T(8,128)(2,1)}, u32[]{:S(2)}) copy-start(bf16[1024,256]{1,0:T(8,128)(2,1)} %param.2) | copy-start | bytes 1572868
  7.2 135.9 %all-gather.2.cloned.1.call-start = ((), (), s32[]{:S(2)}) async-start(), calls=%async_computation.1 | async-start | bytes 8912896 | tf_op jit(solution)/shard_map/all_gather | solution.py:18
  7.9 269.7 %all-reduce.2.cloned.1.call-start = ((), (), s32[]{:S(2)}) async-start(), calls=%async_computation.3 | async-start | bytes 262144 | tf_op jit(solution)/shard_map/psum | solution.py:29
  148.3 7.9 %copy-start.1 = (s32[1024]{0:T(1024)S(1)}, s32[1024]{0:T(1024)}, u32[]{:S(2)}) copy-start(s32[1024]{0:T(1024)} %param.3) | copy-start | bytes 12292
  148.3 238.0 %reduce-scatter.2.cloned.1.call-start = ((), (), s32[]{:S(2)}) async-start(), calls=%async_computation.2 | async-start | bytes 4325376 | tf_op jit(solution)/shard_map/reduce_scatter | solution.py:19
Sparse Core Ops, SparseCore 0:
  10.0 133.0 all-gather.1
  148.4 129.1 all-reduce.1
  282.2 104.1 reduce-scatter.1
where the time goes:
time: 395 us
  waiting for transfers between devices  314 us (79%)
  blocking collectives  49.6 us (13%)
  between operations  13.8 us (3%)
  matrix products  13.1 us (3%)
    all_gather x1, waiting for transfers between devices, body(): gathered = lax.all_gather(activations, 'tensor', axis=1, tiled=True)  135 us
    reduce_scatter x1, waiting for transfers between devices, body(): lax.psum_scatter(lax.dot_general(gathered, activations, (((0,), (0,)), ((...  106 us
    psum x1, waiting for transfers between devices, body(): class_sums, class_counts = lax.psum((wide_local, local_counts), 'dp')  71.6 us
    psum x1, blocking collectives, body(): class_sums, class_counts = lax.psum((wide_local, local_counts), 'dp')  49.6 us
  transfers between devices with their start and end apart: 3, of which 3 were waited for; matrix products, arithmetic and copies ran while one was open for 3% of the time, Pallas kernels for 0%

commit v1 on v0

--- a/solution.py
+++ b/solution.py
@@ -7,10 +7,21 @@
 CLASSES = 8
 
 
+def butterfly_sum(x, axis, n):
+    k = 1
+    while k < n:
+        perm = [(i, i ^ k) for i in range(n)]
+        x = x + lax.ppermute(x, axis, perm)
+        k *= 2
+    return x
+
+
 def body(activations, labels):
     tok_rows, slice_width = activations.shape
-    token_total = tok_rows * lax.axis_size("dp")
-    col_width = D // lax.axis_size("dp")
+    n_dp = lax.axis_size("dp")
+    assert n_dp & (n_dp - 1) == 0
+    token_total = tok_rows * n_dp
+    col_width = D // n_dp
     classes = jnp.arange(CLASSES, dtype=jnp.int32)
     matches = labels[None, :] == classes[:, None]
     onehot = matches.astype(jnp.bfloat16)
@@ -26,7 +37,12 @@
     )
     slice_start = lax.axis_index("tensor") * slice_width
     wide_local = jnp.dot(onehot, gathered, preferred_element_type=jnp.float32)
-    class_sums, class_counts = lax.psum((wide_local, local_counts), "dp")
+    stats = jnp.concatenate(
+        [wide_local, jnp.broadcast_to(local_counts[:, None], (CLASSES, 128))], axis=1
+    )
+    stats = butterfly_sum(stats, "dp", n_dp)
+    class_sums = stats[:, :D]
+    class_counts = stats[:, D]
     own_sums = lax.dynamic_slice_in_dim(class_sums, slice_start, slice_width, 1)
     overall_mean = jnp.sum(class_sums, axis=0) / token_total
     mean_rows = lax.dynamic_slice_in_dim(overall_mean, slice_start, slice_width, 0)

time: 395 us -> 262 us (0.66)
  the two profiles are of different devices: /device:TPU:6 before, /device:TPU:2 now
where the time goes in v1:
time: 262 us; the launch traced here: 261 us
  waiting for transfers between devices  215 us (82%)
  starting transfers between devices  16.3 us (6%)
  between operations  14.1 us (5%)
  matrix products  12.4 us (5%)
    all_gather x1, waiting for transfers between devices, body(): gathered = lax.all_gather(activations, 'tensor', axis=1, tiled=True)  135 us
    reduce_scatter x1, waiting for transfers between devices, body(): lax.psum_scatter(lax.dot_general(gathered, activations, (((0,), (0,)), ((...  61.4 us
    ppermute x5, waiting for transfers between devices, butterfly_sum(): x = x + lax.ppermute(x, axis, perm)  18.2 us
    ppermute x5, starting transfers between devices, butterfly_sum(): x = x + lax.ppermute(x, axis, perm)  16.2 us
    dot_general x1, matrix products, body(): lax.dot_general(gathered, activations, (((0,), (0,)), ((), ())), preferre...  7.84 us
  transfers between devices with their start and end apart: 7, of which 7 were waited for; matrix products, arithmetic and copies ran while one was open for 2% of the time, Pallas kernels for 0%

profile of v1, /device:TPU:2, one launch (start us, length us, event | category | flops | bytes accessed | tf_op | source)
XLA Modules:
  0.0 261.4 jit_solution(986602660060794046)
XLA Ops:
  7.2 0.0 all-gather.2.cloned.1.call-start
  7.2 0.7 all-gather.2.cloned.1.call-update
  7.9 0.0 copy-start
  7.9 0.0 reduce-scatter.2.cloned.1.call-start
  8.0 135.1 %all-gather.2.cloned.1.call-done = bf16[1024,4096]{1,0:T(8,128)(2,1)} async-done(((bf16[1024,256]{1,0:T(8,128)(2,1)}), bf16[1024,4096]{1,0:T(8,128)(2,1)}) %all-gather.2.cloned.1.call-update) | async-done | bytes 8388624 | tf_op jit(solution)/shard_map/all_gather | solution.py:29
  143.1 7.8 %fusion.4 = f32[4096,256]{1,0:T(8,128)} fusion(bf16[1024,4096]{1,0:T(8,128)(2,1)} %all-gather.2.cloned.1.call-done, bf16[1024,256]{1,0:T(8,128)(2,1)} %param.2), kind=kOutput, calls=%fused_computation.12 | convolution fusion | flops 2147483648 | bytes 13107200 | tf_op jit(solution)/shard_map/dot_general | solution.py:31
  150.9 0.0 reduce-scatter.2.cloned.1.call-update
  150.9 0.0 copy-done
  151.0 0.1 convert_reduce_fusion
  151.1 4.6 %fusion = f32[8,4096]{1,0:T(8,128)S(1)} fusion(bf16[1024,4096]{1,0:T(8,128)(2,1)} %all-gather.2.cloned.1.call-done, s32[1024]{0:T(1024)S(1)} %copy-done), kind=kOutput, calls=%fused_computation.4 | convolution fusion | flops 67117056 | bytes 8523776 | tf_op jit(solution)/shard_map/dot_general | solution.py:39
  155.7 0.1 broadcast_in_dim.2
  155.7 1.9 collective-permute-start
  157.7 1.3 collective-permute-done
  159.0 2.0 collective-permute-start.1
  161.0 5.5 %collective-permute-done.1 = f32[8,4224]{1,0:T(8,128)S(1)} collective-permute-done((f32[8,4224]{1,0:T(8,128)S(1)}, f32[8,4224]{1,0:T(8,128)S(1)}, u32[]{:S(2)}, u32[]{:S(2)}) %collective-permute-start.1) | collective-permute-done | bytes 135200 | tf_op jit(solution)/shard_map/ppermute | solution.py:14
  166.6 4.0 %collective-permute-start.2 = (f32[8,4224]{1,0:T(8,128)S(1)}, f32[8,4224]{1,0:T(8,128)S(1)}, u32[]{:S(2)}, u32[]{:S(2)}) collective-permute-start(f32[8,4224]{1,0:T(8,128)S(1)} %add.25), channel_id=1, source_target_pairs={{0,64},{16,80},{32,96},{48,112},{64,0},{80,16},{96,32},{112,48},{1... | collective-permute-start | bytes 405512 | tf_op jit(solution)/shard_map/ppermute | solution.py:14
  170.6 4.4 %collective-permute-done.2 = f32[8,4224]{1,0:T(8,128)S(1)} collective-permute-done((f32[8,4224]{1,0:T(8,128)S(1)}, f32[8,4224]{1,0:T(8,128)S(1)}, u32[]{:S(2)}, u32[]{:S(2)}) %collective-permute-start.2) | collective-permute-done | bytes 135200 | tf_op jit(solution)/shard_map/ppermute | solution.py:14
  175.0 3.4 %collective-permute-start.3 = (f32[8,4224]{1,0:T(8,128)S(1)}, f32[8,4224]{1,0:T(8,128)S(1)}, u32[]{:S(2)}, u32[]{:S(2)}) collective-permute-start(f32[8,4224]{1,0:T(8,128)S(1)} %add.26), channel_id=1, source_target_pairs={{0,128},{16,144},{32,160},{48,176},{64,192},{80,208},{96,224},{112... | collective-permute-start | bytes 405512 | tf_op jit(solution)/shard_map/ppermute | solution.py:14
  178.4 3.5 %collective-permute-done.3 = f32[8,4224]{1,0:T(8,128)S(1)} collective-permute-done((f32[8,4224]{1,0:T(8,128)S(1)}, f32[8,4224]{1,0:T(8,128)S(1)}, u32[]{:S(2)}, u32[]{:S(2)}) %collective-permute-start.3) | collective-permute-done | bytes 135200 | tf_op jit(solution)/shard_map/ppermute | solution.py:14
  181.9 4.9 %collective-permute-start.4 = (f32[8,4224]{1,0:T(8,128)S(1)}, f32[8,4224]{1,0:T(8,128)S(1)}, u32[]{:S(2)}, u32[]{:S(2)}) collective-permute-start(f32[8,4224]{1,0:T(8,128)S(1)} %add.27), channel_id=1, source_target_pairs={{0,256},{16,272},{32,288},{48,304},{64,320},{80,336},{96,352},{112... | collective-permute-start | bytes 405512 | tf_op jit(solution)/shard_map/ppermute | solution.py:14
  186.8 3.5 %collective-permute-done.4 = f32[8,4224]{1,0:T(8,128)S(1)} collective-permute-done((f32[8,4224]{1,0:T(8,128)S(1)}, f32[8,4224]{1,0:T(8,128)S(1)}, u32[]{:S(2)}, u32[]{:S(2)}) %collective-permute-start.4) | collective-permute-done | bytes 135200 | tf_op jit(solution)/shard_map/ppermute | solution.py:14
  190.4 0.1 dynamic_slice.9
  190.5 0.1 dynamic_slice.10
  190.6 0.1 slice_reduce_fusion
  190.7 0.7 subtract_multiply_fusion
  191.3 61.4 %reduce-scatter.2.cloned.1.call-done = f32[128,256]{1,0:T(8,128)} async-done(((f32[4096,256]{1,0:T(8,128)}), f32[128,256]{1,0:T(8,128)}) %reduce-scatter.2.cloned.1.call-update) | async-done | bytes 131088 | tf_op jit(solution)/shard_map/reduce_scatter | solution.py:30
  252.8 1.0 bitcast_subtract_fusion
  253.8 0.8 copy.6
  (8 shorter events, 0.1 us)
Async XLA Ops:
  7.2 135.9 %all-gather.2.cloned.1.call-start = ((), (), s32[]{:S(2)}) async-start(), calls=%async_computation.1 | async-start | bytes 8912896 | tf_op jit(solution)/shard_map/all_gather | solution.py:29
  7.9 143.0 %copy-start = (s32[1024]{0:T(1024)S(1)}, s32[1024]{0:T(1024)}, u32[]{:S(2)}) copy-start(s32[1024]{0:T(1024)} %param.3) | copy-start | bytes 12292
  7.9 244.9 %reduce-scatter.2.cloned.1.call-start = ((), (), s32[]{:S(2)}) async-start(), calls=%async_computation.2 | async-start | bytes 4325376 | tf_op jit(solution)/shard_map/reduce_scatter | solution.py:30
  155.7 3.2 %collective-permute-start = (f32[8,4224]{1,0:T(8,128)S(1)}, f32[8,4224]{1,0:T(8,128)S(1)}, u32[]{:S(2)}, u32[]{:S(2)}) collective-permute-start(f32[8,4224]{1,0:T(8,128)S(1)} %pad_maximum_fusion), channel_id=1, source_target_pairs={{0,16},{16,0},{32,48},{48,32},{64,80},{80,64},{96,112},{112,96},{1... | collective-permute-start | bytes 405512 | tf_op jit(solution)/shard_map/ppermute | solution.py:14
  159.0 7.5 %collective-permute-start.1 = (f32[8,4224]{1,0:T(8,128)S(1)}, f32[8,4224]{1,0:T(8,128)S(1)}, u32[]{:S(2)}, u32[]{:S(2)}) collective-permute-start(f32[8,4224]{1,0:T(8,128)S(1)} %fusion.2), channel_id=1, source_target_pairs={{0,32},{16,48},{32,0},{48,16},{64,96},{80,112},{96,64},{112,80},{1... | collective-permute-start | bytes 405512 | tf_op jit(solution)/shard_map/ppermute | solution.py:14
  166.6 8.4 %collective-permute-start.2 = (f32[8,4224]{1,0:T(8,128)S(1)}, f32[8,4224]{1,0:T(8,128)S(1)}, u32[]{:S(2)}, u32[]{:S(2)}) collective-permute-start(f32[8,4224]{1,0:T(8,128)S(1)} %add.25), channel_id=1, source_target_pairs={{0,64},{16,80},{32,96},{48,112},{64,0},{80,16},{96,32},{112,48},{1... | collective-permute-start | bytes 405512 | tf_op jit(solution)/shard_map/ppermute | solution.py:14
  175.0 6.9 %collective-permute-start.3 = (f32[8,4224]{1,0:T(8,128)S(1)}, f32[8,4224]{1,0:T(8,128)S(1)}, u32[]{:S(2)}, u32[]{:S(2)}) collective-permute-start(f32[8,4224]{1,0:T(8,128)S(1)} %add.26), channel_id=1, source_target_pairs={{0,128},{16,144},{32,160},{48,176},{64,192},{80,208},{96,224},{112... | collective-permute-start | bytes 405512 | tf_op jit(solution)/shard_map/ppermute | solution.py:14
  181.9 8.4 %collective-permute-start.4 = (f32[8,4224]{1,0:T(8,128)S(1)}, f32[8,4224]{1,0:T(8,128)S(1)}, u32[]{:S(2)}, u32[]{:S(2)}) collective-permute-start(f32[8,4224]{1,0:T(8,128)S(1)} %add.27), channel_id=1, source_target_pairs={{0,256},{16,272},{32,288},{48,304},{64,320},{80,336},{96,352},{112... | collective-permute-start | bytes 405512 | tf_op jit(solution)/shard_map/ppermute | solution.py:14
Sparse Core Ops, SparseCore 0:
  10.0 133.0 all-gather.1
  151.1 101.6 reduce-scatter.1

commit v2 on v1

v2 whole, which is shorter than its diff:
```python
import jax
import jax.numpy as jnp
from jax import lax
from jax.sharding import PartitionSpec as P

D = 4096
CLASSES = 8
CHUNKS = 4
RS_BITS = (0, 1, 3, 2, 4)


def butterfly_sum(x, axis, n):
    k = 1
    while k < n:
        perm = [(i, i ^ k) for i in range(n)]
        x = x + lax.ppermute(x, axis, perm)
        k *= 2
    return x


def butterfly_scatter(x, axis, n, bits):
    me = lax.axis_index(axis)
    nb = len(bits)
    tail = x.shape[1:]
    x = x.reshape((2,) * nb + tail)
    left = list(range(nb))
    for b in bits:
        pos = left.index(nb - 1 - b)
        mine = (me >> b) & 1
        keep = lax.dynamic_index_in_dim(x, mine, pos, keepdims=False)
        send = lax.dynamic_index_in_dim(x, 1 - mine, pos, keepdims=False)
        perm = [(i, i ^ (1 << b)) for i in range(n)]
        x = keep + lax.ppermute(send, axis, perm)
        left.pop(pos)
    return x


def body(activations, labels):
    tok_rows, slice_width = activations.shape
    n_dp = lax.axis_size("dp")
    n_t = lax.axis_size("tensor")
    assert n_dp == 1 << len(RS_BITS)
    token_total = tok_rows * n_dp
    col_width = D // n_dp
    halves = slice_width // col_width
    w = col_width // CHUNKS
    classes = jnp.arange(CLASSES, dtype=jnp.int32)
    matches = labels[None, :] == classes[:, None]
    onehot = matches.astype(jnp.bfloat16)
    local_counts = jnp.sum(matches.astype(jnp.float32), axis=1)
    own_local = jnp.dot(onehot, activations, preferred_element_type=jnp.float32)
    stats = jnp.concatenate(
        [own_local, jnp.broadcast_to(local_counts[:, None], (CLASSES, 128))], axis=1
    )
    stats = butterfly_sum(stats, "dp", n_dp)
    own_sums = stats[:, :slice_width]
    class_counts = stats[:, slice_width]

    own_t = activations.T.reshape(halves, col_width, tok_rows)
    parts = [own_t[:, k * w:(k + 1) * w, :].reshape(halves * w, tok_rows) for k in range(CHUNKS)]
    pieces = []
    colsums = []
    for k in range(CHUNKS):
        part = parts[k]
        g = lax.all_gather(part, "tensor", axis=0, tiled=True)
        prod = lax.dot_general(
            g, activations, (((1,), (0,)), ((), ())), preferred_element_type=jnp.float32
        ).reshape(n_dp, w, slice_width)
        colsums.append(jnp.sum(g.astype(jnp.float32), axis=1).reshape(n_dp, w))
        if k == CHUNKS - 1:
            colsum = jnp.concatenate(colsums, axis=1)
            extra = jnp.zeros((n_dp, 8, slice_width), jnp.float32)
            extra = extra.at[:, 0, :col_width].set(colsum)
            prod = jnp.concatenate([prod, extra], axis=1)
        if k + 1 < CHUNKS:
            parts[k + 1], prod = lax.optimization_barrier((parts[k + 1], prod))
        piece = butterfly_scatter(prod, "dp", n_dp, RS_BITS)
        if k + 2 < CHUNKS:
            parts[k + 2], piece = lax.optimization_barrier((parts[k + 2], piece))
        pieces.append(piece)
    mean_cols = pieces[-1][w, :col_width] / token_total
    gram_cols = jnp.concatenate(pieces[:-1] + [pieces[-1][:w]], axis=0)

    mean_rows = jnp.sum(own_sums, axis=0) / token_total
    covariance = gram_cols.T / token_total - mean_rows[:, None] * mean_cols[None, :]
    cross_covariance = (own_sums - class_counts[:, None] * mean_rows[None, :]) / token_total
    return (covariance, cross_covariance)


def solution(mesh):
    in_specs = (P("dp", "tensor"), P("dp"))
    out_specs = (P("tensor", "dp"), P(None, "tensor"))
    return jax.shard_map(body, mesh=mesh, in_specs=in_specs, out_specs=out_specs, check_vma=False)
```

time: 262 us -> 360 us (1.37)
  the two profiles are of different devices: /device:TPU:2 before, /device:TPU:32 now
where the time goes in v2:
time: 360 us; the launch traced here: 359 us
  waiting for transfers between devices  229 us (64%)
  starting transfers between devices  89.7 us (25%)
  between operations  14.4 us (4%)
  other arithmetic  10.6 us (3%)
  matrix products  8.88 us (2%)
  local copies, waits for them, and re-layouts  6.2 us (2%)
    all_gather x4, waiting for transfers between devices, body(): g = lax.all_gather(part, 'tensor', axis=0, tiled=True)  172 us
    ppermute x20, starting transfers between devices, butterfly_scatter(): x = keep + lax.ppermute(send, axis, perm)  70.9 us
    ppermute x20, waiting for transfers between devices, butterfly_scatter(): x = keep + lax.ppermute(send, axis, perm)  47.8 us
    ppermute x5, starting transfers between devices, butterfly_sum(): x = x + lax.ppermute(x, axis, perm)  18.6 us
    ppermute x5, waiting for transfers between devices, butterfly_sum(): x = x + lax.ppermute(x, axis, perm)  9.86 us
    dot_general x4, matrix products, body(): lax.dot_general(g, activations, (((1,), (0,)), ((), ())), preferred_eleme...  8.7 us
  transfers between devices with their start and end apart: 29, of which 24 were waited for; matrix products, arithmetic and copies ran while one was open for 4% of the time, Pallas kernels for 0%

profile of v2, /device:TPU:32, one launch (start us, length us, event | category | flops | bytes accessed | tf_op | source)
XLA Modules:
  0.0 359.2 jit_solution(11233232944824296545)
XLA Ops:
  9.4 78.0 %all-gather.5.cloned.1.call-done = bf16[1024,1024]{1,0:T(8,128)(2,1)} async-done(((bf16[64,1024]{1,0:T(8,128)(2,1)}), bf16[1024,1024]{1,0:T(8,128)(2,1)}) %all-gather.5.cloned.1.call-update) | async-done | bytes 2097168 | tf_op jit(solution)/shard_map/all_gather | solution.py:65
  93.8 3.4 collective-permute-start.1
  97.2 6.9 %collective-permute-done.1 = f32[2,2,2,32,256]{4,3,2,1,0:T(8,128)S(1)} collective-permute-done((f32[2,2,2,32,256]{4,3,2,1,0:T(8,128)S(1)}, f32[2,2,2,32,256]{4,3,2,1,0:T(8,128)S(1)}, u32[]{:S(2)}, u32[]{:S(2)}) %collective-permute-start.1) | collective-permute-done | bytes 262176 | tf_op jit(solution)/shard_map/ppermute | solution.py:33
  104.1 3.4 collective-permute-start.2
  107.5 3.5 collective-permute-done.2
  111.1 4.9 %collective-permute-start.3 = (f32[2,32,256]{2,1,0:T(8,128)S(1)}, f32[2,32,256]{2,1,0:T(8,128)S(1)}, u32[]{:S(2)}, u32[]{:S(2)}) collective-permute-start(f32[2,32,256]{2,1,0:T(8,128)S(1)} %dynamic-slice_bitcast_fusion.11), channel_id=1, source_target_pairs={{0,64},{16,80},{32,96},{48,112},{64,0},{80,16},{96,32},{112,48},{1... | collective-permute-start | bytes 196616 | tf_op jit(solution)/shard_map/ppermute | solution.py:33
  116.0 2.8 collective-permute-done.3
  118.7 4.9 %collective-permute-start.4 = (f32[32,256]{1,0:T(8,128)S(1)}, f32[32,256]{1,0:T(8,128)S(1)}, u32[]{:S(2)}, u32[]{:S(2)}) collective-permute-start(f32[32,256]{1,0:T(8,128)S(1)} %dynamic-slice_bitcast_fusion.15), channel_id=1, source_target_pairs={{0,256},{16,272},{32,288},{48,304},{64,320},{80,336},{96,352},{112... | collective-permute-start | bytes 98312 | tf_op jit(solution)/shard_map/ppermute | solution.py:33
  126.1 33.2 %all-gather.7.cloned.1.call-done = bf16[1024,1024]{1,0:T(8,128)(2,1)} async-done(((bf16[64,1024]{1,0:T(8,128)(2,1)}), bf16[1024,1024]{1,0:T(8,128)(2,1)}) %all-gather.7.cloned.1.call-update) | async-done | bytes 2097168 | tf_op jit(solution)/shard_map/all_gather | solution.py:65
  165.7 3.4 collective-permute-start.6
  169.1 6.8 %collective-permute-done.6 = f32[2,2,2,32,256]{4,3,2,1,0:T(8,128)S(1)} collective-permute-done((f32[2,2,2,32,256]{4,3,2,1,0:T(8,128)S(1)}, f32[2,2,2,32,256]{4,3,2,1,0:T(8,128)S(1)}, u32[]{:S(2)}, u32[]{:S(2)}) %collective-permute-start.6) | collective-permute-done | bytes 262176 | tf_op jit(solution)/shard_map/ppermute | solution.py:33
  176.0 3.5 collective-permute-start.7
  179.5 3.4 collective-permute-done.7
  183.0 4.9 %collective-permute-start.8 = (f32[2,32,256]{2,1,0:T(8,128)S(1)}, f32[2,32,256]{2,1,0:T(8,128)S(1)}, u32[]{:S(2)}, u32[]{:S(2)}) collective-permute-start(f32[2,32,256]{2,1,0:T(8,128)S(1)} %dynamic-slice_bitcast_fusion.10), channel_id=1, source_target_pairs={{0,64},{16,80},{32,96},{48,112},{64,0},{80,16},{96,32},{112,48},{1... | collective-permute-start | bytes 196616 | tf_op jit(solution)/shard_map/ppermute | solution.py:33
  190.6 4.9 %collective-permute-start.9 = (f32[32,256]{1,0:T(8,128)S(1)}, f32[32,256]{1,0:T(8,128)S(1)}, u32[]{:S(2)}, u32[]{:S(2)}) collective-permute-start(f32[32,256]{1,0:T(8,128)S(1)} %dynamic-slice_bitcast_fusion.14), channel_id=1, source_target_pairs={{0,256},{16,272},{32,288},{48,304},{64,320},{80,336},{96,352},{112... | collective-permute-start | bytes 98312 | tf_op jit(solution)/shard_map/ppermute | solution.py:33
  198.0 33.4 %all-gather.9.cloned.1.call-done = bf16[1024,1024]{1,0:T(8,128)(2,1)} async-done(((bf16[64,1024]{1,0:T(8,128)(2,1)}), bf16[1024,1024]{1,0:T(8,128)(2,1)}) %all-gather.9.cloned.1.call-update) | async-done | bytes 2097168 | tf_op jit(solution)/shard_map/all_gather | solution.py:65
  231.3 3.4 fusion.14
  238.3 3.4 collective-permute-start.21
  243.9 4.9 %collective-permute-start.22 = (f32[8,384]{1,0:T(8,128)S(1)}, f32[8,384]{1,0:T(8,128)S(1)}, u32[]{:S(2)}, u32[]{:S(2)}) collective-permute-start(f32[8,384]{1,0:T(8,128)S(1)} %add.185), channel_id=1, source_target_pairs={{0,64},{16,80},{32,96},{48,112},{64,0},{80,16},{96,32},{112,48},{1... | collective-permute-start | bytes 36872 | tf_op jit(solution)/shard_map/ppermute | solution.py:16
  251.0 3.4 collective-permute-start.23
  256.6 4.9 %collective-permute-start.24 = (f32[8,384]{1,0:T(8,128)S(1)}, f32[8,384]{1,0:T(8,128)S(1)}, u32[]{:S(2)}, u32[]{:S(2)}) collective-permute-start(f32[8,384]{1,0:T(8,128)S(1)} %add.187), channel_id=1, source_target_pairs={{0,256},{16,272},{32,288},{48,304},{64,320},{80,336},{96,352},{112... | collective-permute-start | bytes 36872 | tf_op jit(solution)/shard_map/ppermute | solution.py:16
  274.0 3.4 collective-permute-start.11
  277.4 27.1 %all-gather.11.cloned.1.call-done = bf16[1024,1024]{1,0:T(8,128)(2,1)} async-done(((bf16[64,1024]{1,0:T(8,128)(2,1)}), bf16[1024,1024]{1,0:T(8,128)(2,1)}) %all-gather.11.cloned.1.call-update) | async-done | bytes 2097168 | tf_op jit(solution)/shard_map/all_gather | solution.py:65
  311.5 3.4 collective-permute-start.12
  315.0 3.4 collective-permute-start.16
  319.3 4.9 %collective-permute-start.13 = (f32[2,32,256]{2,1,0:T(8,128)S(1)}, f32[2,32,256]{2,1,0:T(8,128)S(1)}, u32[]{:S(2)}, u32[]{:S(2)}) collective-permute-start(f32[2,32,256]{2,1,0:T(8,128)S(1)} %dynamic-slice_bitcast_fusion.9), channel_id=1, source_target_pairs={{0,64},{16,80},{32,96},{48,112},{64,0},{80,16},{96,32},{112,48},{1... | collective-permute-start | bytes 196616 | tf_op jit(solution)/shard_map/ppermute | solution.py:33
  324.2 3.2 collective-permute-done.16
  330.2 4.6 %collective-permute-done.17 = f32[2,2,40,256]{3,2,1,0:T(8,128)S(1)} collective-permute-done((f32[2,2,40,256]{3,2,1,0:T(8,128)S(1)}, f32[2,2,40,256]{3,2,1,0:T(8,128)S(1)}, u32[]{:S(2)}, u32[]{:S(2)}) %collective-permute-start.17) | collective-permute-done | bytes 163872 | tf_op jit(solution)/shard_map/ppermute | solution.py:33
  334.8 4.9 %collective-permute-start.18 = (f32[2,40,256]{2,1,0:T(8,128)S(1)}, f32[2,40,256]{2,1,0:T(8,128)S(1)}, u32[]{:S(2)}, u32[]{:S(2)}) collective-permute-start(f32[2,40,256]{2,1,0:T(8,128)S(1)} %dynamic-slice_bitcast_fusion.8), channel_id=1, source_target_pairs={{0,64},{16,80},{32,96},{48,112},{64,0},{80,16},{96,32},{112,48},{1... | collective-permute-start | bytes 245768 | tf_op jit(solution)/shard_map/ppermute | solution.py:33
  339.7 4.6 %collective-permute-start.14 = (f32[32,256]{1,0:T(8,128)S(1)}, f32[32,256]{1,0:T(8,128)S(1)}, u32[]{:S(2)}, u32[]{:S(2)}) collective-permute-start(f32[32,256]{1,0:T(8,128)S(1)} %dynamic-slice_bitcast_fusion.13), channel_id=1, source_target_pairs={{0,256},{16,272},{32,288},{48,304},{64,320},{80,336},{96,352},{112... | collective-permute-start | bytes 98312 | tf_op jit(solution)/shard_map/ppermute | solution.py:33
  344.4 2.9 collective-permute-start.19
  347.4 4.5 %collective-permute-done.19 = f32[40,256]{1,0:T(8,128)S(1)} collective-permute-done((f32[40,256]{1,0:T(8,128)S(1)}, f32[40,256]{1,0:T(8,128)S(1)}, u32[]{:S(2)}, u32[]{:S(2)}) %collective-permute-start.19) | collective-permute-done | bytes 40992 | tf_op jit(solution)/shard_map/ppermute | solution.py:33
  (117 shorter events, 56.9 us)
Async XLA Ops:
  7.2 80.2 %copy-start.2 = (bf16[1024,256]{1,0:T(8,128)(2,1)S(1)}, bf16[1024,256]{1,0:T(8,128)(2,1)}, u32[]{:S(2)}) copy-start(bf16[1024,256]{1,0:T(8,128)(2,1)} %param.4) | copy-start | bytes 1572868
  7.2 80.2 %all-gather.5.cloned.1.call-start = ((), (), s32[]{:S(2)}) async-start(), calls=%async_computation | async-start | bytes 2228224 | tf_op jit(solution)/shard_map/all_gather | solution.py:65
  9.3 150.0 %all-gather.7.cloned.1.call-start = ((), (), s32[]{:S(2)}) async-start(), calls=%async_computation.1 | async-start | bytes 2228224 | tf_op jit(solution)/shard_map/all_gather | solution.py:65
  89.7 141.6 %all-gather.9.cloned.1.call-start = ((), (), s32[]{:S(2)}) async-start(), calls=%async_computation.2 | async-start | bytes 2228224 | tf_op jit(solution)/shard_map/all_gather | solution.py:65
  89.9 3.8 %collective-permute-start = (f32[2,2,2,2,32,256]{5,4,2,1,0,3:T(8,128)S(1)}, f32[2,2,2,2,32,256]{5,4,2,1,0,3:T(8,128)S(1)}, u32[]{:S(2)}, u32[]{:S(2)}) collective-permute-start(f32[2,2,2,2,32,256]{5,4,2,1,0,3:T(8,128)S(1)} %bitcast.128), channel_id=1, source_target_pairs={{0,16},{16,0},{32,48},{48,32},{64,80},{80,64},{96,112},{112,96},{1... | collective-permute-start | bytes 1572872 | tf_op jit(solution)/shard_map/ppermute | solution.py:33
  93.8 10.2 %collective-permute-start.1 = (f32[2,2,2,32,256]{4,3,2,1,0:T(8,128)S(1)}, f32[2,2,2,32,256]{4,3,2,1,0:T(8,128)S(1)}, u32[]{:S(2)}, u32[]{:S(2)}) collective-permute-start(f32[2,2,2,32,256]{4,3,2,1,0:T(8,128)S(1)} %dynamic-slice_bitcast_fusion.3), channel_id=1, source_target_pairs={{0,32},{16,48},{32,0},{48,16},{64,96},{80,112},{96,64},{112,80},{1... | collective-permute-start | bytes 786440 | tf_op jit(solution)/shard_map/ppermute | solution.py:33
  104.1 6.9 %collective-permute-start.2 = (f32[2,2,32,256]{3,2,1,0:T(8,128)S(1)}, f32[2,2,32,256]{3,2,1,0:T(8,128)S(1)}, u32[]{:S(2)}, u32[]{:S(2)}) collective-permute-start(f32[2,2,32,256]{3,2,1,0:T(8,128)S(1)} %dynamic-slice_bitcast_fusion.7), channel_id=1, source_target_pairs={{0,128},{16,144},{32,160},{48,176},{64,192},{80,208},{96,224},{112... | collective-permute-start | bytes 393224 | tf_op jit(solution)/shard_map/ppermute | solution.py:33
  111.1 7.7 %collective-permute-start.3 = (f32[2,32,256]{2,1,0:T(8,128)S(1)}, f32[2,32,256]{2,1,0:T(8,128)S(1)}, u32[]{:S(2)}, u32[]{:S(2)}) collective-permute-start(f32[2,32,256]{2,1,0:T(8,128)S(1)} %dynamic-slice_bitcast_fusion.11), channel_id=1, source_target_pairs={{0,64},{16,80},{32,96},{48,112},{64,0},{80,16},{96,32},{112,48},{1... | collective-permute-start | bytes 196616 | tf_op jit(solution)/shard_map/ppermute | solution.py:33
  118.7 7.3 %collective-permute-start.4 = (f32[32,256]{1,0:T(8,128)S(1)}, f32[32,256]{1,0:T(8,128)S(1)}, u32[]{:S(2)}, u32[]{:S(2)}) collective-permute-start(f32[32,256]{1,0:T(8,128)S(1)} %dynamic-slice_bitcast_fusion.15), channel_id=1, source_target_pairs={{0,256},{16,272},{32,288},{48,304},{64,320},{80,336},{96,352},{112... | collective-permute-start | bytes 98312 | tf_op jit(solution)/shard_map/ppermute | solution.py:33
  161.6 142.9 %all-gather.11.cloned.1.call-start = ((), (), s32[]{:S(2)}) async-start(), calls=%async_computation.3 | async-start | bytes 2228224 | tf_op jit(solution)/shard_map/all_gather | solution.py:65
  161.8 3.8 %collective-permute-start.5 = (f32[2,2,2,2,32,256]{5,4,2,1,0,3:T(8,128)S(1)}, f32[2,2,2,2,32,256]{5,4,2,1,0,3:T(8,128)S(1)}, u32[]{:S(2)}, u32[]{:S(2)}) collective-permute-start(f32[2,2,2,2,32,256]{5,4,2,1,0,3:T(8,128)S(1)} %bitcast.129), channel_id=1, source_target_pairs={{0,16},{16,0},{32,48},{48,32},{64,80},{80,64},{96,112},{112,96},{1... | collective-permute-start | bytes 1572872 | tf_op jit(solution)/shard_map/ppermute | solution.py:33
  165.7 10.2 %collective-permute-start.6 = (f32[2,2,2,32,256]{4,3,2,1,0:T(8,128)S(1)}, f32[2,2,2,32,256]{4,3,2,1,0:T(8,128)S(1)}, u32[]{:S(2)}, u32[]{:S(2)}) collective-permute-start(f32[2,2,2,32,256]{4,3,2,1,0:T(8,128)S(1)} %dynamic-slice_bitcast_fusion.2), channel_id=1, source_target_pairs={{0,32},{16,48},{32,0},{48,16},{64,96},{80,112},{96,64},{112,80},{1... | collective-permute-start | bytes 786440 | tf_op jit(solution)/shard_map/ppermute | solution.py:33
  176.0 6.9 %collective-permute-start.7 = (f32[2,2,32,256]{3,2,1,0:T(8,128)S(1)}, f32[2,2,32,256]{3,2,1,0:T(8,128)S(1)}, u32[]{:S(2)}, u32[]{:S(2)}) collective-permute-start(f32[2,2,32,256]{3,2,1,0:T(8,128)S(1)} %dynamic-slice_bitcast_fusion.6), channel_id=1, source_target_pairs={{0,128},{16,144},{32,160},{48,176},{64,192},{80,208},{96,224},{112... | collective-permute-start | bytes 393224 | tf_op jit(solution)/shard_map/ppermute | solution.py:33
  183.0 7.7 %collective-permute-start.8 = (f32[2,32,256]{2,1,0:T(8,128)S(1)}, f32[2,32,256]{2,1,0:T(8,128)S(1)}, u32[]{:S(2)}, u32[]{:S(2)}) collective-permute-start(f32[2,32,256]{2,1,0:T(8,128)S(1)} %dynamic-slice_bitcast_fusion.10), channel_id=1, source_target_pairs={{0,64},{16,80},{32,96},{48,112},{64,0},{80,16},{96,32},{112,48},{1... | collective-permute-start | bytes 196616 | tf_op jit(solution)/shard_map/ppermute | solution.py:33
  190.6 7.3 %collective-permute-start.9 = (f32[32,256]{1,0:T(8,128)S(1)}, f32[32,256]{1,0:T(8,128)S(1)}, u32[]{:S(2)}, u32[]{:S(2)}) collective-permute-start(f32[32,256]{1,0:T(8,128)S(1)} %dynamic-slice_bitcast_fusion.14), channel_id=1, source_target_pairs={{0,256},{16,272},{32,288},{48,304},{64,320},{80,336},{96,352},{112... | collective-permute-start | bytes 98312 | tf_op jit(solution)/shard_map/ppermute | solution.py:33
  198.0 36.8 %copy-start.3 = (s32[1024]{0:T(1024)S(1)}, s32[1024]{0:T(1024)}, u32[]{:S(2)}) copy-start(s32[1024]{0:T(1024)} %param.5) | copy-start | bytes 12292
  234.7 33.7 %copy-start = (bf16[1024,1024]{1,0:T(8,128)(2,1)S(1)}, bf16[1024,1024]{1,0:T(8,128)(2,1)}, u32[]{:S(2)}) copy-start(bf16[1024,1024]{1,0:T(8,128)(2,1)} %all-gather.5.cloned.1.call-done) | copy-start | bytes 6291460
  235.1 3.2 collective-permute-start.20
  238.3 5.6 %collective-permute-start.21 = (f32[8,384]{1,0:T(8,128)S(1)}, f32[8,384]{1,0:T(8,128)S(1)}, u32[]{:S(2)}, u32[]{:S(2)}) collective-permute-start(f32[8,384]{1,0:T(8,128)S(1)} %fusion.10), channel_id=1, source_target_pairs={{0,32},{16,48},{32,0},{48,16},{64,96},{80,112},{96,64},{112,80},{1... | collective-permute-start | bytes 36872 | tf_op jit(solution)/shard_map/ppermute | solution.py:16
  243.9 7.1 %collective-permute-start.22 = (f32[8,384]{1,0:T(8,128)S(1)}, f32[8,384]{1,0:T(8,128)S(1)}, u32[]{:S(2)}, u32[]{:S(2)}) collective-permute-start(f32[8,384]{1,0:T(8,128)S(1)} %add.185), channel_id=1, source_target_pairs={{0,64},{16,80},{32,96},{48,112},{64,0},{80,16},{96,32},{112,48},{1... | collective-permute-start | bytes 36872 | tf_op jit(solution)/shard_map/ppermute | solution.py:16
  251.0 5.6 %collective-permute-start.23 = (f32[8,384]{1,0:T(8,128)S(1)}, f32[8,384]{1,0:T(8,128)S(1)}, u32[]{:S(2)}, u32[]{:S(2)}) collective-permute-start(f32[8,384]{1,0:T(8,128)S(1)} %add.186), channel_id=1, source_target_pairs={{0,128},{16,144},{32,160},{48,176},{64,192},{80,208},{96,224},{112... | collective-permute-start | bytes 36872 | tf_op jit(solution)/shard_map/ppermute | solution.py:16
  256.6 7.1 %collective-permute-start.24 = (f32[8,384]{1,0:T(8,128)S(1)}, f32[8,384]{1,0:T(8,128)S(1)}, u32[]{:S(2)}, u32[]{:S(2)}) collective-permute-start(f32[8,384]{1,0:T(8,128)S(1)} %add.187), channel_id=1, source_target_pairs={{0,256},{16,272},{32,288},{48,304},{64,320},{80,336},{96,352},{112... | collective-permute-start | bytes 36872 | tf_op jit(solution)/shard_map/ppermute | solution.py:16
  266.5 6.4 %collective-permute-start.10 = (f32[2,2,2,2,32,256]{5,4,2,1,0,3:T(8,128)}, f32[2,2,2,2,32,256]{5,4,2,1,0,3:T(8,128)}, u32[]{:S(2)}, u32[]{:S(2)}) collective-permute-start(f32[2,2,2,2,32,256]{5,4,2,1,0,3:T(8,128)} %bitcast.117), channel_id=1, source_target_pairs={{0,16},{16,0},{32,48},{48,32},{64,80},{80,64},{96,112},{112,96},{1... | collective-permute-start | bytes 1572872 | tf_op jit(solution)/shard_map/ppermute | solution.py:33
  274.0 36.5 %collective-permute-start.11 = (f32[2,2,2,32,256]{4,3,2,1,0:T(8,128)S(1)}, f32[2,2,2,32,256]{4,3,2,1,0:T(8,128)}, u32[]{:S(2)}, u32[]{:S(2)}) collective-permute-start(f32[2,2,2,32,256]{4,3,2,1,0:T(8,128)S(1)} %dynamic-slice_bitcast_fusion.1), channel_id=1, source_target_pairs={{0,32},{16,48},{32,0},{48,16},{64,96},{80,112},{96,64},{112,80},{1... | collective-permute-start | bytes 786440 | tf_op jit(solution)/shard_map/ppermute | solution.py:33
  307.8 7.1 %collective-permute-start.15 = (f32[2,2,2,2,40,256]{5,4,2,1,0,3:T(8,128)S(1)}, f32[2,2,2,2,40,256]{5,4,2,1,0,3:T(8,128)S(1)}, u32[]{:S(2)}, u32[]{:S(2)}) collective-permute-start(f32[2,2,2,2,40,256]{5,4,2,1,0,3:T(8,128)S(1)} %bitcast.127), channel_id=1, source_target_pairs={{0,16},{16,0},{32,48},{48,32},{64,80},{80,64},{96,112},{112,96},{1... | collective-permute-start | bytes 1966088 | tf_op jit(solution)/shard_map/ppermute | solution.py:33
  311.5 7.8 %collective-permute-start.12 = (f32[2,2,32,256]{3,2,1,0:T(8,128)S(1)}, f32[2,2,32,256]{3,2,1,0:T(8,128)S(1)}, u32[]{:S(2)}, u32[]{:S(2)}) collective-permute-start(f32[2,2,32,256]{3,2,1,0:T(8,128)S(1)} %dynamic-slice_bitcast_fusion.5), channel_id=1, source_target_pairs={{0,128},{16,144},{32,160},{48,176},{64,192},{80,208},{96,224},{112... | collective-permute-start | bytes 393224 | tf_op jit(solution)/shard_map/ppermute | solution.py:33
  315.0 12.4 %collective-permute-start.16 = (f32[2,2,2,40,256]{4,3,2,1,0:T(8,128)S(1)}, f32[2,2,2,40,256]{4,3,2,1,0:T(8,128)S(1)}, u32[]{:S(2)}, u32[]{:S(2)}) collective-permute-start(f32[2,2,2,40,256]{4,3,2,1,0:T(8,128)S(1)} %dynamic-slice_bitcast_fusion), channel_id=1, source_target_pairs={{0,32},{16,48},{32,0},{48,16},{64,96},{80,112},{96,64},{112,80},{1... | collective-permute-start | bytes 983048 | tf_op jit(solution)/shard_map/ppermute | solution.py:33
  319.3 10.8 %collective-permute-start.13 = (f32[2,32,256]{2,1,0:T(8,128)S(1)}, f32[2,32,256]{2,1,0:T(8,128)S(1)}, u32[]{:S(2)}, u32[]{:S(2)}) collective-permute-start(f32[2,32,256]{2,1,0:T(8,128)S(1)} %dynamic-slice_bitcast_fusion.9), channel_id=1, source_target_pairs={{0,64},{16,80},{32,96},{48,112},{64,0},{80,16},{96,32},{112,48},{1... | collective-permute-start | bytes 196616 | tf_op jit(solution)/shard_map/ppermute | solution.py:33
  327.5 7.2 %collective-permute-start.17 = (f32[2,2,40,256]{3,2,1,0:T(8,128)S(1)}, f32[2,2,40,256]{3,2,1,0:T(8,128)S(1)}, u32[]{:S(2)}, u32[]{:S(2)}) collective-permute-start(f32[2,2,40,256]{3,2,1,0:T(8,128)S(1)} %dynamic-slice_bitcast_fusion.4), channel_id=1, source_target_pairs={{0,128},{16,144},{32,160},{48,176},{64,192},{80,208},{96,224},{112... | collective-permute-start | bytes 491528 | tf_op jit(solution)/shard_map/ppermute | solution.py:33
  334.8 9.6 %collective-permute-start.18 = (f32[2,40,256]{2,1,0:T(8,128)S(1)}, f32[2,40,256]{2,1,0:T(8,128)S(1)}, u32[]{:S(2)}, u32[]{:S(2)}) collective-permute-start(f32[2,40,256]{2,1,0:T(8,128)S(1)} %dynamic-slice_bitcast_fusion.8), channel_id=1, source_target_pairs={{0,64},{16,80},{32,96},{48,112},{64,0},{80,16},{96,32},{112,48},{1... | collective-permute-start | bytes 245768 | tf_op jit(solution)/shard_map/ppermute | solution.py:33
  339.7 7.6 %collective-permute-start.14 = (f32[32,256]{1,0:T(8,128)S(1)}, f32[32,256]{1,0:T(8,128)S(1)}, u32[]{:S(2)}, u32[]{:S(2)}) collective-permute-start(f32[32,256]{1,0:T(8,128)S(1)} %dynamic-slice_bitcast_fusion.13), channel_id=1, source_target_pairs={{0,256},{16,272},{32,288},{48,304},{64,320},{80,336},{96,352},{112... | collective-permute-start | bytes 98312 | tf_op jit(solution)/shard_map/ppermute | solution.py:33
  344.4 7.4 %collective-permute-start.19 = (f32[40,256]{1,0:T(8,128)S(1)}, f32[40,256]{1,0:T(8,128)S(1)}, u32[]{:S(2)}, u32[]{:S(2)}) collective-permute-start(f32[40,256]{1,0:T(8,128)S(1)} %dynamic-slice_bitcast_fusion.12), channel_id=1, source_target_pairs={{0,256},{16,272},{32,288},{48,304},{64,320},{80,336},{96,352},{112... | collective-permute-start | bytes 122888 | tf_op jit(solution)/shard_map/ppermute | solution.py:33
  (2 other events, 4.6 us)
Sparse Core Ops, SparseCore 0:
  10.6 76.6 all-gather.4
  89.8 69.4 all-gather.6
  161.8 69.5 all-gather.8
  234.9 69.6 all-gather.10

commit v3 on v1

--- a/solution.py
+++ b/solution.py
@@ -27,14 +27,11 @@
     onehot = matches.astype(jnp.bfloat16)
     local_counts = jnp.sum(matches.astype(jnp.float32), axis=1)
     gathered = lax.all_gather(activations, "tensor", axis=1, tiled=True)
-    gram_cols = lax.psum_scatter(
-        lax.dot_general(
-            gathered, activations, (((0,), (0,)), ((), ())), preferred_element_type=jnp.float32
-        ),
-        "dp",
-        scatter_dimension=0,
-        tiled=True,
-    )
+    prod = lax.dot_general(
+        gathered, activations, (((0,), (0,)), ((), ())), preferred_element_type=jnp.float32
+    ).reshape(n_dp, col_width, slice_width)
+    recv = lax.all_to_all(prod, "dp", 0, 0, tiled=True)
+    gram_cols = jnp.sum(recv, axis=0)
     slice_start = lax.axis_index("tensor") * slice_width
     wide_local = jnp.dot(onehot, gathered, preferred_element_type=jnp.float32)
     stats = jnp.concatenate(

time: 262 us -> 247 us (0.943)
  the two profiles are of different devices: /device:TPU:2 before, /device:TPU:17 now
where the time goes in v3:
time: 247 us; the launch traced here: 242 us
  waiting for transfers between devices  179 us (72%)
  starting transfers between devices  32.5 us (13%)
  between operations  14.1 us (6%)
  matrix products  12.4 us (5%)
  other arithmetic  3.48 us (1%)
    all_gather x1, waiting for transfers between devices, body(): gathered = lax.all_gather(activations, 'tensor', axis=1, tiled=True)  125 us
    ppermute x5, waiting for transfers between devices, butterfly_sum(): x = x + lax.ppermute(x, axis, perm)  53.3 us
    all_to_all x1, starting transfers between devices, body(): recv = lax.all_to_all(prod, 'dp', 0, 0, tiled=True)  18.2 us
    ppermute x5, starting transfers between devices, butterfly_sum(): x = x + lax.ppermute(x, axis, perm)  14.3 us
    dot_general x1, matrix products, body(): lax.dot_general(gathered, activations, (((0,), (0,)), ((), ())), preferre...  7.83 us
  transfers between devices with their start and end apart: 7, of which 6 were waited for; matrix products, arithmetic and copies ran while one was open for 2% of the time, Pallas kernels for 0%

profile of v3, /device:TPU:17, one launch (start us, length us, event | category | flops | bytes accessed | tf_op | source)
XLA Modules:
  0.0 242.3 jit_solution(1144874661513010110)
XLA Ops:
  7.2 0.0 all-gather.2.cloned.1.call-start
  7.2 0.7 all-gather.2.cloned.1.call-update
  7.9 124.7 %all-gather.2.cloned.1.call-done = bf16[1024,4096]{1,0:T(8,128)(2,1)} async-done(((bf16[1024,256]{1,0:T(8,128)(2,1)}), bf16[1024,4096]{1,0:T(8,128)(2,1)}) %all-gather.2.cloned.1.call-update) | async-done | bytes 8388624 | tf_op jit(solution)/shard_map/all_gather | solution.py:29
  132.6 7.8 %fusion.4 = f32[4096,256]{1,0:T(8,128)} fusion(bf16[1024,4096]{1,0:T(8,128)(2,1)} %all-gather.2.cloned.1.call-done, bf16[1024,256]{1,0:T(8,128)(2,1)} %param.2), kind=kOutput, calls=%fused_computation.12 | convolution fusion | flops 2147483648 | bytes 13107200 | tf_op jit(solution)/shard_map/dot_general | solution.py:30
  140.4 0.0 copy-start
  140.4 18.2 %all-to-all-start = ((f32[32,128,256]{2,1,0:T(8,128)}), f32[32,128,256]{2,1,0:T(8,128)}, u32[]{:S(2)}, u32[]{:S(2)}) async-start(f32[32,128,256]{2,1,0:T(8,128)} %bitcast.6), calls=%async_computation | async-start | bytes 8388608 | tf_op jit(solution)/shard_map/all_to_all | solution.py:33
  158.6 0.0 copy-done
  158.6 0.1 convert_reduce_fusion
  158.7 4.6 %fusion = f32[8,4096]{1,0:T(8,128)S(1)} fusion(bf16[1024,4096]{1,0:T(8,128)(2,1)} %all-gather.2.cloned.1.call-done, s32[1024]{0:T(1024)S(1)} %copy-done), kind=kOutput, calls=%fused_computation.4 | convolution fusion | flops 67117056 | bytes 8523776 | tf_op jit(solution)/shard_map/dot_general | solution.py:36
  163.3 0.1 broadcast_in_dim.2
  163.4 2.3 collective-permute-start
  165.7 1.0 collective-permute-done
  166.7 3.1 %collective-permute-start.1 = (f32[8,4224]{1,0:T(8,128)S(1)}, f32[8,4224]{1,0:T(8,128)S(1)}, u32[]{:S(2)}, u32[]{:S(2)}) collective-permute-start(f32[8,4224]{1,0:T(8,128)S(1)} %fusion.2), channel_id=1, source_target_pairs={{0,32},{16,48},{32,0},{48,16},{64,96},{80,112},{96,64},{112,80},{1... | collective-permute-start | bytes 405512 | tf_op jit(solution)/shard_map/ppermute | solution.py:14
  169.8 40.6 %collective-permute-done.1 = f32[8,4224]{1,0:T(8,128)S(1)} collective-permute-done((f32[8,4224]{1,0:T(8,128)S(1)}, f32[8,4224]{1,0:T(8,128)S(1)}, u32[]{:S(2)}, u32[]{:S(2)}) %collective-permute-start.1) | collective-permute-done | bytes 135200 | tf_op jit(solution)/shard_map/ppermute | solution.py:14
  210.5 4.2 %collective-permute-start.2 = (f32[8,4224]{1,0:T(8,128)S(1)}, f32[8,4224]{1,0:T(8,128)S(1)}, u32[]{:S(2)}, u32[]{:S(2)}) collective-permute-start(f32[8,4224]{1,0:T(8,128)S(1)} %add.23), channel_id=1, source_target_pairs={{0,64},{16,80},{32,96},{48,112},{64,0},{80,16},{96,32},{112,48},{1... | collective-permute-start | bytes 405512 | tf_op jit(solution)/shard_map/ppermute | solution.py:14
  214.7 3.3 %collective-permute-done.2 = f32[8,4224]{1,0:T(8,128)S(1)} collective-permute-done((f32[8,4224]{1,0:T(8,128)S(1)}, f32[8,4224]{1,0:T(8,128)S(1)}, u32[]{:S(2)}, u32[]{:S(2)}) %collective-permute-start.2) | collective-permute-done | bytes 135200 | tf_op jit(solution)/shard_map/ppermute | solution.py:14
  218.0 2.1 collective-permute-start.3
  220.1 3.7 %collective-permute-done.3 = f32[8,4224]{1,0:T(8,128)S(1)} collective-permute-done((f32[8,4224]{1,0:T(8,128)S(1)}, f32[8,4224]{1,0:T(8,128)S(1)}, u32[]{:S(2)}, u32[]{:S(2)}) %collective-permute-start.3) | collective-permute-done | bytes 135200 | tf_op jit(solution)/shard_map/ppermute | solution.py:14
  223.8 2.6 %collective-permute-start.4 = (f32[8,4224]{1,0:T(8,128)S(1)}, f32[8,4224]{1,0:T(8,128)S(1)}, u32[]{:S(2)}, u32[]{:S(2)}) collective-permute-start(f32[8,4224]{1,0:T(8,128)S(1)} %add.25), channel_id=1, source_target_pairs={{0,256},{16,272},{32,288},{48,304},{64,320},{80,336},{96,352},{112... | collective-permute-start | bytes 405512 | tf_op jit(solution)/shard_map/ppermute | solution.py:14
  226.4 4.7 %collective-permute-done.4 = f32[8,4224]{1,0:T(8,128)S(1)} collective-permute-done((f32[8,4224]{1,0:T(8,128)S(1)}, f32[8,4224]{1,0:T(8,128)S(1)}, u32[]{:S(2)}, u32[]{:S(2)}) %collective-permute-start.4) | collective-permute-done | bytes 135200 | tf_op jit(solution)/shard_map/ppermute | solution.py:14
  231.2 0.1 dynamic_slice.9
  231.2 0.1 dynamic_slice.10
  231.3 0.1 slice_reduce_fusion
  231.4 0.7 subtract_multiply_fusion
  232.1 0.0 all-to-all-done
  232.1 2.4 %reduce_sum.27 = f32[128,256]{1,0:T(8,128)S(1)} reduce(f32[32,128,256]{2,1,0:T(8,128)} %all-to-all-done, f32[]{:T(128)} %constant.9.clone.1), dimensions={0}, to_apply=%region_0.0 | reduce | flops 1015808 | bytes 4325380 | tf_op jit(solution)/shard_map/reduce_sum | solution.py:34
  234.6 0.1 bitcast_subtract_fusion
  234.7 0.8 copy.5
  (8 shorter events, 0.1 us)
Async XLA Ops:
  7.2 125.4 %all-gather.2.cloned.1.call-start = ((), (), s32[]{:S(2)}) async-start(), calls=%async_computation.1 | async-start | bytes 8912896 | tf_op jit(solution)/shard_map/all_gather | solution.py:29
  140.4 18.2 %copy-start = (s32[1024]{0:T(1024)S(1)}, s32[1024]{0:T(1024)}, u32[]{:S(2)}) copy-start(s32[1024]{0:T(1024)} %param.3) | copy-start | bytes 12292
  140.4 91.7 %all-to-all-start = ((f32[32,128,256]{2,1,0:T(8,128)}), f32[32,128,256]{2,1,0:T(8,128)}, u32[]{:S(2)}, u32[]{:S(2)}) async-start(f32[32,128,256]{2,1,0:T(8,128)} %bitcast.6), calls=%async_computation | async-start | bytes 8388608 | tf_op jit(solution)/shard_map/all_to_all | solution.py:33
  163.4 3.3 %collective-permute-start = (f32[8,4224]{1,0:T(8,128)S(1)}, f32[8,4224]{1,0:T(8,128)S(1)}, u32[]{:S(2)}, u32[]{:S(2)}) collective-permute-start(f32[8,4224]{1,0:T(8,128)S(1)} %pad_maximum_fusion), channel_id=1, source_target_pairs={{0,16},{16,0},{32,48},{48,32},{64,80},{80,64},{96,112},{112,96},{1... | collective-permute-start | bytes 405512 | tf_op jit(solution)/shard_map/ppermute | solution.py:14
  166.7 43.7 %collective-permute-start.1 = (f32[8,4224]{1,0:T(8,128)S(1)}, f32[8,4224]{1,0:T(8,128)S(1)}, u32[]{:S(2)}, u32[]{:S(2)}) collective-permute-start(f32[8,4224]{1,0:T(8,128)S(1)} %fusion.2), channel_id=1, source_target_pairs={{0,32},{16,48},{32,0},{48,16},{64,96},{80,112},{96,64},{112,80},{1... | collective-permute-start | bytes 405512 | tf_op jit(solution)/shard_map/ppermute | solution.py:14
  210.5 7.6 %collective-permute-start.2 = (f32[8,4224]{1,0:T(8,128)S(1)}, f32[8,4224]{1,0:T(8,128)S(1)}, u32[]{:S(2)}, u32[]{:S(2)}) collective-permute-start(f32[8,4224]{1,0:T(8,128)S(1)} %add.23), channel_id=1, source_target_pairs={{0,64},{16,80},{32,96},{48,112},{64,0},{80,16},{96,32},{112,48},{1... | collective-permute-start | bytes 405512 | tf_op jit(solution)/shard_map/ppermute | solution.py:14
  218.0 5.8 %collective-permute-start.3 = (f32[8,4224]{1,0:T(8,128)S(1)}, f32[8,4224]{1,0:T(8,128)S(1)}, u32[]{:S(2)}, u32[]{:S(2)}) collective-permute-start(f32[8,4224]{1,0:T(8,128)S(1)} %add.24), channel_id=1, source_target_pairs={{0,128},{16,144},{32,160},{48,176},{64,192},{80,208},{96,224},{112... | collective-permute-start | bytes 405512 | tf_op jit(solution)/shard_map/ppermute | solution.py:14
  223.8 7.3 %collective-permute-start.4 = (f32[8,4224]{1,0:T(8,128)S(1)}, f32[8,4224]{1,0:T(8,128)S(1)}, u32[]{:S(2)}, u32[]{:S(2)}) collective-permute-start(f32[8,4224]{1,0:T(8,128)S(1)} %add.25), channel_id=1, source_target_pairs={{0,256},{16,272},{32,288},{48,304},{64,320},{80,336},{96,352},{112... | collective-permute-start | bytes 405512 | tf_op jit(solution)/shard_map/ppermute | solution.py:14
Sparse Core Ops, SparseCore 0:
  10.0 122.5 all-gather.1

commit v4 on v3

v4 whole, which is shorter than its diff:
```python
import jax
import jax.numpy as jnp
from jax import lax
from jax.sharding import PartitionSpec as P

D = 4096
CLASSES = 8


def butterfly_sum(x, axis, n):
    k = 1
    while k < n:
        perm = [(i, i ^ k) for i in range(n)]
        x = x + lax.ppermute(x, axis, perm)
        k *= 2
    return x


def body(activations, labels):
    tok_rows, slice_width = activations.shape
    n_dp = lax.axis_size("dp")
    assert n_dp & (n_dp - 1) == 0
    token_total = tok_rows * n_dp
    col_width = D // n_dp
    classes = jnp.arange(CLASSES, dtype=jnp.int32)
    matches = labels[None, :] == classes[:, None]
    onehot = matches.astype(jnp.bfloat16)
    local_counts = jnp.sum(matches.astype(jnp.float32), axis=1)
    own_local = jnp.dot(onehot, activations, preferred_element_type=jnp.float32)
    stats = jnp.concatenate(
        [own_local, jnp.broadcast_to(local_counts[:, None], (CLASSES, 128))], axis=1
    )
    stats = butterfly_sum(stats, "dp", n_dp)

    gathered = lax.all_gather(activations, "tensor", axis=1, tiled=True)
    gathered, stats = lax.optimization_barrier((gathered, stats))
    prod = lax.dot_general(
        gathered, activations, (((0,), (0,)), ((), ())), preferred_element_type=jnp.float32
    ).reshape(n_dp, col_width, slice_width)
    colsum = jnp.sum(gathered.astype(jnp.float32), axis=0).reshape(n_dp, 1, col_width)
    extra = jnp.pad(colsum, ((0, 0), (0, 7), (0, slice_width - col_width)))
    payload = jnp.concatenate([prod, extra], axis=1)
    recv = lax.all_to_all(payload, "dp", 0, 0, tiled=True)
    total = jnp.sum(recv, axis=0)
    gram_cols = total[:col_width]
    mean_cols = total[col_width, :col_width] / token_total

    own_sums = stats[:, :slice_width]
    class_counts = stats[:, slice_width]
    mean_rows = jnp.sum(own_sums, axis=0) / token_total
    covariance = gram_cols.T / token_total - mean_rows[:, None] * mean_cols[None, :]
    cross_covariance = (own_sums - class_counts[:, None] * mean_rows[None, :]) / token_total
    return (covariance, cross_covariance)


def solution(mesh):
    in_specs = (P("dp", "tensor"), P("dp"))
    out_specs = (P("tensor", "dp"), P(None, "tensor"))
    return jax.shard_map(body, mesh=mesh, in_specs=in_specs, out_specs=out_specs, check_vma=False)
```

time: 247 us -> 228 us (0.923)
  the two profiles are of different devices: /device:TPU:17 before, /device:TPU:32 now
where the time goes in v4:
time: 228 us
  waiting for transfers between devices  170 us (75%)
  starting transfers between devices  26.5 us (12%)
  between operations  14.1 us (6%)
  other arithmetic  11.4 us (5%)
  matrix products  3.95 us (2%)
    all_gather x1, waiting for transfers between devices, body(): gathered = lax.all_gather(activations, 'tensor', axis=1, tiled=True)  103 us
    all_to_all x1, waiting for transfers between devices, body(): recv = lax.all_to_all(payload, 'dp', 0, 0, tiled=True)  56.1 us
    ppermute x5, starting transfers between devices, butterfly_sum(): x = x + lax.ppermute(x, axis, perm)  18.8 us
    ppermute x5, waiting for transfers between devices, butterfly_sum(): x = x + lax.ppermute(x, axis, perm)  9.56 us
    all_to_all x1, starting transfers between devices, body(): recv = lax.all_to_all(payload, 'dp', 0, 0, tiled=True)  7.67 us
    reduce_sum x1, other arithmetic, body(): jnp.sum(gathered.astype(jnp.float32), axis=0).reshape(n_dp, 1, col_width)  4.73 us
  transfers between devices with their start and end apart: 7, of which 7 were waited for; matrix products, arithmetic and copies ran while one was open for 1% of the time, Pallas kernels for 0%

profile of v4, /device:TPU:32, one launch (start us, length us, event | category | flops | bytes accessed | tf_op | source)
XLA Modules:
  0.0 227.5 jit_solution(747196064949531017)
XLA Ops:
  7.2 0.0 all-gather.2.cloned.1.call-start
  7.2 0.7 all-gather.2.cloned.1.call-update
  7.9 0.8 convert_reduce_fusion.1
  8.7 0.0 copy-start.1
  8.7 1.3 fusion.2
  10.0 0.1 broadcast_in_dim.2
  10.1 1.9 collective-permute-start
  12.0 1.1 collective-permute-done
  13.2 3.4 %collective-permute-start.1 = (f32[8,384]{1,0:T(8,128)S(1)}, f32[8,384]{1,0:T(8,128)S(1)}, u32[]{:S(2)}, u32[]{:S(2)}) collective-permute-start(f32[8,384]{1,0:T(8,128)S(1)} %fusion.5), channel_id=1, source_target_pairs={{0,32},{16,48},{32,0},{48,16},{64,96},{80,112},{96,64},{112,80},{1... | collective-permute-start | bytes 36872 | tf_op jit(solution)/shard_map/ppermute | solution.py:14
  16.5 2.2 collective-permute-done.1
  18.7 4.9 %collective-permute-start.2 = (f32[8,384]{1,0:T(8,128)S(1)}, f32[8,384]{1,0:T(8,128)S(1)}, u32[]{:S(2)}, u32[]{:S(2)}) collective-permute-start(f32[8,384]{1,0:T(8,128)S(1)} %add.18), channel_id=1, source_target_pairs={{0,64},{16,80},{32,96},{48,112},{64,0},{80,16},{96,32},{112,48},{1... | collective-permute-start | bytes 36872 | tf_op jit(solution)/shard_map/ppermute | solution.py:14
  23.7 2.2 collective-permute-done.2
  25.8 3.5 %collective-permute-start.3 = (f32[8,384]{1,0:T(8,128)S(1)}, f32[8,384]{1,0:T(8,128)S(1)}, u32[]{:S(2)}, u32[]{:S(2)}) collective-permute-start(f32[8,384]{1,0:T(8,128)S(1)} %add.19), channel_id=1, source_target_pairs={{0,128},{16,144},{32,160},{48,176},{64,192},{80,208},{96,224},{112... | collective-permute-start | bytes 36872 | tf_op jit(solution)/shard_map/ppermute | solution.py:14
  29.3 2.1 collective-permute-done.3
  31.4 5.1 %collective-permute-start.4 = (f32[8,384]{1,0:T(8,128)S(1)}, f32[8,384]{1,0:T(8,128)S(1)}, u32[]{:S(2)}, u32[]{:S(2)}) collective-permute-start(f32[8,384]{1,0:T(8,128)S(1)} %add.20), channel_id=1, source_target_pairs={{0,256},{16,272},{32,288},{48,304},{64,320},{80,336},{96,352},{112... | collective-permute-start | bytes 36872 | tf_op jit(solution)/shard_map/ppermute | solution.py:14
  36.5 2.0 collective-permute-done.4
  38.5 103.2 %all-gather.2.cloned.1.call-done = bf16[1024,4096]{1,0:T(8,128)(2,1)} async-done(((bf16[1024,256]{1,0:T(8,128)(2,1)}), bf16[1024,4096]{1,0:T(8,128)(2,1)}) %all-gather.2.cloned.1.call-update) | async-done | bytes 8388624 | tf_op jit(solution)/shard_map/all_gather | solution.py:35
  141.7 0.0 copy-start
  141.7 4.7 %convert_reduce_fusion = f32[4096]{0:T(1024)S(1)} fusion(bf16[1024,4096]{1,0:T(8,128)(2,1)} %all-gather.2.cloned.1.call-done), kind=kLoop, calls=%fused_computation | loop fusion | flops 8384512 | bytes 8404992 | tf_op jit(solution)/shard_map/reduce_sum | solution.py:40
  146.5 0.0 copy-done.1
  146.5 1.0 copy-done
  147.5 2.7 %fusion.6 = f32[4096,256]{1,0:T(8,128)S(1)} fusion(bf16[1024,4096]{1,0:T(8,128)(2,1)S(1)} %copy-done, bf16[1024,256]{1,0:T(8,128)(2,1)S(1)} %copy-done.1), kind=kOutput, calls=%fused_computation.18 | convolution fusion | flops 2147483648 | bytes 13107200 | tf_op jit(solution)/shard_map/dot_general | solution.py:37
  150.2 2.5 %select_maximum_fusion = f32[32,136,256]{2,1,0:T(8,128)} fusion(f32[32,1,128]{2,1,0:T(1,128)S(1)} %bitcast.12, f32[32,128,256]{2,1,0:T(8,128)S(1)} %bitcast.11), kind=kLoop, calls=%fused_computation.1 | loop fusion | flops 3342336 | bytes 8667136 | tf_op jit(solution)/shard_map/concatenate | solution.py:42
  152.7 7.7 %all-to-all-start = ((f32[32,136,256]{2,1,0:T(8,128)}), f32[32,136,256]{2,1,0:T(8,128)}, u32[]{:S(2)}, u32[]{:S(2)}) async-start(f32[32,136,256]{2,1,0:T(8,128)} %select_maximum_fusion), calls=%async_computation | async-start | bytes 8912896 | tf_op jit(solution)/shard_map/all_to_all | solution.py:43
  160.4 0.1 slice_reduce_fusion.1
  160.5 0.7 subtract_multiply_fusion
  161.2 56.1 %all-to-all-done = f32[32,136,256]{2,1,0:T(8,128)} async-done(((f32[32,136,256]{2,1,0:T(8,128)}), f32[32,136,256]{2,1,0:T(8,128)}, u32[]{:S(2)}, u32[]{:S(2)}) %all-to-all-start) | async-done | bytes 4456480 | tf_op jit(solution)/shard_map/all_to_all | solution.py:43
  217.3 2.5 %reduce_sum.38 = f32[136,256]{1,0:T(8,128)S(1)} reduce(f32[32,136,256]{2,1,0:T(8,128)} %all-to-all-done, f32[]{:T(128)} %constant.5.clone.1), dimensions={0}, to_apply=%region_2.3 | reduce | flops 1079296 | bytes 4595716 | tf_op jit(solution)/shard_map/reduce_sum | solution.py:44
  219.9 0.1 fusion.1
  219.9 0.8 copy.5
  (9 shorter events, 0.1 us)
Async XLA Ops:
  7.2 134.6 %all-gather.2.cloned.1.call-start = ((), (), s32[]{:S(2)}) async-start(), calls=%async_computation.1 | async-start | bytes 8912896 | tf_op jit(solution)/shard_map/all_gather | solution.py:35
  8.7 137.7 %copy-start.1 = (bf16[1024,256]{1,0:T(8,128)(2,1)S(1)}, bf16[1024,256]{1,0:T(8,128)(2,1)}, u32[]{:S(2)}) copy-start(bf16[1024,256]{1,0:T(8,128)(2,1)} %param.2) | copy-start | bytes 1572868
  10.1 3.1 %collective-permute-start = (f32[8,384]{1,0:T(8,128)S(1)}, f32[8,384]{1,0:T(8,128)S(1)}, u32[]{:S(2)}, u32[]{:S(2)}) collective-permute-start(f32[8,384]{1,0:T(8,128)S(1)} %pad_maximum_fusion), channel_id=1, source_target_pairs={{0,16},{16,0},{32,48},{48,32},{64,80},{80,64},{96,112},{112,96},{1... | collective-permute-start | bytes 36872 | tf_op jit(solution)/shard_map/ppermute | solution.py:14
  13.2 5.6 %collective-permute-start.1 = (f32[8,384]{1,0:T(8,128)S(1)}, f32[8,384]{1,0:T(8,128)S(1)}, u32[]{:S(2)}, u32[]{:S(2)}) collective-permute-start(f32[8,384]{1,0:T(8,128)S(1)} %fusion.5), channel_id=1, source_target_pairs={{0,32},{16,48},{32,0},{48,16},{64,96},{80,112},{96,64},{112,80},{1... | collective-permute-start | bytes 36872 | tf_op jit(solution)/shard_map/ppermute | solution.py:14
  18.7 7.1 %collective-permute-start.2 = (f32[8,384]{1,0:T(8,128)S(1)}, f32[8,384]{1,0:T(8,128)S(1)}, u32[]{:S(2)}, u32[]{:S(2)}) collective-permute-start(f32[8,384]{1,0:T(8,128)S(1)} %add.18), channel_id=1, source_target_pairs={{0,64},{16,80},{32,96},{48,112},{64,0},{80,16},{96,32},{112,48},{1... | collective-permute-start | bytes 36872 | tf_op jit(solution)/shard_map/ppermute | solution.py:14
  25.8 5.6 %collective-permute-start.3 = (f32[8,384]{1,0:T(8,128)S(1)}, f32[8,384]{1,0:T(8,128)S(1)}, u32[]{:S(2)}, u32[]{:S(2)}) collective-permute-start(f32[8,384]{1,0:T(8,128)S(1)} %add.19), channel_id=1, source_target_pairs={{0,128},{16,144},{32,160},{48,176},{64,192},{80,208},{96,224},{112... | collective-permute-start | bytes 36872 | tf_op jit(solution)/shard_map/ppermute | solution.py:14
  31.4 7.1 %collective-permute-start.4 = (f32[8,384]{1,0:T(8,128)S(1)}, f32[8,384]{1,0:T(8,128)S(1)}, u32[]{:S(2)}, u32[]{:S(2)}) collective-permute-start(f32[8,384]{1,0:T(8,128)S(1)} %add.20), channel_id=1, source_target_pairs={{0,256},{16,272},{32,288},{48,304},{64,320},{80,336},{96,352},{112... | collective-permute-start | bytes 36872 | tf_op jit(solution)/shard_map/ppermute | solution.py:14
  141.7 5.8 %copy-start = (bf16[1024,4096]{1,0:T(8,128)(2,1)S(1)}, bf16[1024,4096]{1,0:T(8,128)(2,1)}, u32[]{:S(2)}) copy-start(bf16[1024,4096]{1,0:T(8,128)(2,1)} %all-gather.2.cloned.1.call-done) | copy-start | bytes 25165828
  152.7 64.6 %all-to-all-start = ((f32[32,136,256]{2,1,0:T(8,128)}), f32[32,136,256]{2,1,0:T(8,128)}, u32[]{:S(2)}, u32[]{:S(2)}) async-start(f32[32,136,256]{2,1,0:T(8,128)} %select_maximum_fusion), calls=%async_computation | async-start | bytes 8912896 | tf_op jit(solution)/shard_map/all_to_all | solution.py:43
Sparse Core Ops, SparseCore 0:
  10.0 131.6 all-gather.1

commit v5 on v4

--- a/solution.py
+++ b/solution.py
@@ -5,6 +5,7 @@
 
 D = 4096
 CLASSES = 8
+EXTRA_ROWS = 16
 
 
 def butterfly_sum(x, axis, n):
@@ -37,11 +38,32 @@
     prod = lax.dot_general(
         gathered, activations, (((0,), (0,)), ((), ())), preferred_element_type=jnp.float32
     ).reshape(n_dp, col_width, slice_width)
-    colsum = jnp.sum(gathered.astype(jnp.float32), axis=0).reshape(n_dp, 1, col_width)
-    extra = jnp.pad(colsum, ((0, 0), (0, 7), (0, slice_width - col_width)))
+    ones = jnp.ones((8, tok_rows), jnp.bfloat16)
+    colsum = jnp.dot(ones, gathered, preferred_element_type=jnp.float32)[0]
+    extra = jnp.pad(
+        colsum.reshape(n_dp, 1, col_width),
+        ((0, 0), (0, EXTRA_ROWS - 1), (0, slice_width - col_width)),
+    )
     payload = jnp.concatenate([prod, extra], axis=1)
-    recv = lax.all_to_all(payload, "dp", 0, 0, tiled=True)
-    total = jnp.sum(recv, axis=0)
+    rows = col_width + EXTRA_ROWS
+    half_rows = rows // 2
+
+    me = lax.axis_index("dp")
+    core = me & 1
+    pairs = payload.reshape(n_dp // 2, 2, rows, slice_width)
+    keep = lax.dynamic_index_in_dim(pairs, core, 1, keepdims=False)
+    send = lax.dynamic_index_in_dim(pairs, 1 - core, 1, keepdims=False)
+    core_swap = [(i, i ^ 1) for i in range(n_dp)]
+    chip_sum = keep + lax.ppermute(send, "dp", core_swap)
+    halves = chip_sum.reshape(n_dp, half_rows, slice_width)
+    recv = lax.all_to_all(halves, "dp", 0, 0, tiled=True)
+    by_core = jnp.sum(recv.reshape(n_dp // 2, 2, half_rows, slice_width), axis=0)
+    mine = lax.dynamic_index_in_dim(by_core, core, 0, keepdims=False)
+    other = lax.dynamic_index_in_dim(by_core, 1 - core, 0, keepdims=False)
+    got = lax.ppermute(other, "dp", core_swap)
+    total = jnp.where(
+        core == 0, jnp.concatenate([mine, got], axis=0), jnp.concatenate([got, mine], axis=0)
+    )
     gram_cols = total[:col_width]
     mean_cols = total[col_width, :col_width] / token_total
 

time: 228 us -> 217 us (0.952)
  the two profiles are of different devices: /device:TPU:32 before, /device:TPU:1 now
where the time goes in v5:
time: 217 us
  waiting for transfers between devices  144 us (66%)
  starting transfers between devices  40 us (18%)
  between operations  14.2 us (7%)
  matrix products  8.53 us (4%)
  other arithmetic  6.03 us (3%)
  local copies, waits for them, and re-layouts  3.93 us (2%)
    all_gather x1, waiting for transfers between devices, body(): gathered = lax.all_gather(activations, 'tensor', axis=1, tiled=True)  93.1 us
    all_to_all x1, waiting for transfers between devices, body(): recv = lax.all_to_all(halves, 'dp', 0, 0, tiled=True)  31.4 us
    ppermute x5, starting transfers between devices, butterfly_sum(): x = x + lax.ppermute(x, axis, perm)  16.4 us
    ppermute x5, waiting for transfers between devices, butterfly_sum(): x = x + lax.ppermute(x, axis, perm)  14.3 us
    ppermute x1, starting transfers between devices, body(): chip_sum = keep + lax.ppermute(send, 'dp', core_swap)  12.1 us
    all_to_all x1, starting transfers between devices, body(): recv = lax.all_to_all(halves, 'dp', 0, 0, tiled=True)  7.69 us
    dot_general x1, matrix products, body(): colsum = jnp.dot(ones, gathered, preferred_element_type=jnp.float32)[0]  4.72 us
  transfers between devices with their start and end apart: 9, of which 9 were waited for; matrix products, arithmetic and copies ran while one was open for 1% of the time, Pallas kernels for 0%

profile of v5, /device:TPU:1, one launch (start us, length us, event | category | flops | bytes accessed | tf_op | source)
XLA Modules:
  0.0 216.7 jit_solution(1376456379972688514)
XLA Ops:
  7.2 0.7 all-gather.2.cloned.1.call-update
  7.9 0.8 convert_reduce_fusion
  8.7 1.2 fusion.7
  9.9 0.1 broadcast_in_dim.4
  10.0 8.7 %collective-permute-start = (f32[8,384]{1,0:T(8,128)S(1)}, f32[8,384]{1,0:T(8,128)S(1)}, u32[]{:S(2)}, u32[]{:S(2)}) collective-permute-start(f32[8,384]{1,0:T(8,128)S(1)} %pad_maximum_fusion), channel_id=1, source_target_pairs={{0,16},{16,0},{32,48},{48,32},{64,80},{80,64},{96,112},{112,96},{1... | collective-permute-start | bytes 36872 | tf_op jit(solution)/shard_map/ppermute | solution.py:15
  18.8 0.8 collective-permute-done
  19.6 1.9 collective-permute-start.1
  21.5 2.5 %collective-permute-done.1 = f32[8,384]{1,0:T(8,128)S(1)} collective-permute-done((f32[8,384]{1,0:T(8,128)S(1)}, f32[8,384]{1,0:T(8,128)S(1)}, u32[]{:S(2)}, u32[]{:S(2)}) %collective-permute-start.1) | collective-permute-done | bytes 12320 | tf_op jit(solution)/shard_map/ppermute | solution.py:15
  24.0 1.9 collective-permute-start.2
  25.9 4.0 %collective-permute-done.2 = f32[8,384]{1,0:T(8,128)S(1)} collective-permute-done((f32[8,384]{1,0:T(8,128)S(1)}, f32[8,384]{1,0:T(8,128)S(1)}, u32[]{:S(2)}, u32[]{:S(2)}) %collective-permute-start.2) | collective-permute-done | bytes 12320 | tf_op jit(solution)/shard_map/ppermute | solution.py:15
  30.0 1.9 collective-permute-start.3
  31.9 2.9 %collective-permute-done.3 = f32[8,384]{1,0:T(8,128)S(1)} collective-permute-done((f32[8,384]{1,0:T(8,128)S(1)}, f32[8,384]{1,0:T(8,128)S(1)}, u32[]{:S(2)}, u32[]{:S(2)}) %collective-permute-start.3) | collective-permute-done | bytes 12320 | tf_op jit(solution)/shard_map/ppermute | solution.py:15
  34.8 1.9 collective-permute-start.4
  36.7 4.1 %collective-permute-done.4 = f32[8,384]{1,0:T(8,128)S(1)} collective-permute-done((f32[8,384]{1,0:T(8,128)S(1)}, f32[8,384]{1,0:T(8,128)S(1)}, u32[]{:S(2)}, u32[]{:S(2)}) %collective-permute-start.4) | collective-permute-done | bytes 12320 | tf_op jit(solution)/shard_map/ppermute | solution.py:15
  40.8 93.1 %all-gather.2.cloned.1.call-done = bf16[1024,4096]{1,0:T(8,128)(2,1)} async-done(((bf16[1024,256]{1,0:T(8,128)(2,1)}), bf16[1024,4096]{1,0:T(8,128)(2,1)}) %all-gather.2.cloned.1.call-update) | async-done | bytes 8388624 | tf_op jit(solution)/shard_map/all_gather | solution.py:36
  133.9 4.7 %convolution_bitcast_fusion = f32[32,1,128]{2,1,0:T(1,128)S(1)} fusion(bf16[1024,4096]{1,0:T(8,128)(2,1)} %all-gather.2.cloned.1.call-done), kind=kOutput, calls=%fused_computation.9 | convolution fusion | flops 8388608 | bytes 8404992 | tf_op jit(solution)/shard_map/dot_general | solution.py:42
  138.6 1.0 copy-done
  139.7 2.6 %fusion.13 = f32[4096,256]{1,0:T(8,128)S(1)} fusion(bf16[1024,4096]{1,0:T(8,128)(2,1)S(1)} %copy-done, bf16[1024,256]{1,0:T(8,128)(2,1)S(1)} %copy-done.2), kind=kOutput, calls=%fused_computation.30 | convolution fusion | flops 2147483648 | bytes 13107200 | tf_op jit(solution)/shard_map/dot_general | solution.py:38
  142.3 1.9 copy-done.1
  144.2 0.2 fusion.1
  144.3 12.1 %collective-permute-start.5 = (f32[16,144,256]{2,1,0:T(8,128)S(1)}, f32[16,144,256]{2,1,0:T(8,128)}, u32[]{:S(2)}, u32[]{:S(2)}) collective-permute-start(f32[16,144,256]{2,1,0:T(8,128)S(1)} %fusion.1), channel_id=1, source_target_pairs={{0,16},{16,0},{32,48},{48,32},{64,80},{80,64},{96,112},{112,96},{1... | collective-permute-start | bytes 7077896 | tf_op jit(solution)/shard_map/ppermute | solution.py:57
  156.5 4.3 %collective-permute-done.5 = f32[16,144,256]{2,1,0:T(8,128)} collective-permute-done((f32[16,144,256]{2,1,0:T(8,128)S(1)}, f32[16,144,256]{2,1,0:T(8,128)}, u32[]{:S(2)}, u32[]{:S(2)}) %collective-permute-start.5) | collective-permute-done | bytes 2359328 | tf_op jit(solution)/shard_map/ppermute | solution.py:57
  160.8 4.1 %fusion.4 = f32[16,144,256]{2,1,0:T(8,128)} fusion(f32[16,144,256]{2,1,0:T(8,128)} %collective-permute-done.5, s32[]{:T(128)S(6)} %select_n.19, f32[16,2,128,256]{3,2,1,0:T(8,128)} %bitcast.29, f32[16,2,16,256]{3,2,1,0:T(8,128)S(1)} %bitcast.33), kind=kLoop, calls=%fused_computation.8 | loop fusion | flops 1179648 | bytes 9437188 | tf_op jit(solution)/shard_map/add | solution.py:57
  164.9 7.7 %all-to-all-start = ((f32[32,72,256]{2,1,0:T(8,128)}), f32[32,72,256]{2,1,0:T(8,128)S(1)}, u32[]{:S(2)}, u32[]{:S(2)}) async-start(f32[32,72,256]{2,1,0:T(8,128)} %bitcast.31), calls=%async_computation | async-start | bytes 4718592 | tf_op jit(solution)/shard_map/all_to_all | solution.py:59
  172.6 0.1 slice_reduce_fusion.1
  172.7 31.4 %all-to-all-done = f32[32,72,256]{2,1,0:T(8,128)S(1)} async-done(((f32[32,72,256]{2,1,0:T(8,128)}), f32[32,72,256]{2,1,0:T(8,128)S(1)}, u32[]{:S(2)}, u32[]{:S(2)}) %all-to-all-start) | async-done | bytes 2359328 | tf_op jit(solution)/shard_map/all_to_all | solution.py:59
  204.1 0.1 reduce_sum.28
  204.2 3.8 %collective-permute-start.6 = (f32[72,256]{1,0:T(8,128)S(1)}, f32[72,256]{1,0:T(8,128)S(1)}, u32[]{:S(2)}, u32[]{:S(2)}) collective-permute-start(f32[72,256]{1,0:T(8,128)S(1)} %get-tuple-element.11), channel_id=1, source_target_pairs={{0,16},{16,0},{32,48},{48,32},{64,80},{80,64},{96,112},{112,96},{1... | collective-permute-start | bytes 221192 | tf_op jit(solution)/shard_map/ppermute | solution.py:63
  208.1 0.7 subtract_multiply_fusion
  208.7 0.2 collective-permute-done.6
  209.0 0.1 fusion.6
  209.1 0.8 copy.10
  (17 shorter events, 0.2 us)
Async XLA Ops:
  7.2 126.7 %all-gather.2.cloned.1.call-start = ((), (), s32[]{:S(2)}) async-start(), calls=%async_computation.1 | async-start | bytes 8912896 | tf_op jit(solution)/shard_map/all_gather | solution.py:36
  10.0 9.6 %collective-permute-start = (f32[8,384]{1,0:T(8,128)S(1)}, f32[8,384]{1,0:T(8,128)S(1)}, u32[]{:S(2)}, u32[]{:S(2)}) collective-permute-start(f32[8,384]{1,0:T(8,128)S(1)} %pad_maximum_fusion), channel_id=1, source_target_pairs={{0,16},{16,0},{32,48},{48,32},{64,80},{80,64},{96,112},{112,96},{1... | collective-permute-start | bytes 36872 | tf_op jit(solution)/shard_map/ppermute | solution.py:15
  19.6 4.4 %collective-permute-start.1 = (f32[8,384]{1,0:T(8,128)S(1)}, f32[8,384]{1,0:T(8,128)S(1)}, u32[]{:S(2)}, u32[]{:S(2)}) collective-permute-start(f32[8,384]{1,0:T(8,128)S(1)} %fusion.12), channel_id=1, source_target_pairs={{0,32},{16,48},{32,0},{48,16},{64,96},{80,112},{96,64},{112,80},{1... | collective-permute-start | bytes 36872 | tf_op jit(solution)/shard_map/ppermute | solution.py:15
  24.0 5.9 %collective-permute-start.2 = (f32[8,384]{1,0:T(8,128)S(1)}, f32[8,384]{1,0:T(8,128)S(1)}, u32[]{:S(2)}, u32[]{:S(2)}) collective-permute-start(f32[8,384]{1,0:T(8,128)S(1)} %add.32), channel_id=1, source_target_pairs={{0,64},{16,80},{32,96},{48,112},{64,0},{80,16},{96,32},{112,48},{1... | collective-permute-start | bytes 36872 | tf_op jit(solution)/shard_map/ppermute | solution.py:15
  30.0 4.8 %collective-permute-start.3 = (f32[8,384]{1,0:T(8,128)S(1)}, f32[8,384]{1,0:T(8,128)S(1)}, u32[]{:S(2)}, u32[]{:S(2)}) collective-permute-start(f32[8,384]{1,0:T(8,128)S(1)} %add.33), channel_id=1, source_target_pairs={{0,128},{16,144},{32,160},{48,176},{64,192},{80,208},{96,224},{112... | collective-permute-start | bytes 36872 | tf_op jit(solution)/shard_map/ppermute | solution.py:15
  34.8 6.0 %collective-permute-start.4 = (f32[8,384]{1,0:T(8,128)S(1)}, f32[8,384]{1,0:T(8,128)S(1)}, u32[]{:S(2)}, u32[]{:S(2)}) collective-permute-start(f32[8,384]{1,0:T(8,128)S(1)} %add.34), channel_id=1, source_target_pairs={{0,256},{16,272},{32,288},{48,304},{64,320},{80,336},{96,352},{112... | collective-permute-start | bytes 36872 | tf_op jit(solution)/shard_map/ppermute | solution.py:15
  40.8 97.9 %copy-start.2 = (bf16[1024,256]{1,0:T(8,128)(2,1)S(1)}, bf16[1024,256]{1,0:T(8,128)(2,1)}, u32[]{:S(2)}) copy-start(bf16[1024,256]{1,0:T(8,128)(2,1)} %param.2) | copy-start | bytes 1572868
  133.9 5.8 %copy-start = (bf16[1024,4096]{1,0:T(8,128)(2,1)S(1)}, bf16[1024,4096]{1,0:T(8,128)(2,1)}, u32[]{:S(2)}) copy-start(bf16[1024,4096]{1,0:T(8,128)(2,1)} %all-gather.2.cloned.1.call-done) | copy-start | bytes 25165828
  142.2 1.9 copy-start.1
  144.3 16.4 %collective-permute-start.5 = (f32[16,144,256]{2,1,0:T(8,128)S(1)}, f32[16,144,256]{2,1,0:T(8,128)}, u32[]{:S(2)}, u32[]{:S(2)}) collective-permute-start(f32[16,144,256]{2,1,0:T(8,128)S(1)} %fusion.1), channel_id=1, source_target_pairs={{0,16},{16,0},{32,48},{48,32},{64,80},{80,64},{96,112},{112,96},{1... | collective-permute-start | bytes 7077896 | tf_op jit(solution)/shard_map/ppermute | solution.py:57
  164.9 39.2 %all-to-all-start = ((f32[32,72,256]{2,1,0:T(8,128)}), f32[32,72,256]{2,1,0:T(8,128)S(1)}, u32[]{:S(2)}, u32[]{:S(2)}) async-start(f32[32,72,256]{2,1,0:T(8,128)} %bitcast.31), calls=%async_computation | async-start | bytes 4718592 | tf_op jit(solution)/shard_map/all_to_all | solution.py:59
  204.2 4.7 %collective-permute-start.6 = (f32[72,256]{1,0:T(8,128)S(1)}, f32[72,256]{1,0:T(8,128)S(1)}, u32[]{:S(2)}, u32[]{:S(2)}) collective-permute-start(f32[72,256]{1,0:T(8,128)S(1)} %get-tuple-element.11), channel_id=1, source_target_pairs={{0,16},{16,0},{32,48},{48,32},{64,80},{80,64},{96,112},{112,96},{1... | collective-permute-start | bytes 221192 | tf_op jit(solution)/shard_map/ppermute | solution.py:63
Sparse Core Ops, SparseCore 0:
  10.0 123.8 all-gather.1

commit v6 on v5

--- a/solution.py
+++ b/solution.py
@@ -33,13 +33,15 @@
     )
     stats = butterfly_sum(stats, "dp", n_dp)
 
-    gathered = lax.all_gather(activations, "tensor", axis=1, tiled=True)
+    gathered = lax.all_gather(activations, "tensor", axis=0, tiled=False)
     gathered, stats = lax.optimization_barrier((gathered, stats))
     prod = lax.dot_general(
-        gathered, activations, (((0,), (0,)), ((), ())), preferred_element_type=jnp.float32
+        gathered, activations, (((1,), (0,)), ((), ())), preferred_element_type=jnp.float32
     ).reshape(n_dp, col_width, slice_width)
     ones = jnp.ones((8, tok_rows), jnp.bfloat16)
-    colsum = jnp.dot(ones, gathered, preferred_element_type=jnp.float32)[0]
+    colsum = lax.dot_general(
+        gathered, ones, (((1,), (1,)), ((), ())), preferred_element_type=jnp.float32
+    )[..., 0].reshape(D)
     extra = jnp.pad(
         colsum.reshape(n_dp, 1, col_width),
         ((0, 0), (0, EXTRA_ROWS - 1), (0, slice_width - col_width)),

time: 217 us -> 194 us (0.89)
  waiting for transfers between devices: 144 us -> 131 us
  starting transfers between devices: 40 us -> 30.2 us
    all_gather x1, waiting for transfers between devices: 93.1 us -> 80.3 us  [body(): gathered = lax.all_gather(activations, 'tensor', axis=0, tiled=False)]
    ppermute x1, starting transfers between devices: 12.1 us -> 2.75 us  [body(): chip_sum = keep + lax.ppermute(send, 'dp', core_swap)]
  transfers between devices with their start and end apart: 9 -> 9, of which waited for: 9 -> 9; matrix products, arithmetic and copies ran while one was open for 1% -> 2% of each run, Pallas kernels for 0% -> 0%
where the time goes in v6:
time: 194 us
  waiting for transfers between devices  131 us (68%)
  starting transfers between devices  30.2 us (16%)
  between operations  14.2 us (7%)
  matrix products  8.49 us (4%)
  other arithmetic  6.03 us (3%)
  local copies, waits for them, and re-layouts  3.98 us (2%)
    all_gather x1, waiting for transfers between devices, body(): gathered = lax.all_gather(activations, 'tensor', axis=0, tiled=False)  80.3 us
    all_to_all x1, waiting for transfers between devices, body(): recv = lax.all_to_all(halves, 'dp', 0, 0, tiled=True)  31.4 us
    ppermute x5, starting transfers between devices, butterfly_sum(): x = x + lax.ppermute(x, axis, perm)  16.4 us
    ppermute x5, waiting for transfers between devices, butterfly_sum(): x = x + lax.ppermute(x, axis, perm)  14.3 us
    all_to_all x1, starting transfers between devices, body(): recv = lax.all_to_all(halves, 'dp', 0, 0, tiled=True)  7.23 us
    dot_general x1, matrix products, body(): lax.dot_general(gathered, ones, (((1,), (1,)), ((), ())), preferred_eleme...  4.72 us
    ppermute x1, waiting for transfers between devices, body(): chip_sum = keep + lax.ppermute(send, 'dp', core_swap)  4.27 us
    add x1, other arithmetic, body(): chip_sum = keep + lax.ppermute(send, 'dp', core_swap)  4.1 us
  transfers between devices with their start and end apart: 9, of which 9 were waited for; matrix products, arithmetic and copies ran while one was open for 2% of the time, Pallas kernels for 0%

profile of v6, /device:TPU:1, one launch (start us, length us, event | category | flops | bytes accessed | tf_op | source)
XLA Modules:
  0.0 194.0 jit_solution(13075789072454639117)
XLA Ops:
  7.2 0.7 all-gather.3.cloned.1.call-update
  7.9 0.8 convert_reduce_fusion
  8.7 1.2 fusion.9
  9.9 0.1 broadcast_in_dim.4
  10.0 8.7 %collective-permute-start = (f32[8,384]{1,0:T(8,128)S(1)}, f32[8,384]{1,0:T(8,128)S(1)}, u32[]{:S(2)}, u32[]{:S(2)}) collective-permute-start(f32[8,384]{1,0:T(8,128)S(1)} %pad_maximum_fusion), channel_id=1, source_target_pairs={{0,16},{16,0},{32,48},{48,32},{64,80},{80,64},{96,112},{112,96},{1... | collective-permute-start | bytes 36872 | tf_op jit(solution)/shard_map/ppermute | solution.py:15
  18.8 0.8 collective-permute-done
  19.6 1.9 collective-permute-start.1
  21.5 2.5 %collective-permute-done.1 = f32[8,384]{1,0:T(8,128)S(1)} collective-permute-done((f32[8,384]{1,0:T(8,128)S(1)}, f32[8,384]{1,0:T(8,128)S(1)}, u32[]{:S(2)}, u32[]{:S(2)}) %collective-permute-start.1) | collective-permute-done | bytes 12320 | tf_op jit(solution)/shard_map/ppermute | solution.py:15
  24.0 1.9 collective-permute-start.2
  25.9 4.0 %collective-permute-done.2 = f32[8,384]{1,0:T(8,128)S(1)} collective-permute-done((f32[8,384]{1,0:T(8,128)S(1)}, f32[8,384]{1,0:T(8,128)S(1)}, u32[]{:S(2)}, u32[]{:S(2)}) %collective-permute-start.2) | collective-permute-done | bytes 12320 | tf_op jit(solution)/shard_map/ppermute | solution.py:15
  30.0 1.9 collective-permute-start.3
  31.9 2.9 %collective-permute-done.3 = f32[8,384]{1,0:T(8,128)S(1)} collective-permute-done((f32[8,384]{1,0:T(8,128)S(1)}, f32[8,384]{1,0:T(8,128)S(1)}, u32[]{:S(2)}, u32[]{:S(2)}) %collective-permute-start.3) | collective-permute-done | bytes 12320 | tf_op jit(solution)/shard_map/ppermute | solution.py:15
  34.8 1.9 collective-permute-start.4
  36.7 4.1 %collective-permute-done.4 = f32[8,384]{1,0:T(8,128)S(1)} collective-permute-done((f32[8,384]{1,0:T(8,128)S(1)}, f32[8,384]{1,0:T(8,128)S(1)}, u32[]{:S(2)}, u32[]{:S(2)}) %collective-permute-start.4) | collective-permute-done | bytes 12320 | tf_op jit(solution)/shard_map/ppermute | solution.py:15
  40.8 80.3 %all-gather.3.cloned.1.call-done = bf16[16384,256]{1,0:T(8,128)(2,1)} async-done(((bf16[1024,256]{1,0:T(8,128)(2,1)}), bf16[16384,256]{1,0:T(8,128)(2,1)}) %all-gather.3.cloned.1.call-update) | async-done | bytes 8388624 | tf_op jit(solution)/shard_map/all_gather | solution.py:36
  121.1 4.7 %fusion.11 = f32[16,256,1]{1,2,0:T(1,128)S(1)} fusion(bf16[16,1024,256]{2,1,0:T(8,128)(2,1)} %bitcast.30), kind=kOutput, calls=%fused_computation.25 | convolution fusion | flops 8388608 | bytes 8404992 | tf_op jit(solution)/shard_map/dot_general | solution.py:42
  125.8 1.0 copy-done
  126.9 2.5 %fusion.5 = f32[16,256,256]{2,1,0:T(8,128)S(1)} fusion(bf16[16,1024,256]{2,1,0:T(8,128)(2,1)S(1)} %bitcast.31, bf16[1024,256]{1,0:T(8,128)(2,1)S(1)} %copy-done.2), kind=kOutput, calls=%fused_computation.9 | convolution fusion | flops 2147483648 | bytes 13107200 | tf_op jit(solution)/shard_map/dot_general | solution.py:38
  129.5 1.9 copy-done.1
  131.4 0.2 fusion.1
  131.5 2.8 %collective-permute-start.5 = (f32[16,144,256]{2,1,0:T(8,128)S(1)}, f32[16,144,256]{2,1,0:T(8,128)}, u32[]{:S(2)}, u32[]{:S(2)}) collective-permute-start(f32[16,144,256]{2,1,0:T(8,128)S(1)} %fusion.1), channel_id=1, source_target_pairs={{0,16},{16,0},{32,48},{48,32},{64,80},{80,64},{96,112},{112,96},{1... | collective-permute-start | bytes 7077896 | tf_op jit(solution)/shard_map/ppermute | solution.py:59
  134.3 4.3 %collective-permute-done.5 = f32[16,144,256]{2,1,0:T(8,128)} collective-permute-done((f32[16,144,256]{2,1,0:T(8,128)S(1)}, f32[16,144,256]{2,1,0:T(8,128)}, u32[]{:S(2)}, u32[]{:S(2)}) %collective-permute-start.5) | collective-permute-done | bytes 2359328 | tf_op jit(solution)/shard_map/ppermute | solution.py:59
  138.6 4.1 %fusion.4 = f32[16,144,256]{2,1,0:T(8,128)} fusion(f32[16,144,256]{2,1,0:T(8,128)} %collective-permute-done.5, s32[]{:T(128)S(6)} %select_n.19, f32[16,2,128,256]{3,2,1,0:T(8,128)} %bitcast.33, f32[16,2,16,256]{3,2,1,0:T(8,128)S(1)} %bitcast.37), kind=kLoop, calls=%fused_computation.8 | loop fusion | flops 1179648 | bytes 9437188 | tf_op jit(solution)/shard_map/add | solution.py:59
  142.7 7.2 %all-to-all-start = ((f32[32,72,256]{2,1,0:T(8,128)}), f32[32,72,256]{2,1,0:T(8,128)S(1)}, u32[]{:S(2)}, u32[]{:S(2)}) async-start(f32[32,72,256]{2,1,0:T(8,128)} %bitcast.35), calls=%async_computation | async-start | bytes 4718592 | tf_op jit(solution)/shard_map/all_to_all | solution.py:61
  149.9 0.1 slice_reduce_fusion.1
  150.1 31.4 %all-to-all-done = f32[32,72,256]{2,1,0:T(8,128)S(1)} async-done(((f32[32,72,256]{2,1,0:T(8,128)}), f32[32,72,256]{2,1,0:T(8,128)S(1)}, u32[]{:S(2)}, u32[]{:S(2)}) %all-to-all-start) | async-done | bytes 2359328 | tf_op jit(solution)/shard_map/all_to_all | solution.py:61
  181.4 0.1 reduce_sum.28
  181.6 3.8 %collective-permute-start.6 = (f32[72,256]{1,0:T(8,128)S(1)}, f32[72,256]{1,0:T(8,128)S(1)}, u32[]{:S(2)}, u32[]{:S(2)}) collective-permute-start(f32[72,256]{1,0:T(8,128)S(1)} %get-tuple-element.11), channel_id=1, source_target_pairs={{0,16},{16,0},{32,48},{48,32},{64,80},{80,64},{96,112},{112,96},{1... | collective-permute-start | bytes 221192 | tf_op jit(solution)/shard_map/ppermute | solution.py:65
  185.4 0.7 subtract_multiply_fusion
  186.1 0.2 collective-permute-done.6
  186.3 0.1 fusion.8
  186.4 0.8 copy.15
  (17 shorter events, 0.2 us)
Async XLA Ops:
  7.2 113.9 %all-gather.3.cloned.1.call-start = ((), (), s32[]{:S(2)}) async-start(), calls=%async_computation.1 | async-start | bytes 8912896 | tf_op jit(solution)/shard_map/all_gather | solution.py:36
  10.0 9.6 %collective-permute-start = (f32[8,384]{1,0:T(8,128)S(1)}, f32[8,384]{1,0:T(8,128)S(1)}, u32[]{:S(2)}, u32[]{:S(2)}) collective-permute-start(f32[8,384]{1,0:T(8,128)S(1)} %pad_maximum_fusion), channel_id=1, source_target_pairs={{0,16},{16,0},{32,48},{48,32},{64,80},{80,64},{96,112},{112,96},{1... | collective-permute-start | bytes 36872 | tf_op jit(solution)/shard_map/ppermute | solution.py:15
  19.6 4.4 %collective-permute-start.1 = (f32[8,384]{1,0:T(8,128)S(1)}, f32[8,384]{1,0:T(8,128)S(1)}, u32[]{:S(2)}, u32[]{:S(2)}) collective-permute-start(f32[8,384]{1,0:T(8,128)S(1)} %fusion.15), channel_id=1, source_target_pairs={{0,32},{16,48},{32,0},{48,16},{64,96},{80,112},{96,64},{112,80},{1... | collective-permute-start | bytes 36872 | tf_op jit(solution)/shard_map/ppermute | solution.py:15
  24.0 5.9 %collective-permute-start.2 = (f32[8,384]{1,0:T(8,128)S(1)}, f32[8,384]{1,0:T(8,128)S(1)}, u32[]{:S(2)}, u32[]{:S(2)}) collective-permute-start(f32[8,384]{1,0:T(8,128)S(1)} %add.32), channel_id=1, source_target_pairs={{0,64},{16,80},{32,96},{48,112},{64,0},{80,16},{96,32},{112,48},{1... | collective-permute-start | bytes 36872 | tf_op jit(solution)/shard_map/ppermute | solution.py:15
  30.0 4.8 %collective-permute-start.3 = (f32[8,384]{1,0:T(8,128)S(1)}, f32[8,384]{1,0:T(8,128)S(1)}, u32[]{:S(2)}, u32[]{:S(2)}) collective-permute-start(f32[8,384]{1,0:T(8,128)S(1)} %add.33), channel_id=1, source_target_pairs={{0,128},{16,144},{32,160},{48,176},{64,192},{80,208},{96,224},{112... | collective-permute-start | bytes 36872 | tf_op jit(solution)/shard_map/ppermute | solution.py:15
  34.8 6.0 %collective-permute-start.4 = (f32[8,384]{1,0:T(8,128)S(1)}, f32[8,384]{1,0:T(8,128)S(1)}, u32[]{:S(2)}, u32[]{:S(2)}) collective-permute-start(f32[8,384]{1,0:T(8,128)S(1)} %add.34), channel_id=1, source_target_pairs={{0,256},{16,272},{32,288},{48,304},{64,320},{80,336},{96,352},{112... | collective-permute-start | bytes 36872 | tf_op jit(solution)/shard_map/ppermute | solution.py:15
  121.1 5.8 %copy-start = (bf16[16384,256]{1,0:T(8,128)(2,1)S(1)}, bf16[16384,256]{1,0:T(8,128)(2,1)}, u32[]{:S(2)}) copy-start(bf16[16384,256]{1,0:T(8,128)(2,1)} %all-gather.3.cloned.1.call-done) | copy-start | bytes 25165828
  121.1 5.8 %copy-start.2 = (bf16[1024,256]{1,0:T(8,128)(2,1)S(1)}, bf16[1024,256]{1,0:T(8,128)(2,1)}, u32[]{:S(2)}) copy-start(bf16[1024,256]{1,0:T(8,128)(2,1)} %param.2) | copy-start | bytes 1572868
  129.4 1.9 copy-start.1
  131.5 7.0 %collective-permute-start.5 = (f32[16,144,256]{2,1,0:T(8,128)S(1)}, f32[16,144,256]{2,1,0:T(8,128)}, u32[]{:S(2)}, u32[]{:S(2)}) collective-permute-start(f32[16,144,256]{2,1,0:T(8,128)S(1)} %fusion.1), channel_id=1, source_target_pairs={{0,16},{16,0},{32,48},{48,32},{64,80},{80,64},{96,112},{112,96},{1... | collective-permute-start | bytes 7077896 | tf_op jit(solution)/shard_map/ppermute | solution.py:59
  142.7 38.7 %all-to-all-start = ((f32[32,72,256]{2,1,0:T(8,128)}), f32[32,72,256]{2,1,0:T(8,128)S(1)}, u32[]{:S(2)}, u32[]{:S(2)}) async-start(f32[32,72,256]{2,1,0:T(8,128)} %bitcast.35), calls=%async_computation | async-start | bytes 4718592 | tf_op jit(solution)/shard_map/all_to_all | solution.py:61
  181.6 4.7 %collective-permute-start.6 = (f32[72,256]{1,0:T(8,128)S(1)}, f32[72,256]{1,0:T(8,128)S(1)}, u32[]{:S(2)}, u32[]{:S(2)}) collective-permute-start(f32[72,256]{1,0:T(8,128)S(1)} %get-tuple-element.11), channel_id=1, source_target_pairs={{0,16},{16,0},{32,48},{48,32},{64,80},{80,64},{96,112},{112,96},{1... | collective-permute-start | bytes 221192 | tf_op jit(solution)/shard_map/ppermute | solution.py:65
Sparse Core Ops, SparseCore 0:
  10.0 110.9 all-gather.2

commit v7 on v6

--- a/solution.py
+++ b/solution.py
@@ -5,7 +5,6 @@
 
 D = 4096
 CLASSES = 8
-EXTRA_ROWS = 16
 
 
 def butterfly_sum(x, axis, n):
@@ -33,21 +32,22 @@
     )
     stats = butterfly_sum(stats, "dp", n_dp)
 
+    own_sums = stats[:, :slice_width]
+    class_counts = stats[:, slice_width]
+    mean_rows = jnp.sum(own_sums, axis=0) / token_total
+    mean_all = lax.all_gather(mean_rows, "tensor", axis=0, tiled=True)
+
     gathered = lax.all_gather(activations, "tensor", axis=0, tiled=False)
-    gathered, stats = lax.optimization_barrier((gathered, stats))
+    gathered, stats, mean_all = lax.optimization_barrier((gathered, stats, mean_all))
     prod = lax.dot_general(
         gathered, activations, (((1,), (0,)), ((), ())), preferred_element_type=jnp.float32
     ).reshape(n_dp, col_width, slice_width)
-    ones = jnp.ones((8, tok_rows), jnp.bfloat16)
-    colsum = lax.dot_general(
-        gathered, ones, (((1,), (1,)), ((), ())), preferred_element_type=jnp.float32
-    )[..., 0].reshape(D)
-    extra = jnp.pad(
-        colsum.reshape(n_dp, 1, col_width),
-        ((0, 0), (0, EXTRA_ROWS - 1), (0, slice_width - col_width)),
-    )
-    payload = jnp.concatenate([prod, extra], axis=1)
-    rows = col_width + EXTRA_ROWS
+    own_sums = stats[:, :slice_width]
+    class_counts = stats[:, slice_width]
+    mean_rows = jnp.sum(own_sums, axis=0) / token_total
+    mean_cols = lax.dynamic_slice_in_dim(mean_all, lax.axis_index("dp") * col_width, col_width)
+    payload = prod
+    rows = col_width
     half_rows = rows // 2
 
     me = lax.axis_index("dp")
@@ -66,12 +66,7 @@
     total = jnp.where(
         core == 0, jnp.concatenate([mine, got], axis=0), jnp.concatenate([got, mine], axis=0)
     )
-    gram_cols = total[:col_width]
-    mean_cols = total[col_width, :col_width] / token_total
-
-    own_sums = stats[:, :slice_width]
-    class_counts = stats[:, slice_width]
-    mean_rows = jnp.sum(own_sums, axis=0) / token_total
+    gram_cols = total
     covariance = gram_cols.T / token_total - mean_rows[:, None] * mean_cols[None, :]
     cross_covariance = (own_sums - class_counts[:, None] * mean_rows[None, :]) / token_total
     return (covariance, cross_covariance)

time: 194 us -> 189 us (0.974)
  waiting for transfers between devices: 131 us -> 101 us
  blocking collectives: 0 us -> 26.6 us
    all_gather x0 -> x1, blocking collectives: none -> 26.6 us  [body(): mean_all = lax.all_gather(mean_rows, 'tensor', axis=0, tiled=True)]
    all_gather x1, waiting for transfers between devices: 80.3 us -> 53.9 us  [body(): gathered = lax.all_gather(activations, 'tensor', axis=0, tiled=False)]
    dot_general x1 -> x0, matrix products: 4.72 us -> none  [body(): lax.dot_general(gathered, ones, (((1,), (1,)), ((), ())), preferred_eleme...]
    dot_general x1, matrix products: 2.54 us -> 5.9 us  [body(): lax.dot_general(gathered, activations, (((1,), (0,)), ((), ())), preferre...]
    all_to_all x1, waiting for transfers between devices: 31.4 us -> 28.4 us  [body(): recv = lax.all_to_all(halves, 'dp', 0, 0, tiled=True)]
where the time goes in v7:
time: 189 us
  waiting for transfers between devices  101 us (53%)
  starting transfers between devices  30 us (16%)
  blocking collectives  26.6 us (14%)
  between operations  14.1 us (7%)
  matrix products  7.14 us (4%)
  other arithmetic  4.97 us (3%)
  local copies, waits for them, and re-layouts  4.42 us (2%)
    all_gather x1, waiting for transfers between devices, body(): gathered = lax.all_gather(activations, 'tensor', axis=0, tiled=False)  53.9 us
    all_to_all x1, waiting for transfers between devices, body(): recv = lax.all_to_all(halves, 'dp', 0, 0, tiled=True)  28.4 us
    all_gather x1, blocking collectives, body(): mean_all = lax.all_gather(mean_rows, 'tensor', axis=0, tiled=True)  26.6 us
    ppermute x5, starting transfers between devices, butterfly_sum(): x = x + lax.ppermute(x, axis, perm)  16.4 us
    ppermute x5, waiting for transfers between devices, butterfly_sum(): x = x + lax.ppermute(x, axis, perm)  14.3 us
    all_to_all x1, starting transfers between devices, body(): recv = lax.all_to_all(halves, 'dp', 0, 0, tiled=True)  7.23 us
    dot_general x1, matrix products, body(): lax.dot_general(gathered, activations, (((1,), (0,)), ((), ())), preferre...  5.9 us
    ppermute x1, waiting for transfers between devices, body(): chip_sum = keep + lax.ppermute(send, 'dp', core_swap)  3.97 us
  transfers between devices with their start and end apart: 9, of which 9 were waited for; matrix products, arithmetic and copies ran while one was open for 2% of the time, Pallas kernels for 0%

profile of v7, /device:TPU:1, one launch (start us, length us, event | category | flops | bytes accessed | tf_op | source)
XLA Modules:
  0.0 188.7 jit_solution(13402112052483701563)
XLA Ops:
  7.2 0.7 all-gather.4.cloned.1.call-update
  7.9 0.8 convert_reduce_fusion
  8.7 1.2 fusion.5
  9.9 0.1 broadcast_in_dim.2
  10.0 8.7 %collective-permute-start = (f32[8,384]{1,0:T(8,128)S(1)}, f32[8,384]{1,0:T(8,128)S(1)}, u32[]{:S(2)}, u32[]{:S(2)}) collective-permute-start(f32[8,384]{1,0:T(8,128)S(1)} %pad_maximum_fusion), channel_id=1, source_target_pairs={{0,16},{16,0},{32,48},{48,32},{64,80},{80,64},{96,112},{112,96},{1... | collective-permute-start | bytes 36872 | tf_op jit(solution)/shard_map/ppermute | solution.py:14
  18.8 0.8 collective-permute-done
  19.6 1.9 %collective-permute-start.1 = (f32[8,384]{1,0:T(8,128)S(1)}, f32[8,384]{1,0:T(8,128)S(1)}, u32[]{:S(2)}, u32[]{:S(2)}) collective-permute-start(f32[8,384]{1,0:T(8,128)S(1)} %fusion.7), channel_id=1, source_target_pairs={{0,32},{16,48},{32,0},{48,16},{64,96},{80,112},{96,64},{112,80},{1... | collective-permute-start | bytes 36872 | tf_op jit(solution)/shard_map/ppermute | solution.py:14
  21.5 2.5 %collective-permute-done.1 = f32[8,384]{1,0:T(8,128)S(1)} collective-permute-done((f32[8,384]{1,0:T(8,128)S(1)}, f32[8,384]{1,0:T(8,128)S(1)}, u32[]{:S(2)}, u32[]{:S(2)}) %collective-permute-start.1) | collective-permute-done | bytes 12320 | tf_op jit(solution)/shard_map/ppermute | solution.py:14
  24.0 1.9 %collective-permute-start.2 = (f32[8,384]{1,0:T(8,128)S(1)}, f32[8,384]{1,0:T(8,128)S(1)}, u32[]{:S(2)}, u32[]{:S(2)}) collective-permute-start(f32[8,384]{1,0:T(8,128)S(1)} %add.33), channel_id=1, source_target_pairs={{0,64},{16,80},{32,96},{48,112},{64,0},{80,16},{96,32},{112,48},{1... | collective-permute-start | bytes 36872 | tf_op jit(solution)/shard_map/ppermute | solution.py:14
  25.9 4.0 %collective-permute-done.2 = f32[8,384]{1,0:T(8,128)S(1)} collective-permute-done((f32[8,384]{1,0:T(8,128)S(1)}, f32[8,384]{1,0:T(8,128)S(1)}, u32[]{:S(2)}, u32[]{:S(2)}) %collective-permute-start.2) | collective-permute-done | bytes 12320 | tf_op jit(solution)/shard_map/ppermute | solution.py:14
  30.0 1.9 %collective-permute-start.3 = (f32[8,384]{1,0:T(8,128)S(1)}, f32[8,384]{1,0:T(8,128)S(1)}, u32[]{:S(2)}, u32[]{:S(2)}) collective-permute-start(f32[8,384]{1,0:T(8,128)S(1)} %add.34), channel_id=1, source_target_pairs={{0,128},{16,144},{32,160},{48,176},{64,192},{80,208},{96,224},{112... | collective-permute-start | bytes 36872 | tf_op jit(solution)/shard_map/ppermute | solution.py:14
  31.9 2.9 %collective-permute-done.3 = f32[8,384]{1,0:T(8,128)S(1)} collective-permute-done((f32[8,384]{1,0:T(8,128)S(1)}, f32[8,384]{1,0:T(8,128)S(1)}, u32[]{:S(2)}, u32[]{:S(2)}) %collective-permute-start.3) | collective-permute-done | bytes 12320 | tf_op jit(solution)/shard_map/ppermute | solution.py:14
  34.8 1.9 %collective-permute-start.4 = (f32[8,384]{1,0:T(8,128)S(1)}, f32[8,384]{1,0:T(8,128)S(1)}, u32[]{:S(2)}, u32[]{:S(2)}) collective-permute-start(f32[8,384]{1,0:T(8,128)S(1)} %add.35), channel_id=1, source_target_pairs={{0,256},{16,272},{32,288},{48,304},{64,320},{80,336},{96,352},{112... | collective-permute-start | bytes 36872 | tf_op jit(solution)/shard_map/ppermute | solution.py:14
  36.7 4.1 %collective-permute-done.4 = f32[8,384]{1,0:T(8,128)S(1)} collective-permute-done((f32[8,384]{1,0:T(8,128)S(1)}, f32[8,384]{1,0:T(8,128)S(1)}, u32[]{:S(2)}, u32[]{:S(2)}) %collective-permute-start.4) | collective-permute-done | bytes 12320 | tf_op jit(solution)/shard_map/ppermute | solution.py:14
  40.8 26.6 %all-gather.1 = f32[16,1,256]{2,1,0:T(1,128)S(1)} all-gather(f32[1,1,256]{2,1,0:T(1,128)S(1)} %bitcast.27), channel_id=1, replica_groups=mesh['dp'=32,'tensor'=16] {'tensor'}, dimensions={0}, use_global_device_ids=true | all-gather | bytes 17408 | tf_op jit(solution)/shard_map/all_gather | solution.py:38
  67.4 53.9 %all-gather.4.cloned.1.call-done = bf16[16384,256]{1,0:T(8,128)(2,1)} async-done(((bf16[1024,256]{1,0:T(8,128)(2,1)}), bf16[16384,256]{1,0:T(8,128)(2,1)}) %all-gather.4.cloned.1.call-update) | async-done | bytes 8388624 | tf_op jit(solution)/shard_map/all_gather | solution.py:40
  121.3 5.9 %fusion = f32[16,256,256]{2,1,0:T(8,128)S(1)} fusion(bf16[16,1024,256]{2,1,0:T(8,128)(2,1)} %bitcast.28, bf16[1024,256]{1,0:T(8,128)(2,1)} %param.2), kind=kOutput, calls=%fused_computation.2 | convolution fusion | flops 2147483648 | bytes 13107200 | tf_op jit(solution)/shard_map/dot_general | solution.py:42
  127.2 1.9 %copy-done = f32[16,256,256]{2,1,0:T(8,128)} copy-done((f32[16,256,256]{2,1,0:T(8,128)}, f32[16,256,256]{2,1,0:T(8,128)S(1)}, u32[]{:S(2)}) %copy-start) | copy-done | bytes 4194328
  129.1 1.5 dynamic-slice_bitcast_fusion
  130.6 2.7 %collective-permute-start.5 = (f32[16,128,256]{2,1,0:T(8,128)}, f32[16,128,256]{2,1,0:T(8,128)S(1)}, u32[]{:S(2)}, u32[]{:S(2)}) collective-permute-start(f32[16,128,256]{2,1,0:T(8,128)} %dynamic-slice_bitcast_fusion), channel_id=1, source_target_pairs={{0,16},{16,0},{32,48},{48,32},{64,80},{80,64},{96,112},{112,96},{1... | collective-permute-start | bytes 6291464 | tf_op jit(solution)/shard_map/ppermute | solution.py:59
  133.3 4.0 %collective-permute-done.5 = f32[16,128,256]{2,1,0:T(8,128)S(1)} collective-permute-done((f32[16,128,256]{2,1,0:T(8,128)}, f32[16,128,256]{2,1,0:T(8,128)S(1)}, u32[]{:S(2)}, u32[]{:S(2)}) %collective-permute-start.5) | collective-permute-done | bytes 2097184 | tf_op jit(solution)/shard_map/ppermute | solution.py:59
  137.3 3.2 %bitcast_add_fusion = f32[16,128,256]{2,1,0:T(8,128)} fusion(f32[16,128,256]{2,1,0:T(8,128)S(1)} %collective-permute-done.5, f32[16,2,128,256]{3,2,1,0:T(8,128)} %bitcast.25, s32[]{:T(128)S(6)} %select_n.22), kind=kLoop, calls=%fused_computation | loop fusion | flops 524288 | bytes 6291460 | tf_op jit(solution)/shard_map/add | solution.py:59
  140.5 7.2 %all-to-all-start = ((f32[32,64,256]{2,1,0:T(8,128)}), f32[32,64,256]{2,1,0:T(8,128)S(1)}, u32[]{:S(2)}, u32[]{:S(2)}) async-start(f32[32,64,256]{2,1,0:T(8,128)} %bitcast.7), calls=%async_computation | async-start | bytes 4194304 | tf_op jit(solution)/shard_map/all_to_all | solution.py:61
  147.7 0.1 slice_reduce_fusion.2
  147.9 28.4 %all-to-all-done = f32[32,64,256]{2,1,0:T(8,128)S(1)} async-done(((f32[32,64,256]{2,1,0:T(8,128)}), f32[32,64,256]{2,1,0:T(8,128)S(1)}, u32[]{:S(2)}, u32[]{:S(2)}) %all-to-all-start) | async-done | bytes 2097184 | tf_op jit(solution)/shard_map/all_to_all | solution.py:61
  176.3 0.1 reduce_sum.38
  176.5 3.6 %collective-permute-start.6 = (f32[64,256]{1,0:T(8,128)S(1)}, f32[64,256]{1,0:T(8,128)S(1)}, u32[]{:S(2)}, u32[]{:S(2)}) collective-permute-start(f32[64,256]{1,0:T(8,128)S(1)} %get-tuple-element.13), channel_id=1, source_target_pairs={{0,16},{16,0},{32,48},{48,32},{64,80},{80,64},{96,112},{112,96},{1... | collective-permute-start | bytes 196616 | tf_op jit(solution)/shard_map/ppermute | solution.py:65
  180.1 0.7 subtract_multiply_fusion
  180.8 0.1 dynamic_slice.21
  180.8 0.1 collective-permute-done.6
  181.0 0.1 fusion.4
  181.1 0.8 copy.10
  (13 shorter events, 0.1 us)
Async XLA Ops:
  7.2 114.1 %all-gather.4.cloned.1.call-start = ((), (), s32[]{:S(2)}) async-start(), calls=%async_computation.1 | async-start | bytes 8912896 | tf_op jit(solution)/shard_map/all_gather | solution.py:40
  10.0 9.6 %collective-permute-start = (f32[8,384]{1,0:T(8,128)S(1)}, f32[8,384]{1,0:T(8,128)S(1)}, u32[]{:S(2)}, u32[]{:S(2)}) collective-permute-start(f32[8,384]{1,0:T(8,128)S(1)} %pad_maximum_fusion), channel_id=1, source_target_pairs={{0,16},{16,0},{32,48},{48,32},{64,80},{80,64},{96,112},{112,96},{1... | collective-permute-start | bytes 36872 | tf_op jit(solution)/shard_map/ppermute | solution.py:14
  19.6 4.4 %collective-permute-start.1 = (f32[8,384]{1,0:T(8,128)S(1)}, f32[8,384]{1,0:T(8,128)S(1)}, u32[]{:S(2)}, u32[]{:S(2)}) collective-permute-start(f32[8,384]{1,0:T(8,128)S(1)} %fusion.7), channel_id=1, source_target_pairs={{0,32},{16,48},{32,0},{48,16},{64,96},{80,112},{96,64},{112,80},{1... | collective-permute-start | bytes 36872 | tf_op jit(solution)/shard_map/ppermute | solution.py:14
  24.0 5.9 %collective-permute-start.2 = (f32[8,384]{1,0:T(8,128)S(1)}, f32[8,384]{1,0:T(8,128)S(1)}, u32[]{:S(2)}, u32[]{:S(2)}) collective-permute-start(f32[8,384]{1,0:T(8,128)S(1)} %add.33), channel_id=1, source_target_pairs={{0,64},{16,80},{32,96},{48,112},{64,0},{80,16},{96,32},{112,48},{1... | collective-permute-start | bytes 36872 | tf_op jit(solution)/shard_map/ppermute | solution.py:14
  30.0 4.8 %collective-permute-start.3 = (f32[8,384]{1,0:T(8,128)S(1)}, f32[8,384]{1,0:T(8,128)S(1)}, u32[]{:S(2)}, u32[]{:S(2)}) collective-permute-start(f32[8,384]{1,0:T(8,128)S(1)} %add.34), channel_id=1, source_target_pairs={{0,128},{16,144},{32,160},{48,176},{64,192},{80,208},{96,224},{112... | collective-permute-start | bytes 36872 | tf_op jit(solution)/shard_map/ppermute | solution.py:14
  34.8 6.0 %collective-permute-start.4 = (f32[8,384]{1,0:T(8,128)S(1)}, f32[8,384]{1,0:T(8,128)S(1)}, u32[]{:S(2)}, u32[]{:S(2)}) collective-permute-start(f32[8,384]{1,0:T(8,128)S(1)} %add.35), channel_id=1, source_target_pairs={{0,256},{16,272},{32,288},{48,304},{64,320},{80,336},{96,352},{112... | collective-permute-start | bytes 36872 | tf_op jit(solution)/shard_map/ppermute | solution.py:14
  127.2 1.9 %copy-start = (f32[16,256,256]{2,1,0:T(8,128)}, f32[16,256,256]{2,1,0:T(8,128)S(1)}, u32[]{:S(2)}) copy-start(f32[16,256,256]{2,1,0:T(8,128)S(1)} %fusion) | copy-start | bytes 12582916
  130.6 6.7 %collective-permute-start.5 = (f32[16,128,256]{2,1,0:T(8,128)}, f32[16,128,256]{2,1,0:T(8,128)S(1)}, u32[]{:S(2)}, u32[]{:S(2)}) collective-permute-start(f32[16,128,256]{2,1,0:T(8,128)} %dynamic-slice_bitcast_fusion), channel_id=1, source_target_pairs={{0,16},{16,0},{32,48},{48,32},{64,80},{80,64},{96,112},{112,96},{1... | collective-permute-start | bytes 6291464 | tf_op jit(solution)/shard_map/ppermute | solution.py:59
  140.5 35.8 %all-to-all-start = ((f32[32,64,256]{2,1,0:T(8,128)}), f32[32,64,256]{2,1,0:T(8,128)S(1)}, u32[]{:S(2)}, u32[]{:S(2)}) async-start(f32[32,64,256]{2,1,0:T(8,128)} %bitcast.7), calls=%async_computation | async-start | bytes 4194304 | tf_op jit(solution)/shard_map/all_to_all | solution.py:61
  176.5 4.5 %collective-permute-start.6 = (f32[64,256]{1,0:T(8,128)S(1)}, f32[64,256]{1,0:T(8,128)S(1)}, u32[]{:S(2)}, u32[]{:S(2)}) collective-permute-start(f32[64,256]{1,0:T(8,128)S(1)} %get-tuple-element.13), channel_id=1, source_target_pairs={{0,16},{16,0},{32,48},{48,32},{64,80},{80,64},{96,112},{112,96},{1... | collective-permute-start | bytes 196616 | tf_op jit(solution)/shard_map/ppermute | solution.py:65
Sparse Core Ops, SparseCore 0:
  10.0 111.1 all-gather.3

commit v8 on v5

--- a/solution.py
+++ b/solution.py
@@ -33,20 +33,46 @@
     )
     stats = butterfly_sum(stats, "dp", n_dp)
 
-    gathered = lax.all_gather(activations, "tensor", axis=1, tiled=True)
-    gathered, stats = lax.optimization_barrier((gathered, stats))
-    prod = lax.dot_general(
-        gathered, activations, (((0,), (0,)), ((), ())), preferred_element_type=jnp.float32
-    ).reshape(n_dp, col_width, slice_width)
+    n_t = lax.axis_size("tensor")
+    assert n_t % 4 == 0 and n_dp == 2 * n_t and slice_width == 2 * col_width
+    win = n_t // 4
+    m = lax.axis_index("tensor")
+    blocks = [None] * (2 * win + 1)
+    blocks[win] = activations
+    fwd = activations
+    bwd = activations
+    up = [(i, (i + 1) % n_t) for i in range(n_t)]
+    down = [(i, (i - 1) % n_t) for i in range(n_t)]
+    for step in range(1, win + 1):
+        fwd = lax.ppermute(fwd, "tensor", up)
+        bwd = lax.ppermute(bwd, "tensor", down)
+        blocks[win - step] = fwd
+        blocks[win + step] = bwd
+    wst = jnp.stack(blocks)
+    contract = (((1,), (0,)), ((), ()))
+    near = lax.dot_general(wst, activations, contract, preferred_element_type=jnp.float32)
+    far_a = lax.dot_general(
+        wst[win + 1:], wst[0], contract, preferred_element_type=jnp.float32
+    )
+    n_b = n_t - 3 * win - 1
+    far_b = lax.dot_general(
+        wst[0], wst[win + 1:win + 1 + n_b], (((0,), (1,)), ((), ())),
+        preferred_element_type=jnp.float32,
+    ).transpose(1, 0, 2)
+    prod = jnp.concatenate([near, far_a, far_b], axis=0).reshape(n_dp, col_width, slice_width)
     ones = jnp.ones((8, tok_rows), jnp.bfloat16)
-    colsum = jnp.dot(ones, gathered, preferred_element_type=jnp.float32)[0]
+    cs = lax.dot_general(wst, ones, (((1,), (1,)), ((), ())), preferred_element_type=jnp.float32)[..., 0]
+    cs_off = jnp.concatenate([cs, cs[win + 1:], jnp.broadcast_to(cs[0], (n_b, slice_width))], axis=0)
     extra = jnp.pad(
-        colsum.reshape(n_dp, 1, col_width),
+        cs_off.reshape(n_dp, 1, col_width),
         ((0, 0), (0, EXTRA_ROWS - 1), (0, slice_width - col_width)),
     )
-    payload = jnp.concatenate([prod, extra], axis=1)
+    off_payload = jnp.concatenate([prod, extra], axis=1)
     rows = col_width + EXTRA_ROWS
     half_rows = rows // 2
+    shift = (2 * m - 2 * win) % n_dp
+    doubled = jnp.concatenate([off_payload, off_payload], axis=0)
+    payload = lax.dynamic_slice_in_dim(doubled, (n_dp - shift) % n_dp, n_dp, axis=0)
 
     me = lax.axis_index("dp")
     core = me & 1
@@ -64,9 +90,25 @@
     total = jnp.where(
         core == 0, jnp.concatenate([mine, got], axis=0), jnp.concatenate([got, mine], axis=0)
     )
-    gram_cols = total[:col_width]
-    mean_cols = total[col_width, :col_width] / token_total
-
+    me = lax.axis_index("dp")
+    perm = []
+    for src_s in range(n_dp):
+        for src_m in range(n_t):
+            o = (src_s // 2 - src_m) % n_t
+            h = src_s % 2
+            if win < o <= 2 * win:
+                dst = ((src_s - 2 * win) % n_dp, (src_m - win) % n_t)
+            elif o > 2 * win and o < n_t - win:
+                dst = ((2 * (src_m - win) + h) % n_dp, (src_m + o - 2 * win) % n_t)
+            else:
+                continue
+            perm.append((src_s * n_t + src_m, dst[0] * n_t + dst[1]))
+    moved = lax.ppermute(total, ("dp", "tensor"), perm)
+    my_o = (me // 2 - m) % n_t
+    is_far = jnp.logical_and(my_o > win, my_o < n_t - win)
+    final = jnp.where(is_far, moved, total)
+    gram_cols = final[:col_width]
+    mean_cols = final[col_width, :col_width] / token_total
     own_sums = stats[:, :slice_width]
     class_counts = stats[:, slice_width]
     mean_rows = jnp.sum(own_sums, axis=0) / token_total

time: 217 us -> 182 us (0.84)
  the two profiles are of different devices: /device:TPU:1 before, /device:TPU:17 now
where the time goes in v8:
time: 182 us; the launch traced here: 181 us
  waiting for transfers between devices  80 us (44%)
  starting transfers between devices  74.2 us (41%)
  local copies, waits for them, and re-layouts  10.2 us (6%)
  other arithmetic  8.6 us (5%)
  matrix products  7.12 us (4%)
    ppermute x4, waiting for transfers between devices, body(): fwd = lax.ppermute(fwd, 'tensor', up)  33.8 us
    ppermute x5, waiting for transfers between devices, butterfly_sum(): x = x + lax.ppermute(x, axis, perm)  27.2 us
    ppermute x4, starting transfers between devices, body(): bwd = lax.ppermute(bwd, 'tensor', down)  23.2 us
    ppermute x5, starting transfers between devices, butterfly_sum(): x = x + lax.ppermute(x, axis, perm)  16.4 us
    ppermute x1, waiting for transfers between devices, body(): moved = lax.ppermute(total, ('dp', 'tensor'), perm)  13.8 us
    ppermute x4, starting transfers between devices, body(): fwd = lax.ppermute(fwd, 'tensor', up)  9.27 us
    unnamed x34, local copies, waits for them, and re-layouts  7.5 us
    all_to_all x1, starting transfers between devices, body(): recv = lax.all_to_all(halves, 'dp', 0, 0, tiled=True)  7.42 us
  transfers between devices with their start and end apart: 17, of which 12 were waited for; matrix products, arithmetic and copies ran while one was open for 2% of the time, Pallas kernels for 0%

profile of v8, /device:TPU:17, one launch (start us, length us, event | category | flops | bytes accessed | tf_op | source)
XLA Modules:
  0.0 181.3 jit_solution(15387065249710976432)
XLA Ops:
  1.9 3.5 %collective-permute-start = (bf16[1024,256]{0,1:T(8,128)(2,1)S(1)}, bf16[1024,256]{0,1:T(8,128)(2,1)S(1)}, u32[]{:S(2)}, u32[]{:S(2)}) collective-permute-start(bf16[1024,256]{0,1:T(8,128)(2,1)S(1)} %copy.33), channel_id=1, source_target_pairs={{0,1},{1,2},{2,3},{3,4},{4,5},{5,6},{6,7},{7,8},{8,9},{9,10},{10,1... | collective-permute-start | bytes 1572872 | tf_op jit(solution)/shard_map/ppermute | solution.py:47
  5.4 9.5 %collective-permute-start.4 = (bf16[1024,256]{0,1:T(8,128)(2,1)S(1)}, bf16[1024,256]{0,1:T(8,128)(2,1)S(1)}, u32[]{:S(2)}, u32[]{:S(2)}) collective-permute-start(bf16[1024,256]{0,1:T(8,128)(2,1)S(1)} %copy.33), channel_id=1, source_target_pairs={{0,15},{1,0},{2,1},{3,2},{4,3},{5,4},{6,5},{7,6},{8,7},{9,8},{10,9... | collective-permute-start | bytes 1572872 | tf_op jit(solution)/shard_map/ppermute | solution.py:48
  14.9 9.7 %collective-permute-done = bf16[1024,256]{0,1:T(8,128)(2,1)S(1)} collective-permute-done((bf16[1024,256]{0,1:T(8,128)(2,1)S(1)}, bf16[1024,256]{0,1:T(8,128)(2,1)S(1)}, u32[]{:S(2)}, u32[]{:S(2)}) %collective-permute-start) | collective-permute-done | bytes 524320 | tf_op jit(solution)/shard_map/ppermute | solution.py:47
  24.6 1.9 %collective-permute-start.1 = (bf16[1024,256]{0,1:T(8,128)(2,1)S(1)}, bf16[1024,256]{0,1:T(8,128)(2,1)S(1)}, u32[]{:S(2)}, u32[]{:S(2)}) collective-permute-start(bf16[1024,256]{0,1:T(8,128)(2,1)S(1)} %collective-permute-done), channel_id=1, source_target_pairs={{0,1},{1,2},{2,3},{3,4},{4,5},{5,6},{6,7},{7,8},{8,9},{9,10},{10,1... | collective-permute-start | bytes 1572872 | tf_op jit(solution)/shard_map/ppermute | solution.py:47
  26.6 4.6 %collective-permute-start.5 = (bf16[1024,256]{0,1:T(8,128)(2,1)S(1)}, bf16[1024,256]{0,1:T(8,128)(2,1)S(1)}, u32[]{:S(2)}, u32[]{:S(2)}) collective-permute-start(bf16[1024,256]{0,1:T(8,128)(2,1)S(1)} %collective-permute-done.4), channel_id=1, source_target_pairs={{0,15},{1,0},{2,1},{3,2},{4,3},{5,4},{6,5},{7,6},{8,7},{9,8},{10,9... | collective-permute-start | bytes 1572872 | tf_op jit(solution)/shard_map/ppermute | solution.py:48
  31.1 8.8 %collective-permute-done.1 = bf16[1024,256]{0,1:T(8,128)(2,1)S(1)} collective-permute-done((bf16[1024,256]{0,1:T(8,128)(2,1)S(1)}, bf16[1024,256]{0,1:T(8,128)(2,1)S(1)}, u32[]{:S(2)}, u32[]{:S(2)}) %collective-permute-start.1) | collective-permute-done | bytes 524320 | tf_op jit(solution)/shard_map/ppermute | solution.py:47
  40.0 1.9 %collective-permute-start.2 = (bf16[1024,256]{0,1:T(8,128)(2,1)S(1)}, bf16[1024,256]{0,1:T(8,128)(2,1)}, u32[]{:S(2)}, u32[]{:S(2)}) collective-permute-start(bf16[1024,256]{0,1:T(8,128)(2,1)S(1)} %collective-permute-done.1), channel_id=1, source_target_pairs={{0,1},{1,2},{2,3},{3,4},{4,5},{5,6},{6,7},{7,8},{8,9},{9,10},{10,1... | collective-permute-start | bytes 1572872 | tf_op jit(solution)/shard_map/ppermute | solution.py:47
  41.9 4.6 %collective-permute-start.6 = (bf16[1024,256]{0,1:T(8,128)(2,1)S(1)}, bf16[1024,256]{0,1:T(8,128)(2,1)S(1)}, u32[]{:S(2)}, u32[]{:S(2)}) collective-permute-start(bf16[1024,256]{0,1:T(8,128)(2,1)S(1)} %collective-permute-done.5), channel_id=1, source_target_pairs={{0,15},{1,0},{2,1},{3,2},{4,3},{5,4},{6,5},{7,6},{8,7},{9,8},{10,9... | collective-permute-start | bytes 1572872 | tf_op jit(solution)/shard_map/ppermute | solution.py:48
  46.5 8.0 %collective-permute-done.2 = bf16[1024,256]{0,1:T(8,128)(2,1)} collective-permute-done((bf16[1024,256]{0,1:T(8,128)(2,1)S(1)}, bf16[1024,256]{0,1:T(8,128)(2,1)}, u32[]{:S(2)}, u32[]{:S(2)}) %collective-permute-start.2) | collective-permute-done | bytes 524320 | tf_op jit(solution)/shard_map/ppermute | solution.py:47
  54.5 1.9 %collective-permute-start.3 = (bf16[1024,256]{0,1:T(8,128)(2,1)}, bf16[1024,256]{0,1:T(8,128)(2,1)S(1)}, u32[]{:S(2)}, u32[]{:S(2)}) collective-permute-start(bf16[1024,256]{0,1:T(8,128)(2,1)} %collective-permute-done.2), channel_id=1, source_target_pairs={{0,1},{1,2},{2,3},{3,4},{4,5},{5,6},{6,7},{7,8},{8,9},{9,10},{10,1... | collective-permute-start | bytes 1572872 | tf_op jit(solution)/shard_map/ppermute | solution.py:47
  56.5 4.6 %collective-permute-start.7 = (bf16[1024,256]{0,1:T(8,128)(2,1)S(1)}, bf16[1024,256]{0,1:T(8,128)(2,1)S(1)}, u32[]{:S(2)}, u32[]{:S(2)}) collective-permute-start(bf16[1024,256]{0,1:T(8,128)(2,1)S(1)} %collective-permute-done.6), channel_id=1, source_target_pairs={{0,15},{1,0},{2,1},{3,2},{4,3},{5,4},{6,5},{7,6},{8,7},{9,8},{10,9... | collective-permute-start | bytes 1572872 | tf_op jit(solution)/shard_map/ppermute | solution.py:48
  61.1 7.3 %collective-permute-done.3 = bf16[1024,256]{0,1:T(8,128)(2,1)S(1)} collective-permute-done((bf16[1024,256]{0,1:T(8,128)(2,1)}, bf16[1024,256]{0,1:T(8,128)(2,1)S(1)}, u32[]{:S(2)}, u32[]{:S(2)}) %collective-permute-start.3) | collective-permute-done | bytes 524320 | tf_op jit(solution)/shard_map/ppermute | solution.py:47
  73.2 1.4 fusion.22
  75.5 2.0 %fusion.17 = f32[3,256,256]{2,1,0:T(8,128)S(1)} fusion(bf16[1,1024,256]{1,2,0:T(8,128)(2,1)} %bitcast.66, bf16[1,1024,256]{1,2,0:T(8,128)(2,1)} %bitcast.64, bf16[1,1024,256]{1,2,0:T(8,128)(2,1)S(1)} %bitcast.62, bf16[1024,256]{0,1:T(8,128)(2,1)} %copy-done.7), kind=kOutput, calls=%fused_computation.24 | convolution fusion | flops 404226048 | bytes 2883584 | tf_op jit(solution)/shard_map/dot_general | solution.py:58
  77.5 2.3 %fusion.3 = f32[4,256,256]{2,1,0:T(8,128)S(1)} fusion(bf16[1,1024,256]{1,2,0:T(8,128)(2,1)} %bitcast.68, bf16[1,1024,256]{1,2,0:T(8,128)(2,1)} %bitcast.67, bf16[1,1024,256]{1,2,0:T(8,128)(2,1)} %bitcast.65, bf16[1,1024,256]{1,2,0:T(8,128)(2,1)S(1)} %bitcast.63, bf16[1024,256]{0,1:T(8,128)(2,1)} %copy-done.7), kind=kOutput, calls=%fused_computation.10 | convolution fusion | flops 540016640 | bytes 3670016 | tf_op jit(solution)/shard_map/dot_general | solution.py:54
  80.2 3.7 %fusion.1 = f32[32,144,256]{2,1,0:T(8,128)S(1)} fusion(s32[]{:T(128)S(6)} %select_n.52, f32[32,128,256]{2,1,0:T(8,128)S(1)} %bitcast.60, f32[32,16,256]{2,1,0:T(8,128)} %pad.4), kind=kLoop, calls=%fused_computation.5 | loop fusion | flops 3538944 | bytes 9437188 | tf_op jit(solution)/shard_map/concatenate | solution.py:74
  83.9 2.1 %copy-done = f32[32,144,256]{2,1,0:T(8,128)} copy-done((f32[32,144,256]{2,1,0:T(8,128)}, f32[32,144,256]{2,1,0:T(8,128)S(1)}, u32[]{:S(2)}) %copy-start) | copy-done | bytes 4718616
  86.0 1.6 dynamic-slice_bitcast_fusion
  87.6 5.7 %collective-permute-start.8 = (f32[16,144,256]{2,1,0:T(8,128)}, f32[16,144,256]{2,1,0:T(8,128)S(1)}, u32[]{:S(2)}, u32[]{:S(2)}) collective-permute-start(f32[16,144,256]{2,1,0:T(8,128)} %dynamic-slice_bitcast_fusion), channel_id=1, source_target_pairs={{0,16},{16,0},{32,48},{48,32},{64,80},{80,64},{96,112},{112,96},{1... | collective-permute-start | bytes 7077896 | tf_op jit(solution)/shard_map/ppermute | solution.py:83
  93.3 4.3 %collective-permute-done.8 = f32[16,144,256]{2,1,0:T(8,128)S(1)} collective-permute-done((f32[16,144,256]{2,1,0:T(8,128)}, f32[16,144,256]{2,1,0:T(8,128)S(1)}, u32[]{:S(2)}, u32[]{:S(2)}) %collective-permute-start.8) | collective-permute-done | bytes 2359328 | tf_op jit(solution)/shard_map/ppermute | solution.py:83
  97.7 3.4 %bitcast_add_fusion = f32[16,144,256]{2,1,0:T(8,128)} fusion(f32[16,144,256]{2,1,0:T(8,128)S(1)} %collective-permute-done.8, f32[16,2,144,256]{3,2,1,0:T(8,128)} %bitcast.59, s32[]{:T(128)S(6)} %select_n.53), kind=kLoop, calls=%fused_computation.8 | loop fusion | flops 589824 | bytes 7077892 | tf_op jit(solution)/shard_map/add | solution.py:83
  101.1 7.4 %all-to-all-start = ((f32[32,72,256]{2,1,0:T(8,128)}), f32[32,72,256]{2,1,0:T(8,128)S(1)}, u32[]{:S(2)}, u32[]{:S(2)}) async-start(f32[32,72,256]{2,1,0:T(8,128)} %bitcast.19), calls=%async_computation | async-start | bytes 4718592 | tf_op jit(solution)/shard_map/all_to_all | solution.py:85
  108.9 2.3 %collective-permute-start.11 = (f32[8,384]{1,0:T(8,128)S(1)}, f32[8,384]{1,0:T(8,128)S(1)}, u32[]{:S(2)}, u32[]{:S(2)}) collective-permute-start(f32[8,384]{1,0:T(8,128)S(1)} %pad_maximum_fusion.2), channel_id=1, source_target_pairs={{0,16},{16,0},{32,48},{48,32},{64,80},{80,64},{96,112},{112,96},{1... | collective-permute-start | bytes 36872 | tf_op jit(solution)/shard_map/ppermute | solution.py:15
  112.0 3.1 %collective-permute-start.12 = (f32[8,384]{1,0:T(8,128)S(1)}, f32[8,384]{1,0:T(8,128)S(1)}, u32[]{:S(2)}, u32[]{:S(2)}) collective-permute-start(f32[8,384]{1,0:T(8,128)S(1)} %fusion.34), channel_id=1, source_target_pairs={{0,32},{16,48},{32,0},{48,16},{64,96},{80,112},{96,64},{112,80},{1... | collective-permute-start | bytes 36872 | tf_op jit(solution)/shard_map/ppermute | solution.py:15
  115.1 20.8 %collective-permute-done.12 = f32[8,384]{1,0:T(8,128)S(1)} collective-permute-done((f32[8,384]{1,0:T(8,128)S(1)}, f32[8,384]{1,0:T(8,128)S(1)}, u32[]{:S(2)}, u32[]{:S(2)}) %collective-permute-start.12) | collective-permute-done | bytes 12320 | tf_op jit(solution)/shard_map/ppermute | solution.py:15
  135.9 4.5 %collective-permute-start.13 = (f32[8,384]{1,0:T(8,128)S(1)}, f32[8,384]{1,0:T(8,128)S(1)}, u32[]{:S(2)}, u32[]{:S(2)}) collective-permute-start(f32[8,384]{1,0:T(8,128)S(1)} %add.54), channel_id=1, source_target_pairs={{0,64},{16,80},{32,96},{48,112},{64,0},{80,16},{96,32},{112,48},{1... | collective-permute-start | bytes 36872 | tf_op jit(solution)/shard_map/ppermute | solution.py:15
  141.9 3.7 %collective-permute-start.14 = (f32[8,384]{1,0:T(8,128)S(1)}, f32[8,384]{1,0:T(8,128)S(1)}, u32[]{:S(2)}, u32[]{:S(2)}) collective-permute-start(f32[8,384]{1,0:T(8,128)S(1)} %add.55), channel_id=1, source_target_pairs={{0,128},{16,144},{32,160},{48,176},{64,192},{80,208},{96,224},{112... | collective-permute-start | bytes 36872 | tf_op jit(solution)/shard_map/ppermute | solution.py:15
  146.6 2.7 %collective-permute-start.15 = (f32[8,384]{1,0:T(8,128)S(1)}, f32[8,384]{1,0:T(8,128)S(1)}, u32[]{:S(2)}, u32[]{:S(2)}) collective-permute-start(f32[8,384]{1,0:T(8,128)S(1)} %add.56), channel_id=1, source_target_pairs={{0,256},{16,272},{32,288},{48,304},{64,320},{80,336},{96,352},{112... | collective-permute-start | bytes 36872 | tf_op jit(solution)/shard_map/ppermute | solution.py:15
  149.4 3.1 %collective-permute-done.15 = f32[8,384]{1,0:T(8,128)S(1)} collective-permute-done((f32[8,384]{1,0:T(8,128)S(1)}, f32[8,384]{1,0:T(8,128)S(1)}, u32[]{:S(2)}, u32[]{:S(2)}) %collective-permute-start.15) | collective-permute-done | bytes 12320 | tf_op jit(solution)/shard_map/ppermute | solution.py:15
  152.8 6.3 %collective-permute-start.9 = (f32[72,256]{1,0:T(8,128)S(1)}, f32[72,256]{1,0:T(8,128)S(1)}, u32[]{:S(2)}, u32[]{:S(2)}) collective-permute-start(f32[72,256]{1,0:T(8,128)S(1)} %get-tuple-element.7), channel_id=1, source_target_pairs={{0,16},{16,0},{32,48},{48,32},{64,80},{80,64},{96,112},{112,96},{1... | collective-permute-start | bytes 221192 | tf_op jit(solution)/shard_map/ppermute | solution.py:89
  160.0 5.9 %collective-permute-start.10 = (f32[144,256]{1,0:T(8,128)S(1)}, f32[144,256]{1,0:T(8,128)S(1)}, u32[]{:S(2)}, u32[]{:S(2)}) collective-permute-start(f32[144,256]{1,0:T(8,128)S(1)} %maximum_select_fusion), channel_id=1, source_target_pairs={{5,40},{6,72},{7,104},{8,388},{9,389},{10,390},{11,391},{21,56},{2... | collective-permute-start | bytes 442376 | tf_op jit(solution)/shard_map/ppermute | solution.py:106
  166.6 13.8 %collective-permute-done.10 = f32[144,256]{1,0:T(8,128)S(1)} collective-permute-done((f32[144,256]{1,0:T(8,128)S(1)}, f32[144,256]{1,0:T(8,128)S(1)}, u32[]{:S(2)}, u32[]{:S(2)}) %collective-permute-start.10) | collective-permute-done | bytes 147488 | tf_op jit(solution)/shard_map/ppermute | solution.py:106
  (71 shorter events, 13.5 us)
Async XLA Ops:
  1.9 22.7 %collective-permute-start = (bf16[1024,256]{0,1:T(8,128)(2,1)S(1)}, bf16[1024,256]{0,1:T(8,128)(2,1)S(1)}, u32[]{:S(2)}, u32[]{:S(2)}) collective-permute-start(bf16[1024,256]{0,1:T(8,128)(2,1)S(1)} %copy.33), channel_id=1, source_target_pairs={{0,1},{1,2},{2,3},{3,4},{4,5},{5,6},{6,7},{7,8},{8,9},{9,10},{10,1... | collective-permute-start | bytes 1572872 | tf_op jit(solution)/shard_map/ppermute | solution.py:47
  5.4 21.1 %collective-permute-start.4 = (bf16[1024,256]{0,1:T(8,128)(2,1)S(1)}, bf16[1024,256]{0,1:T(8,128)(2,1)S(1)}, u32[]{:S(2)}, u32[]{:S(2)}) collective-permute-start(bf16[1024,256]{0,1:T(8,128)(2,1)S(1)} %copy.33), channel_id=1, source_target_pairs={{0,15},{1,0},{2,1},{3,2},{4,3},{5,4},{6,5},{7,6},{8,7},{9,8},{10,9... | collective-permute-start | bytes 1572872 | tf_op jit(solution)/shard_map/ppermute | solution.py:48
  24.6 15.3 %collective-permute-start.1 = (bf16[1024,256]{0,1:T(8,128)(2,1)S(1)}, bf16[1024,256]{0,1:T(8,128)(2,1)S(1)}, u32[]{:S(2)}, u32[]{:S(2)}) collective-permute-start(bf16[1024,256]{0,1:T(8,128)(2,1)S(1)} %collective-permute-done), channel_id=1, source_target_pairs={{0,1},{1,2},{2,3},{3,4},{4,5},{5,6},{6,7},{7,8},{8,9},{9,10},{10,1... | collective-permute-start | bytes 1572872 | tf_op jit(solution)/shard_map/ppermute | solution.py:47
  26.6 45.3 %copy-start.3 = (bf16[1024,256]{0,1:T(8,128)(2,1)}, bf16[1024,256]{0,1:T(8,128)(2,1)S(1)}, u32[]{:S(2)}) copy-start(bf16[1024,256]{0,1:T(8,128)(2,1)S(1)} %collective-permute-done.4) | copy-start | bytes 1572868
  26.6 15.3 %collective-permute-start.5 = (bf16[1024,256]{0,1:T(8,128)(2,1)S(1)}, bf16[1024,256]{0,1:T(8,128)(2,1)S(1)}, u32[]{:S(2)}, u32[]{:S(2)}) collective-permute-start(bf16[1024,256]{0,1:T(8,128)(2,1)S(1)} %collective-permute-done.4), channel_id=1, source_target_pairs={{0,15},{1,0},{2,1},{3,2},{4,3},{5,4},{6,5},{7,6},{8,7},{9,8},{10,9... | collective-permute-start | bytes 1572872 | tf_op jit(solution)/shard_map/ppermute | solution.py:48
  40.0 6.5 %copy-start.8 = (bf16[1024,256]{0,1:T(8,128)(2,1)}, bf16[1024,256]{0,1:T(8,128)(2,1)S(1)}, u32[]{:S(2)}) copy-start(bf16[1024,256]{0,1:T(8,128)(2,1)S(1)} %collective-permute-done.1) | copy-start | bytes 1572868
  40.0 14.6 %collective-permute-start.2 = (bf16[1024,256]{0,1:T(8,128)(2,1)S(1)}, bf16[1024,256]{0,1:T(8,128)(2,1)}, u32[]{:S(2)}, u32[]{:S(2)}) collective-permute-start(bf16[1024,256]{0,1:T(8,128)(2,1)S(1)} %collective-permute-done.1), channel_id=1, source_target_pairs={{0,1},{1,2},{2,3},{3,4},{4,5},{5,6},{6,7},{7,8},{8,9},{9,10},{10,1... | collective-permute-start | bytes 1572872 | tf_op jit(solution)/shard_map/ppermute | solution.py:47
  41.9 31.3 %copy-start.5 = (bf16[1024,256]{0,1:T(8,128)(2,1)}, bf16[1024,256]{0,1:T(8,128)(2,1)S(1)}, u32[]{:S(2)}) copy-start(bf16[1024,256]{0,1:T(8,128)(2,1)S(1)} %collective-permute-done.5) | copy-start | bytes 1572868
  41.9 14.6 %collective-permute-start.6 = (bf16[1024,256]{0,1:T(8,128)(2,1)S(1)}, bf16[1024,256]{0,1:T(8,128)(2,1)S(1)}, u32[]{:S(2)}, u32[]{:S(2)}) collective-permute-start(bf16[1024,256]{0,1:T(8,128)(2,1)S(1)} %collective-permute-done.5), channel_id=1, source_target_pairs={{0,15},{1,0},{2,1},{3,2},{4,3},{5,4},{6,5},{7,6},{8,7},{9,8},{10,9... | collective-permute-start | bytes 1572872 | tf_op jit(solution)/shard_map/ppermute | solution.py:48
  54.5 13.8 %collective-permute-start.3 = (bf16[1024,256]{0,1:T(8,128)(2,1)}, bf16[1024,256]{0,1:T(8,128)(2,1)S(1)}, u32[]{:S(2)}, u32[]{:S(2)}) collective-permute-start(bf16[1024,256]{0,1:T(8,128)(2,1)} %collective-permute-done.2), channel_id=1, source_target_pairs={{0,1},{1,2},{2,3},{3,4},{4,5},{5,6},{6,7},{7,8},{8,9},{9,10},{10,1... | collective-permute-start | bytes 1572872 | tf_op jit(solution)/shard_map/ppermute | solution.py:47
  56.5 16.7 %copy-start.6 = (bf16[1024,256]{0,1:T(8,128)(2,1)}, bf16[1024,256]{0,1:T(8,128)(2,1)S(1)}, u32[]{:S(2)}) copy-start(bf16[1024,256]{0,1:T(8,128)(2,1)S(1)} %collective-permute-done.6) | copy-start | bytes 1572868
  56.5 14.4 %collective-permute-start.7 = (bf16[1024,256]{0,1:T(8,128)(2,1)S(1)}, bf16[1024,256]{0,1:T(8,128)(2,1)S(1)}, u32[]{:S(2)}, u32[]{:S(2)}) collective-permute-start(bf16[1024,256]{0,1:T(8,128)(2,1)S(1)} %collective-permute-done.6), channel_id=1, source_target_pairs={{0,15},{1,0},{2,1},{3,2},{4,3},{5,4},{6,5},{7,6},{8,7},{9,8},{10,9... | collective-permute-start | bytes 1572872 | tf_op jit(solution)/shard_map/ppermute | solution.py:48
  68.4 3.5 %copy-start.7 = (bf16[1024,256]{0,1:T(8,128)(2,1)}, bf16[1024,256]{0,1:T(8,128)(2,1)S(1)}, u32[]{:S(2)}) copy-start(bf16[1024,256]{0,1:T(8,128)(2,1)S(1)} %collective-permute-done.3) | copy-start | bytes 1572868
  70.8 2.4 %copy-start.1 = (bf16[1024,256]{1,0:T(8,128)(2,1)S(1)}, bf16[1024,256]{1,0:T(8,128)(2,1)}, u32[]{:S(2)}) copy-start(bf16[1024,256]{1,0:T(8,128)(2,1)} %param.2) | copy-start | bytes 1572868
  71.0 0.8 copy-start.9
  73.2 2.3 %copy-start.4 = (bf16[1024,256]{0,1:T(8,128)(2,1)S(1)}, bf16[1024,256]{0,1:T(8,128)(2,1)}, u32[]{:S(2)}) copy-start(bf16[1024,256]{0,1:T(8,128)(2,1)} %copy-done.3) | copy-start | bytes 1572868
  83.9 2.1 %copy-start = (f32[32,144,256]{2,1,0:T(8,128)}, f32[32,144,256]{2,1,0:T(8,128)S(1)}, u32[]{:S(2)}) copy-start(f32[32,144,256]{2,1,0:T(8,128)S(1)} %fusion.1) | copy-start | bytes 14155780
  87.6 10.1 %collective-permute-start.8 = (f32[16,144,256]{2,1,0:T(8,128)}, f32[16,144,256]{2,1,0:T(8,128)S(1)}, u32[]{:S(2)}, u32[]{:S(2)}) collective-permute-start(f32[16,144,256]{2,1,0:T(8,128)} %dynamic-slice_bitcast_fusion), channel_id=1, source_target_pairs={{0,16},{16,0},{32,48},{48,32},{64,80},{80,64},{96,112},{112,96},{1... | collective-permute-start | bytes 7077896 | tf_op jit(solution)/shard_map/ppermute | solution.py:83
  93.3 15.2 %copy-start.10 = (s32[1024]{0:T(1024)S(1)}, s32[1024]{0:T(1024)}, u32[]{:S(2)}) copy-start(s32[1024]{0:T(1024)} %param.3) | copy-start | bytes 12292
  93.3 15.3 %copy-start.2 = (bf16[1024,256]{1,0:T(8,128)(2,1)S(1)}, bf16[1024,256]{1,0:T(8,128)(2,1)}, u32[]{:S(2)}) copy-start(bf16[1024,256]{1,0:T(8,128)(2,1)} %param.2) | copy-start | bytes 1572868
  101.1 51.5 %all-to-all-start = ((f32[32,72,256]{2,1,0:T(8,128)}), f32[32,72,256]{2,1,0:T(8,128)S(1)}, u32[]{:S(2)}, u32[]{:S(2)}) async-start(f32[32,72,256]{2,1,0:T(8,128)} %bitcast.19), calls=%async_computation | async-start | bytes 4718592 | tf_op jit(solution)/shard_map/all_to_all | solution.py:85
  108.9 3.1 %collective-permute-start.11 = (f32[8,384]{1,0:T(8,128)S(1)}, f32[8,384]{1,0:T(8,128)S(1)}, u32[]{:S(2)}, u32[]{:S(2)}) collective-permute-start(f32[8,384]{1,0:T(8,128)S(1)} %pad_maximum_fusion.2), channel_id=1, source_target_pairs={{0,16},{16,0},{32,48},{48,32},{64,80},{80,64},{96,112},{112,96},{1... | collective-permute-start | bytes 36872 | tf_op jit(solution)/shard_map/ppermute | solution.py:15
  112.0 23.9 %collective-permute-start.12 = (f32[8,384]{1,0:T(8,128)S(1)}, f32[8,384]{1,0:T(8,128)S(1)}, u32[]{:S(2)}, u32[]{:S(2)}) collective-permute-start(f32[8,384]{1,0:T(8,128)S(1)} %fusion.34), channel_id=1, source_target_pairs={{0,32},{16,48},{32,0},{48,16},{64,96},{80,112},{96,64},{112,80},{1... | collective-permute-start | bytes 36872 | tf_op jit(solution)/shard_map/ppermute | solution.py:15
  135.9 5.9 %collective-permute-start.13 = (f32[8,384]{1,0:T(8,128)S(1)}, f32[8,384]{1,0:T(8,128)S(1)}, u32[]{:S(2)}, u32[]{:S(2)}) collective-permute-start(f32[8,384]{1,0:T(8,128)S(1)} %add.54), channel_id=1, source_target_pairs={{0,64},{16,80},{32,96},{48,112},{64,0},{80,16},{96,32},{112,48},{1... | collective-permute-start | bytes 36872 | tf_op jit(solution)/shard_map/ppermute | solution.py:15
  141.9 4.8 %collective-permute-start.14 = (f32[8,384]{1,0:T(8,128)S(1)}, f32[8,384]{1,0:T(8,128)S(1)}, u32[]{:S(2)}, u32[]{:S(2)}) collective-permute-start(f32[8,384]{1,0:T(8,128)S(1)} %add.55), channel_id=1, source_target_pairs={{0,128},{16,144},{32,160},{48,176},{64,192},{80,208},{96,224},{112... | collective-permute-start | bytes 36872 | tf_op jit(solution)/shard_map/ppermute | solution.py:15
  146.6 5.9 %collective-permute-start.15 = (f32[8,384]{1,0:T(8,128)S(1)}, f32[8,384]{1,0:T(8,128)S(1)}, u32[]{:S(2)}, u32[]{:S(2)}) collective-permute-start(f32[8,384]{1,0:T(8,128)S(1)} %add.56), channel_id=1, source_target_pairs={{0,256},{16,272},{32,288},{48,304},{64,320},{80,336},{96,352},{112... | collective-permute-start | bytes 36872 | tf_op jit(solution)/shard_map/ppermute | solution.py:15
  152.8 7.2 %collective-permute-start.9 = (f32[72,256]{1,0:T(8,128)S(1)}, f32[72,256]{1,0:T(8,128)S(1)}, u32[]{:S(2)}, u32[]{:S(2)}) collective-permute-start(f32[72,256]{1,0:T(8,128)S(1)} %get-tuple-element.7), channel_id=1, source_target_pairs={{0,16},{16,0},{32,48},{48,32},{64,80},{80,64},{96,112},{112,96},{1... | collective-permute-start | bytes 221192 | tf_op jit(solution)/shard_map/ppermute | solution.py:89
  160.0 20.4 %collective-permute-start.10 = (f32[144,256]{1,0:T(8,128)S(1)}, f32[144,256]{1,0:T(8,128)S(1)}, u32[]{:S(2)}, u32[]{:S(2)}) collective-permute-start(f32[144,256]{1,0:T(8,128)S(1)} %maximum_select_fusion), channel_id=1, source_target_pairs={{5,40},{6,72},{7,104},{8,388},{9,389},{10,390},{11,391},{21,56},{2... | collective-permute-start | bytes 442376 | tf_op jit(solution)/shard_map/ppermute | solution.py:106

commit v9 on v8

--- a/solution.py
+++ b/solution.py
@@ -49,6 +49,7 @@
         blocks[win - step] = fwd
         blocks[win + step] = bwd
     wst = jnp.stack(blocks)
+    wst, stats = lax.optimization_barrier((wst, stats))
     contract = (((1,), (0,)), ((), ()))
     near = lax.dot_general(wst, activations, contract, preferred_element_type=jnp.float32)
     far_a = lax.dot_general(

time: 182 us -> 190 us (1.044)
  waiting for transfers between devices: 80 us -> 90.9 us
  local copies, waits for them, and re-layouts: 10.2 us -> 7.97 us
  other arithmetic: 8.6 us -> 10.7 us
  starting transfers between devices: 74.2 us -> 72.2 us
    all_to_all x1, waiting for transfers between devices: 0.01 us -> 30.8 us  [body(): recv = lax.all_to_all(halves, 'dp', 0, 0, tiled=True)]
    ppermute x5, waiting for transfers between devices: 27.2 us -> 9.26 us  [butterfly_sum(): x = x + lax.ppermute(x, axis, perm)]
    ppermute x4, waiting for transfers between devices: 33.8 us -> 26.8 us  [body(): fwd = lax.ppermute(fwd, 'tensor', up)]
    ppermute x1, starting transfers between devices: 6.34 us -> 2.3 us  [body(): got = lax.ppermute(other, 'dp', core_swap)]
    ppermute x4, waiting for transfers between devices: 0.01 us -> 3.94 us  [body(): bwd = lax.ppermute(bwd, 'tensor', down)]
    unnamed x34 -> x15, local copies, waits for them, and re-layouts: 7.5 us -> 5.26 us
    ppermute x1, starting transfers between devices: 5.71 us -> 7.64 us  [body(): chip_sum = keep + lax.ppermute(send, 'dp', core_swap)]
  transfers between devices with their start and end apart: 17 -> 17, of which waited for: 12 -> 13; matrix products, arithmetic and copies ran while one was open for 2% -> 3% of each run, Pallas kernels for 0% -> 0%
where the time goes in v9:
time: 190 us; the launch traced here: 189 us
  waiting for transfers between devices  90.9 us (48%)
  starting transfers between devices  72.2 us (38%)
  other arithmetic  10.7 us (6%)
  local copies, waits for them, and re-layouts  7.97 us (4%)
  matrix products  6.67 us (4%)
    all_to_all x1, waiting for transfers between devices, body(): recv = lax.all_to_all(halves, 'dp', 0, 0, tiled=True)  30.8 us
    ppermute x4, waiting for transfers between devices, body(): fwd = lax.ppermute(fwd, 'tensor', up)  26.8 us
    ppermute x4, starting transfers between devices, body(): bwd = lax.ppermute(bwd, 'tensor', down)  23.1 us
    ppermute x5, starting transfers between devices, butterfly_sum(): x = x + lax.ppermute(x, axis, perm)  17.5 us
    ppermute x1, waiting for transfers between devices, body(): moved = lax.ppermute(total, ('dp', 'tensor'), perm)  15 us
    ppermute x4, starting transfers between devices, body(): fwd = lax.ppermute(fwd, 'tensor', up)  9.41 us
    ppermute x5, waiting for transfers between devices, butterfly_sum(): x = x + lax.ppermute(x, axis, perm)  9.26 us
    ppermute x1, starting transfers between devices, body(): chip_sum = keep + lax.ppermute(send, 'dp', core_swap)  7.64 us
  transfers between devices with their start and end apart: 17, of which 13 were waited for; matrix products, arithmetic and copies ran while one was open for 3% of the time, Pallas kernels for 0%

profile of v9, /device:TPU:17, one launch (start us, length us, event | category | flops | bytes accessed | tf_op | source)
XLA Modules:
  0.0 189.5 jit_solution(810835702300581167)
XLA Ops:
  0.6 3.7 %collective-permute-start = (bf16[1024,256]{1,0:T(8,128)(2,1)}, bf16[1024,256]{1,0:T(8,128)(2,1)S(1)}, u32[]{:S(2)}, u32[]{:S(2)}) collective-permute-start(bf16[1024,256]{1,0:T(8,128)(2,1)} %param.2), channel_id=1, source_target_pairs={{0,1},{1,2},{2,3},{3,4},{4,5},{5,6},{6,7},{7,8},{8,9},{9,10},{10,1... | collective-permute-start | bytes 1572872 | tf_op jit(solution)/shard_map/ppermute | solution.py:47
  4.3 9.5 %collective-permute-start.4 = (bf16[1024,256]{1,0:T(8,128)(2,1)}, bf16[1024,256]{1,0:T(8,128)(2,1)S(1)}, u32[]{:S(2)}, u32[]{:S(2)}) collective-permute-start(bf16[1024,256]{1,0:T(8,128)(2,1)} %param.2), channel_id=1, source_target_pairs={{0,15},{1,0},{2,1},{3,2},{4,3},{5,4},{6,5},{7,6},{8,7},{9,8},{10,9... | collective-permute-start | bytes 1572872 | tf_op jit(solution)/shard_map/ppermute | solution.py:48
  13.8 9.9 %collective-permute-done = bf16[1024,256]{1,0:T(8,128)(2,1)S(1)} collective-permute-done((bf16[1024,256]{1,0:T(8,128)(2,1)}, bf16[1024,256]{1,0:T(8,128)(2,1)S(1)}, u32[]{:S(2)}, u32[]{:S(2)}) %collective-permute-start) | collective-permute-done | bytes 524320 | tf_op jit(solution)/shard_map/ppermute | solution.py:47
  23.7 1.9 %collective-permute-start.1 = (bf16[1024,256]{1,0:T(8,128)(2,1)S(1)}, bf16[1024,256]{1,0:T(8,128)(2,1)S(1)}, u32[]{:S(2)}, u32[]{:S(2)}) collective-permute-start(bf16[1024,256]{1,0:T(8,128)(2,1)S(1)} %collective-permute-done), channel_id=1, source_target_pairs={{0,1},{1,2},{2,3},{3,4},{4,5},{5,6},{6,7},{7,8},{8,9},{9,10},{10,1... | collective-permute-start | bytes 1572872 | tf_op jit(solution)/shard_map/ppermute | solution.py:47
  25.7 4.6 %collective-permute-start.5 = (bf16[1024,256]{1,0:T(8,128)(2,1)S(1)}, bf16[1024,256]{1,0:T(8,128)(2,1)S(1)}, u32[]{:S(2)}, u32[]{:S(2)}) collective-permute-start(bf16[1024,256]{1,0:T(8,128)(2,1)S(1)} %collective-permute-done.4), channel_id=1, source_target_pairs={{0,15},{1,0},{2,1},{3,2},{4,3},{5,4},{6,5},{7,6},{8,7},{9,8},{10,9... | collective-permute-start | bytes 1572872 | tf_op jit(solution)/shard_map/ppermute | solution.py:48
  30.2 8.8 %collective-permute-done.1 = bf16[1024,256]{1,0:T(8,128)(2,1)S(1)} collective-permute-done((bf16[1024,256]{1,0:T(8,128)(2,1)S(1)}, bf16[1024,256]{1,0:T(8,128)(2,1)S(1)}, u32[]{:S(2)}, u32[]{:S(2)}) %collective-permute-start.1) | collective-permute-done | bytes 524320 | tf_op jit(solution)/shard_map/ppermute | solution.py:47
  39.0 1.9 %collective-permute-start.2 = (bf16[1024,256]{1,0:T(8,128)(2,1)S(1)}, bf16[1024,256]{1,0:T(8,128)(2,1)}, u32[]{:S(2)}, u32[]{:S(2)}) collective-permute-start(bf16[1024,256]{1,0:T(8,128)(2,1)S(1)} %collective-permute-done.1), channel_id=1, source_target_pairs={{0,1},{1,2},{2,3},{3,4},{4,5},{5,6},{6,7},{7,8},{8,9},{9,10},{10,1... | collective-permute-start | bytes 1572872 | tf_op jit(solution)/shard_map/ppermute | solution.py:47
  41.0 4.6 %collective-permute-start.6 = (bf16[1024,256]{1,0:T(8,128)(2,1)S(1)}, bf16[1024,256]{1,0:T(8,128)(2,1)S(1)}, u32[]{:S(2)}, u32[]{:S(2)}) collective-permute-start(bf16[1024,256]{1,0:T(8,128)(2,1)S(1)} %collective-permute-done.5), channel_id=1, source_target_pairs={{0,15},{1,0},{2,1},{3,2},{4,3},{5,4},{6,5},{7,6},{8,7},{9,8},{10,9... | collective-permute-start | bytes 1572872 | tf_op jit(solution)/shard_map/ppermute | solution.py:48
  45.6 8.1 %collective-permute-done.2 = bf16[1024,256]{1,0:T(8,128)(2,1)} collective-permute-done((bf16[1024,256]{1,0:T(8,128)(2,1)S(1)}, bf16[1024,256]{1,0:T(8,128)(2,1)}, u32[]{:S(2)}, u32[]{:S(2)}) %collective-permute-start.2) | collective-permute-done | bytes 524320 | tf_op jit(solution)/shard_map/ppermute | solution.py:47
  53.6 1.9 %collective-permute-start.3 = (bf16[1024,256]{1,0:T(8,128)(2,1)}, bf16[1024,256]{1,0:T(8,128)(2,1)}, u32[]{:S(2)}, u32[]{:S(2)}) collective-permute-start(bf16[1024,256]{1,0:T(8,128)(2,1)} %collective-permute-done.2), channel_id=1, source_target_pairs={{0,1},{1,2},{2,3},{3,4},{4,5},{5,6},{6,7},{7,8},{8,9},{9,10},{10,1... | collective-permute-start | bytes 1572872 | tf_op jit(solution)/shard_map/ppermute | solution.py:47
  57.7 4.9 %collective-permute-start.8 = (f32[8,384]{1,0:T(8,128)S(1)}, f32[8,384]{1,0:T(8,128)S(1)}, u32[]{:S(2)}, u32[]{:S(2)}) collective-permute-start(f32[8,384]{1,0:T(8,128)S(1)} %pad_maximum_fusion.2), channel_id=1, source_target_pairs={{0,16},{16,0},{32,48},{48,32},{64,80},{80,64},{96,112},{112,96},{1... | collective-permute-start | bytes 36872 | tf_op jit(solution)/shard_map/ppermute | solution.py:15
  63.4 3.1 %collective-permute-start.9 = (f32[8,384]{1,0:T(8,128)S(1)}, f32[8,384]{1,0:T(8,128)S(1)}, u32[]{:S(2)}, u32[]{:S(2)}) collective-permute-start(f32[8,384]{1,0:T(8,128)S(1)} %fusion.23), channel_id=1, source_target_pairs={{0,32},{16,48},{32,0},{48,16},{64,96},{80,112},{96,64},{112,80},{1... | collective-permute-start | bytes 36872 | tf_op jit(solution)/shard_map/ppermute | solution.py:15
  66.5 1.7 collective-permute-done.9
  68.2 4.6 %collective-permute-start.10 = (f32[8,384]{1,0:T(8,128)S(1)}, f32[8,384]{1,0:T(8,128)S(1)}, u32[]{:S(2)}, u32[]{:S(2)}) collective-permute-start(f32[8,384]{1,0:T(8,128)S(1)} %add.48), channel_id=1, source_target_pairs={{0,64},{16,80},{32,96},{48,112},{64,0},{80,16},{96,32},{112,48},{1... | collective-permute-start | bytes 36872 | tf_op jit(solution)/shard_map/ppermute | solution.py:15
  74.1 2.9 %collective-permute-start.11 = (f32[8,384]{1,0:T(8,128)S(1)}, f32[8,384]{1,0:T(8,128)S(1)}, u32[]{:S(2)}, u32[]{:S(2)}) collective-permute-start(f32[8,384]{1,0:T(8,128)S(1)} %add.49), channel_id=1, source_target_pairs={{0,128},{16,144},{32,160},{48,176},{64,192},{80,208},{96,224},{112... | collective-permute-start | bytes 36872 | tf_op jit(solution)/shard_map/ppermute | solution.py:15
  78.6 2.0 %collective-permute-start.12 = (f32[8,384]{1,0:T(8,128)S(1)}, f32[8,384]{1,0:T(8,128)S(1)}, u32[]{:S(2)}, u32[]{:S(2)}) collective-permute-start(f32[8,384]{1,0:T(8,128)S(1)} %add.50), channel_id=1, source_target_pairs={{0,256},{16,272},{32,288},{48,304},{64,320},{80,336},{96,352},{112... | collective-permute-start | bytes 36872 | tf_op jit(solution)/shard_map/ppermute | solution.py:15
  80.6 3.9 %collective-permute-done.12 = f32[8,384]{1,0:T(8,128)S(1)} collective-permute-done((f32[8,384]{1,0:T(8,128)S(1)}, f32[8,384]{1,0:T(8,128)S(1)}, u32[]{:S(2)}, u32[]{:S(2)}) %collective-permute-start.12) | collective-permute-done | bytes 12320 | tf_op jit(solution)/shard_map/ppermute | solution.py:15
  84.5 4.4 %collective-permute-start.7 = (bf16[1024,256]{1,0:T(8,128)(2,1)S(1)}, bf16[1024,256]{1,0:T(8,128)(2,1)S(1)}, u32[]{:S(2)}, u32[]{:S(2)}) collective-permute-start(bf16[1024,256]{1,0:T(8,128)(2,1)S(1)} %collective-permute-done.6), channel_id=1, source_target_pairs={{0,15},{1,0},{2,1},{3,2},{4,3},{5,4},{6,5},{7,6},{8,7},{9,8},{10,9... | collective-permute-start | bytes 1572872 | tf_op jit(solution)/shard_map/ppermute | solution.py:48
  91.4 3.9 %collective-permute-done.7 = bf16[1024,256]{1,0:T(8,128)(2,1)S(1)} collective-permute-done((bf16[1024,256]{1,0:T(8,128)(2,1)S(1)}, bf16[1024,256]{1,0:T(8,128)(2,1)S(1)}, u32[]{:S(2)}, u32[]{:S(2)}) %collective-permute-start.7) | collective-permute-done | bytes 524320 | tf_op jit(solution)/shard_map/ppermute | solution.py:48
  97.6 1.7 fusion.9
  101.7 1.7 pad_maximum_fusion
  103.5 3.7 %fusion.1 = f32[32,144,256]{2,1,0:T(8,128)S(1)} fusion(s32[]{:T(128)S(6)} %select_n.52, f32[32,128,256]{2,1,0:T(8,128)S(1)} %bitcast.63, f32[32,16,256]{2,1,0:T(8,128)} %pad.4), kind=kLoop, calls=%fused_computation.5 | loop fusion | flops 3538944 | bytes 9437188 | tf_op jit(solution)/shard_map/concatenate | solution.py:75
  107.2 2.1 %copy-done = f32[32,144,256]{2,1,0:T(8,128)} copy-done((f32[32,144,256]{2,1,0:T(8,128)}, f32[32,144,256]{2,1,0:T(8,128)S(1)}, u32[]{:S(2)}) %copy-start) | copy-done | bytes 4718616
  109.3 1.6 dynamic-slice_bitcast_fusion
  110.9 7.6 %collective-permute-start.13 = (f32[16,144,256]{2,1,0:T(8,128)}, f32[16,144,256]{2,1,0:T(8,128)S(1)}, u32[]{:S(2)}, u32[]{:S(2)}) collective-permute-start(f32[16,144,256]{2,1,0:T(8,128)} %dynamic-slice_bitcast_fusion), channel_id=1, source_target_pairs={{0,16},{16,0},{32,48},{48,32},{64,80},{80,64},{96,112},{112,96},{1... | collective-permute-start | bytes 7077896 | tf_op jit(solution)/shard_map/ppermute | solution.py:84
  118.6 4.3 %collective-permute-done.13 = f32[16,144,256]{2,1,0:T(8,128)S(1)} collective-permute-done((f32[16,144,256]{2,1,0:T(8,128)}, f32[16,144,256]{2,1,0:T(8,128)S(1)}, u32[]{:S(2)}, u32[]{:S(2)}) %collective-permute-start.13) | collective-permute-done | bytes 2359328 | tf_op jit(solution)/shard_map/ppermute | solution.py:84
  122.9 3.4 %bitcast_add_fusion = f32[16,144,256]{2,1,0:T(8,128)} fusion(f32[16,144,256]{2,1,0:T(8,128)S(1)} %collective-permute-done.13, f32[16,2,144,256]{3,2,1,0:T(8,128)} %bitcast.62, s32[]{:T(128)S(6)} %select_n.53), kind=kLoop, calls=%fused_computation.8 | loop fusion | flops 589824 | bytes 7077892 | tf_op jit(solution)/shard_map/add | solution.py:84
  126.3 7.4 %all-to-all-start = ((f32[32,72,256]{2,1,0:T(8,128)}), f32[32,72,256]{2,1,0:T(8,128)S(1)}, u32[]{:S(2)}, u32[]{:S(2)}) async-start(f32[32,72,256]{2,1,0:T(8,128)} %bitcast.20), calls=%async_computation | async-start | bytes 4718592 | tf_op jit(solution)/shard_map/all_to_all | solution.py:86
  133.8 30.8 %all-to-all-done = f32[32,72,256]{2,1,0:T(8,128)S(1)} async-done(((f32[32,72,256]{2,1,0:T(8,128)}), f32[32,72,256]{2,1,0:T(8,128)S(1)}, u32[]{:S(2)}, u32[]{:S(2)}) %all-to-all-start) | async-done | bytes 2359328 | tf_op jit(solution)/shard_map/all_to_all | solution.py:86
  164.8 2.3 %collective-permute-start.14 = (f32[72,256]{1,0:T(8,128)S(1)}, f32[72,256]{1,0:T(8,128)S(1)}, u32[]{:S(2)}, u32[]{:S(2)}) collective-permute-start(f32[72,256]{1,0:T(8,128)S(1)} %get-tuple-element.11), channel_id=1, source_target_pairs={{0,16},{16,0},{32,48},{48,32},{64,80},{80,64},{96,112},{112,96},{1... | collective-permute-start | bytes 221192 | tf_op jit(solution)/shard_map/ppermute | solution.py:90
  168.0 4.9 %collective-permute-start.15 = (f32[144,256]{1,0:T(8,128)S(1)}, f32[144,256]{1,0:T(8,128)S(1)}, u32[]{:S(2)}, u32[]{:S(2)}) collective-permute-start(f32[144,256]{1,0:T(8,128)S(1)} %maximum_select_fusion), channel_id=1, source_target_pairs={{5,40},{6,72},{7,104},{8,388},{9,389},{10,390},{11,391},{21,56},{2... | collective-permute-start | bytes 442376 | tf_op jit(solution)/shard_map/ppermute | solution.py:107
  173.6 15.0 %collective-permute-done.15 = f32[144,256]{1,0:T(8,128)S(1)} collective-permute-done((f32[144,256]{1,0:T(8,128)S(1)}, f32[144,256]{1,0:T(8,128)S(1)}, u32[]{:S(2)}, u32[]{:S(2)}) %collective-permute-start.15) | collective-permute-done | bytes 147488 | tf_op jit(solution)/shard_map/ppermute | solution.py:107
  (52 shorter events, 15.4 us)
Async XLA Ops:
  0.6 90.6 %copy-start.1 = (bf16[1024,256]{1,0:T(8,128)(2,1)S(1)}, bf16[1024,256]{1,0:T(8,128)(2,1)}, u32[]{:S(2)}) copy-start(bf16[1024,256]{1,0:T(8,128)(2,1)} %param.2) | copy-start | bytes 1572868
  0.6 23.1 %collective-permute-start = (bf16[1024,256]{1,0:T(8,128)(2,1)}, bf16[1024,256]{1,0:T(8,128)(2,1)S(1)}, u32[]{:S(2)}, u32[]{:S(2)}) collective-permute-start(bf16[1024,256]{1,0:T(8,128)(2,1)} %param.2), channel_id=1, source_target_pairs={{0,1},{1,2},{2,3},{3,4},{4,5},{5,6},{6,7},{7,8},{8,9},{9,10},{10,1... | collective-permute-start | bytes 1572872 | tf_op jit(solution)/shard_map/ppermute | solution.py:47
  4.3 21.3 %collective-permute-start.4 = (bf16[1024,256]{1,0:T(8,128)(2,1)}, bf16[1024,256]{1,0:T(8,128)(2,1)S(1)}, u32[]{:S(2)}, u32[]{:S(2)}) collective-permute-start(bf16[1024,256]{1,0:T(8,128)(2,1)} %param.2), channel_id=1, source_target_pairs={{0,15},{1,0},{2,1},{3,2},{4,3},{5,4},{6,5},{7,6},{8,7},{9,8},{10,9... | collective-permute-start | bytes 1572872 | tf_op jit(solution)/shard_map/ppermute | solution.py:48
  23.7 15.3 %collective-permute-start.1 = (bf16[1024,256]{1,0:T(8,128)(2,1)S(1)}, bf16[1024,256]{1,0:T(8,128)(2,1)S(1)}, u32[]{:S(2)}, u32[]{:S(2)}) collective-permute-start(bf16[1024,256]{1,0:T(8,128)(2,1)S(1)} %collective-permute-done), channel_id=1, source_target_pairs={{0,1},{1,2},{2,3},{3,4},{4,5},{5,6},{6,7},{7,8},{8,9},{9,10},{10,1... | collective-permute-start | bytes 1572872 | tf_op jit(solution)/shard_map/ppermute | solution.py:47
  25.7 15.3 %collective-permute-start.5 = (bf16[1024,256]{1,0:T(8,128)(2,1)S(1)}, bf16[1024,256]{1,0:T(8,128)(2,1)S(1)}, u32[]{:S(2)}, u32[]{:S(2)}) collective-permute-start(bf16[1024,256]{1,0:T(8,128)(2,1)S(1)} %collective-permute-done.4), channel_id=1, source_target_pairs={{0,15},{1,0},{2,1},{3,2},{4,3},{5,4},{6,5},{7,6},{8,7},{9,8},{10,9... | collective-permute-start | bytes 1572872 | tf_op jit(solution)/shard_map/ppermute | solution.py:48
  39.0 14.6 %collective-permute-start.2 = (bf16[1024,256]{1,0:T(8,128)(2,1)S(1)}, bf16[1024,256]{1,0:T(8,128)(2,1)}, u32[]{:S(2)}, u32[]{:S(2)}) collective-permute-start(bf16[1024,256]{1,0:T(8,128)(2,1)S(1)} %collective-permute-done.1), channel_id=1, source_target_pairs={{0,1},{1,2},{2,3},{3,4},{4,5},{5,6},{6,7},{7,8},{8,9},{9,10},{10,1... | collective-permute-start | bytes 1572872 | tf_op jit(solution)/shard_map/ppermute | solution.py:47
  41.0 43.5 %collective-permute-start.6 = (bf16[1024,256]{1,0:T(8,128)(2,1)S(1)}, bf16[1024,256]{1,0:T(8,128)(2,1)S(1)}, u32[]{:S(2)}, u32[]{:S(2)}) collective-permute-start(bf16[1024,256]{1,0:T(8,128)(2,1)S(1)} %collective-permute-done.5), channel_id=1, source_target_pairs={{0,15},{1,0},{2,1},{3,2},{4,3},{5,4},{6,5},{7,6},{8,7},{9,8},{10,9... | collective-permute-start | bytes 1572872 | tf_op jit(solution)/shard_map/ppermute | solution.py:48
  53.6 35.3 %collective-permute-start.3 = (bf16[1024,256]{1,0:T(8,128)(2,1)}, bf16[1024,256]{1,0:T(8,128)(2,1)}, u32[]{:S(2)}, u32[]{:S(2)}) collective-permute-start(bf16[1024,256]{1,0:T(8,128)(2,1)} %collective-permute-done.2), channel_id=1, source_target_pairs={{0,1},{1,2},{2,3},{3,4},{4,5},{5,6},{6,7},{7,8},{8,9},{9,10},{10,1... | collective-permute-start | bytes 1572872 | tf_op jit(solution)/shard_map/ppermute | solution.py:47
  57.7 5.7 %collective-permute-start.8 = (f32[8,384]{1,0:T(8,128)S(1)}, f32[8,384]{1,0:T(8,128)S(1)}, u32[]{:S(2)}, u32[]{:S(2)}) collective-permute-start(f32[8,384]{1,0:T(8,128)S(1)} %pad_maximum_fusion.2), channel_id=1, source_target_pairs={{0,16},{16,0},{32,48},{48,32},{64,80},{80,64},{96,112},{112,96},{1... | collective-permute-start | bytes 36872 | tf_op jit(solution)/shard_map/ppermute | solution.py:15
  63.4 4.8 %collective-permute-start.9 = (f32[8,384]{1,0:T(8,128)S(1)}, f32[8,384]{1,0:T(8,128)S(1)}, u32[]{:S(2)}, u32[]{:S(2)}) collective-permute-start(f32[8,384]{1,0:T(8,128)S(1)} %fusion.23), channel_id=1, source_target_pairs={{0,32},{16,48},{32,0},{48,16},{64,96},{80,112},{96,64},{112,80},{1... | collective-permute-start | bytes 36872 | tf_op jit(solution)/shard_map/ppermute | solution.py:15
  68.2 5.9 %collective-permute-start.10 = (f32[8,384]{1,0:T(8,128)S(1)}, f32[8,384]{1,0:T(8,128)S(1)}, u32[]{:S(2)}, u32[]{:S(2)}) collective-permute-start(f32[8,384]{1,0:T(8,128)S(1)} %add.48), channel_id=1, source_target_pairs={{0,64},{16,80},{32,96},{48,112},{64,0},{80,16},{96,32},{112,48},{1... | collective-permute-start | bytes 36872 | tf_op jit(solution)/shard_map/ppermute | solution.py:15
  74.1 4.4 %collective-permute-start.11 = (f32[8,384]{1,0:T(8,128)S(1)}, f32[8,384]{1,0:T(8,128)S(1)}, u32[]{:S(2)}, u32[]{:S(2)}) collective-permute-start(f32[8,384]{1,0:T(8,128)S(1)} %add.49), channel_id=1, source_target_pairs={{0,128},{16,144},{32,160},{48,176},{64,192},{80,208},{96,224},{112... | collective-permute-start | bytes 36872 | tf_op jit(solution)/shard_map/ppermute | solution.py:15
  78.6 5.9 %collective-permute-start.12 = (f32[8,384]{1,0:T(8,128)S(1)}, f32[8,384]{1,0:T(8,128)S(1)}, u32[]{:S(2)}, u32[]{:S(2)}) collective-permute-start(f32[8,384]{1,0:T(8,128)S(1)} %add.50), channel_id=1, source_target_pairs={{0,256},{16,272},{32,288},{48,304},{64,320},{80,336},{96,352},{112... | collective-permute-start | bytes 36872 | tf_op jit(solution)/shard_map/ppermute | solution.py:15
  84.5 10.8 %collective-permute-start.7 = (bf16[1024,256]{1,0:T(8,128)(2,1)S(1)}, bf16[1024,256]{1,0:T(8,128)(2,1)S(1)}, u32[]{:S(2)}, u32[]{:S(2)}) collective-permute-start(bf16[1024,256]{1,0:T(8,128)(2,1)S(1)} %collective-permute-done.6), channel_id=1, source_target_pairs={{0,15},{1,0},{2,1},{3,2},{4,3},{5,4},{6,5},{7,6},{8,7},{9,8},{10,9... | collective-permute-start | bytes 1572872 | tf_op jit(solution)/shard_map/ppermute | solution.py:48
  107.2 2.1 %copy-start = (f32[32,144,256]{2,1,0:T(8,128)}, f32[32,144,256]{2,1,0:T(8,128)S(1)}, u32[]{:S(2)}) copy-start(f32[32,144,256]{2,1,0:T(8,128)S(1)} %fusion.1) | copy-start | bytes 14155780
  110.9 12.0 %collective-permute-start.13 = (f32[16,144,256]{2,1,0:T(8,128)}, f32[16,144,256]{2,1,0:T(8,128)S(1)}, u32[]{:S(2)}, u32[]{:S(2)}) collective-permute-start(f32[16,144,256]{2,1,0:T(8,128)} %dynamic-slice_bitcast_fusion), channel_id=1, source_target_pairs={{0,16},{16,0},{32,48},{48,32},{64,80},{80,64},{96,112},{112,96},{1... | collective-permute-start | bytes 7077896 | tf_op jit(solution)/shard_map/ppermute | solution.py:84
  126.3 38.3 %all-to-all-start = ((f32[32,72,256]{2,1,0:T(8,128)}), f32[32,72,256]{2,1,0:T(8,128)S(1)}, u32[]{:S(2)}, u32[]{:S(2)}) async-start(f32[32,72,256]{2,1,0:T(8,128)} %bitcast.20), calls=%async_computation | async-start | bytes 4718592 | tf_op jit(solution)/shard_map/all_to_all | solution.py:86
  164.8 3.2 %collective-permute-start.14 = (f32[72,256]{1,0:T(8,128)S(1)}, f32[72,256]{1,0:T(8,128)S(1)}, u32[]{:S(2)}, u32[]{:S(2)}) collective-permute-start(f32[72,256]{1,0:T(8,128)S(1)} %get-tuple-element.11), channel_id=1, source_target_pairs={{0,16},{16,0},{32,48},{48,32},{64,80},{80,64},{96,112},{112,96},{1... | collective-permute-start | bytes 221192 | tf_op jit(solution)/shard_map/ppermute | solution.py:90
  168.0 20.6 %collective-permute-start.15 = (f32[144,256]{1,0:T(8,128)S(1)}, f32[144,256]{1,0:T(8,128)S(1)}, u32[]{:S(2)}, u32[]{:S(2)}) collective-permute-start(f32[144,256]{1,0:T(8,128)S(1)} %maximum_select_fusion), channel_id=1, source_target_pairs={{5,40},{6,72},{7,104},{8,388},{9,389},{10,390},{11,391},{21,56},{2... | collective-permute-start | bytes 442376 | tf_op jit(solution)/shard_map/ppermute | solution.py:107

commit v10 on v8

--- a/solution.py
+++ b/solution.py
@@ -31,7 +31,6 @@
     stats = jnp.concatenate(
         [own_local, jnp.broadcast_to(local_counts[:, None], (CLASSES, 128))], axis=1
     )
-    stats = butterfly_sum(stats, "dp", n_dp)
 
     n_t = lax.axis_size("tensor")
     assert n_t % 4 == 0 and n_dp == 2 * n_t and slice_width == 2 * col_width
@@ -43,9 +42,14 @@
     bwd = activations
     up = [(i, (i + 1) % n_t) for i in range(n_t)]
     down = [(i, (i - 1) % n_t) for i in range(n_t)]
+    bfly = [1 << b for b in range(n_dp.bit_length() - 1)]
+    per_step = [bfly[i::win] for i in range(win)]
     for step in range(1, win + 1):
         fwd = lax.ppermute(fwd, "tensor", up)
         bwd = lax.ppermute(bwd, "tensor", down)
+        for k in per_step[step - 1]:
+            stats = stats + lax.ppermute(stats, "dp", [(i, i ^ k) for i in range(n_dp)])
+        fwd, bwd, stats = lax.optimization_barrier((fwd, bwd, stats))
         blocks[win - step] = fwd
         blocks[win + step] = bwd
     wst = jnp.stack(blocks)

time: 182 us -> 174 us (0.956)
  starting transfers between devices: 74.2 us -> 67.2 us
  waiting for transfers between devices: 80 us -> 76.9 us
    all_to_all x1, waiting for transfers between devices: 0.01 us -> 30.8 us  [body(): recv = lax.all_to_all(halves, 'dp', 0, 0, tiled=True)]
    ppermute x4, waiting for transfers between devices: 33.8 us -> 10.2 us  [body(): fwd = lax.ppermute(fwd, 'tensor', up)]
    ppermute x5, waiting for transfers between devices: 27.2 us -> 9.55 us  [body(): stats = stats + lax.ppermute(stats, 'dp', [(i, i ^ k) for i in range(n_dp)])]
    ppermute x4, waiting for transfers between devices: 0.01 us -> 5.23 us  [body(): bwd = lax.ppermute(bwd, 'tensor', down)]
    ppermute x1, starting transfers between devices: 6.34 us -> 2.3 us  [body(): got = lax.ppermute(other, 'dp', core_swap)]
    ppermute x4, starting transfers between devices: 23.2 us -> 20.1 us  [body(): bwd = lax.ppermute(bwd, 'tensor', down)]
    ppermute x1, waiting for transfers between devices: 13.8 us -> 16 us  [body(): moved = lax.ppermute(total, ('dp', 'tensor'), perm)]
    unnamed x34 -> x24, local copies, waits for them, and re-layouts: 7.5 us -> 6.52 us
  transfers between devices with their start and end apart: 17 -> 17, of which waited for: 12 -> 15; matrix products, arithmetic and copies ran while one was open for 2% -> 2% of each run, Pallas kernels for 0% -> 0%
where the time goes in v10:
time: 174 us; the launch traced here: 173 us
  waiting for transfers between devices  76.9 us (44%)
  starting transfers between devices  67.2 us (39%)
  local copies, waits for them, and re-layouts  10.3 us (6%)
  other arithmetic  9.28 us (5%)
  matrix products  8.17 us (5%)
    all_to_all x1, waiting for transfers between devices, body(): recv = lax.all_to_all(halves, 'dp', 0, 0, tiled=True)  30.8 us
    ppermute x4, starting transfers between devices, body(): bwd = lax.ppermute(bwd, 'tensor', down)  20.1 us
    ppermute x1, waiting for transfers between devices, body(): moved = lax.ppermute(total, ('dp', 'tensor'), perm)  16 us
    ppermute x5, starting transfers between devices, body(): stats = stats + lax.ppermute(stats, 'dp', [(i, i ^ k) for i in range(n_dp)])  15.5 us
    ppermute x4, starting transfers between devices, body(): fwd = lax.ppermute(fwd, 'tensor', up)  10.7 us
    ppermute x4, waiting for transfers between devices, body(): fwd = lax.ppermute(fwd, 'tensor', up)  10.2 us
    ppermute x5, waiting for transfers between devices, body(): stats = stats + lax.ppermute(stats, 'dp', [(i, i ^ k) for i in range(n_dp)])  9.55 us
    all_to_all x1, starting transfers between devices, body(): recv = lax.all_to_all(halves, 'dp', 0, 0, tiled=True)  7.41 us
  transfers between devices with their start and end apart: 17, of which 15 were waited for; matrix products, arithmetic and copies ran while one was open for 2% of the time, Pallas kernels for 0%

profile of v10, /device:TPU:17, one launch (start us, length us, event | category | flops | bytes accessed | tf_op | source)
XLA Modules:
  0.0 173.0 jit_solution(11807743604569220903)
XLA Ops:
  1.9 3.5 %collective-permute-start = (bf16[1024,256]{0,1:T(8,128)(2,1)S(1)}, bf16[1024,256]{0,1:T(8,128)(2,1)S(1)}, u32[]{:S(2)}, u32[]{:S(2)}) collective-permute-start(bf16[1024,256]{0,1:T(8,128)(2,1)S(1)} %copy.33), channel_id=1, source_target_pairs={{0,1},{1,2},{2,3},{3,4},{4,5},{5,6},{6,7},{7,8},{8,9},{9,10},{10,1... | collective-permute-start | bytes 1572872 | tf_op jit(solution)/shard_map/ppermute | solution.py:48
  5.4 9.5 %collective-permute-start.1 = (bf16[1024,256]{0,1:T(8,128)(2,1)S(1)}, bf16[1024,256]{0,1:T(8,128)(2,1)S(1)}, u32[]{:S(2)}, u32[]{:S(2)}) collective-permute-start(bf16[1024,256]{0,1:T(8,128)(2,1)S(1)} %copy.33), channel_id=1, source_target_pairs={{0,15},{1,0},{2,1},{3,2},{4,3},{5,4},{6,5},{7,6},{8,7},{9,8},{10,9... | collective-permute-start | bytes 1572872 | tf_op jit(solution)/shard_map/ppermute | solution.py:49
  17.1 2.9 %collective-permute-start.2 = (f32[8,384]{1,0:T(8,128)S(1)}, f32[8,384]{1,0:T(8,128)S(1)}, u32[]{:S(2)}, u32[]{:S(2)}) collective-permute-start(f32[8,384]{1,0:T(8,128)S(1)} %pad_maximum_fusion.2), channel_id=1, source_target_pairs={{0,16},{16,0},{32,48},{48,32},{64,80},{80,64},{96,112},{112,96},{1... | collective-permute-start | bytes 36872 | tf_op jit(solution)/shard_map/ppermute | solution.py:51
  20.8 2.0 %collective-permute-start.3 = (f32[8,384]{1,0:T(8,128)S(1)}, f32[8,384]{1,0:T(8,128)S(1)}, u32[]{:S(2)}, u32[]{:S(2)}) collective-permute-start(f32[8,384]{1,0:T(8,128)S(1)} %fusion.34), channel_id=1, source_target_pairs={{0,256},{16,272},{32,288},{48,304},{64,320},{80,336},{96,352},{112... | collective-permute-start | bytes 36872 | tf_op jit(solution)/shard_map/ppermute | solution.py:51
  22.7 4.0 %collective-permute-done.3 = f32[8,384]{1,0:T(8,128)S(1)} collective-permute-done((f32[8,384]{1,0:T(8,128)S(1)}, f32[8,384]{1,0:T(8,128)S(1)}, u32[]{:S(2)}, u32[]{:S(2)}) %collective-permute-start.3) | collective-permute-done | bytes 12320 | tf_op jit(solution)/shard_map/ppermute | solution.py:51
  26.7 4.1 %collective-permute-start.5 = (bf16[1024,256]{0,1:T(8,128)(2,1)S(1)}, bf16[1024,256]{0,1:T(8,128)(2,1)S(1)}, u32[]{:S(2)}, u32[]{:S(2)}) collective-permute-start(bf16[1024,256]{0,1:T(8,128)(2,1)S(1)} %collective-permute-done.1), channel_id=1, source_target_pairs={{0,15},{1,0},{2,1},{3,2},{4,3},{5,4},{6,5},{7,6},{8,7},{9,8},{10,9... | collective-permute-start | bytes 1572872 | tf_op jit(solution)/shard_map/ppermute | solution.py:49
  30.8 1.9 %collective-permute-start.4 = (bf16[1024,256]{0,1:T(8,128)(2,1)S(1)}, bf16[1024,256]{0,1:T(8,128)(2,1)S(1)}, u32[]{:S(2)}, u32[]{:S(2)}) collective-permute-start(bf16[1024,256]{0,1:T(8,128)(2,1)S(1)} %collective-permute-done), channel_id=1, source_target_pairs={{0,1},{1,2},{2,3},{3,4},{4,5},{5,6},{6,7},{7,8},{8,9},{9,10},{10,1... | collective-permute-start | bytes 1572872 | tf_op jit(solution)/shard_map/ppermute | solution.py:48
  32.8 3.1 %collective-permute-start.6 = (f32[8,384]{1,0:T(8,128)S(1)}, f32[8,384]{1,0:T(8,128)S(1)}, u32[]{:S(2)}, u32[]{:S(2)}) collective-permute-start(f32[8,384]{1,0:T(8,128)S(1)} %add.48), channel_id=1, source_target_pairs={{0,32},{16,48},{32,0},{48,16},{64,96},{80,112},{96,64},{112,80},{1... | collective-permute-start | bytes 36872 | tf_op jit(solution)/shard_map/ppermute | solution.py:51
  35.9 1.6 collective-permute-done.6
  37.5 3.1 %collective-permute-done.5 = bf16[1024,256]{0,1:T(8,128)(2,1)S(1)} collective-permute-done((bf16[1024,256]{0,1:T(8,128)(2,1)S(1)}, bf16[1024,256]{0,1:T(8,128)(2,1)S(1)}, u32[]{:S(2)}, u32[]{:S(2)}) %collective-permute-start.5) | collective-permute-done | bytes 524320 | tf_op jit(solution)/shard_map/ppermute | solution.py:49
  40.6 5.0 %collective-permute-done.4 = bf16[1024,256]{0,1:T(8,128)(2,1)S(1)} collective-permute-done((bf16[1024,256]{0,1:T(8,128)(2,1)S(1)}, bf16[1024,256]{0,1:T(8,128)(2,1)S(1)}, u32[]{:S(2)}, u32[]{:S(2)}) %collective-permute-start.4) | collective-permute-done | bytes 524320 | tf_op jit(solution)/shard_map/ppermute | solution.py:48
  45.6 1.9 %collective-permute-start.8 = (bf16[1024,256]{0,1:T(8,128)(2,1)S(1)}, bf16[1024,256]{0,1:T(8,128)(2,1)S(1)}, u32[]{:S(2)}, u32[]{:S(2)}) collective-permute-start(bf16[1024,256]{0,1:T(8,128)(2,1)S(1)} %collective-permute-done.5), channel_id=1, source_target_pairs={{0,15},{1,0},{2,1},{3,2},{4,3},{5,4},{6,5},{7,6},{8,7},{9,8},{10,9... | collective-permute-start | bytes 1572872 | tf_op jit(solution)/shard_map/ppermute | solution.py:49
  47.5 3.4 %collective-permute-start.7 = (bf16[1024,256]{0,1:T(8,128)(2,1)S(1)}, bf16[1024,256]{0,1:T(8,128)(2,1)}, u32[]{:S(2)}, u32[]{:S(2)}) collective-permute-start(bf16[1024,256]{0,1:T(8,128)(2,1)S(1)} %collective-permute-done.4), channel_id=1, source_target_pairs={{0,1},{1,2},{2,3},{3,4},{4,5},{5,6},{6,7},{7,8},{8,9},{9,10},{10,1... | collective-permute-start | bytes 1572872 | tf_op jit(solution)/shard_map/ppermute | solution.py:48
  50.9 4.7 %collective-permute-start.9 = (f32[8,384]{1,0:T(8,128)S(1)}, f32[8,384]{1,0:T(8,128)S(1)}, u32[]{:S(2)}, u32[]{:S(2)}) collective-permute-start(f32[8,384]{1,0:T(8,128)S(1)} %add.49), channel_id=1, source_target_pairs={{0,64},{16,80},{32,96},{48,112},{64,0},{80,16},{96,32},{112,48},{1... | collective-permute-start | bytes 36872 | tf_op jit(solution)/shard_map/ppermute | solution.py:51
  58.4 3.1 %collective-permute-done.7 = bf16[1024,256]{0,1:T(8,128)(2,1)} collective-permute-done((bf16[1024,256]{0,1:T(8,128)(2,1)S(1)}, bf16[1024,256]{0,1:T(8,128)(2,1)}, u32[]{:S(2)}, u32[]{:S(2)}) %collective-permute-start.7) | collective-permute-done | bytes 524320 | tf_op jit(solution)/shard_map/ppermute | solution.py:48
  61.6 1.9 %collective-permute-start.10 = (bf16[1024,256]{0,1:T(8,128)(2,1)}, bf16[1024,256]{0,1:T(8,128)(2,1)}, u32[]{:S(2)}, u32[]{:S(2)}) collective-permute-start(bf16[1024,256]{0,1:T(8,128)(2,1)} %collective-permute-done.7), channel_id=1, source_target_pairs={{0,1},{1,2},{2,3},{3,4},{4,5},{5,6},{6,7},{7,8},{8,9},{9,10},{10,1... | collective-permute-start | bytes 1572872 | tf_op jit(solution)/shard_map/ppermute | solution.py:48
  63.5 4.6 %collective-permute-start.11 = (bf16[1024,256]{0,1:T(8,128)(2,1)S(1)}, bf16[1024,256]{0,1:T(8,128)(2,1)}, u32[]{:S(2)}, u32[]{:S(2)}) collective-permute-start(bf16[1024,256]{0,1:T(8,128)(2,1)S(1)} %collective-permute-done.8), channel_id=1, source_target_pairs={{0,15},{1,0},{2,1},{3,2},{4,3},{5,4},{6,5},{7,6},{8,7},{9,8},{10,9... | collective-permute-start | bytes 1572872 | tf_op jit(solution)/shard_map/ppermute | solution.py:49
  68.1 2.9 %collective-permute-start.12 = (f32[8,384]{1,0:T(8,128)S(1)}, f32[8,384]{1,0:T(8,128)S(1)}, u32[]{:S(2)}, u32[]{:S(2)}) collective-permute-start(f32[8,384]{1,0:T(8,128)S(1)} %add.50), channel_id=1, source_target_pairs={{0,128},{16,144},{32,160},{48,176},{64,192},{80,208},{96,224},{112... | collective-permute-start | bytes 36872 | tf_op jit(solution)/shard_map/ppermute | solution.py:51
  71.0 1.9 %collective-permute-done.12 = f32[8,384]{1,0:T(8,128)S(1)} collective-permute-done((f32[8,384]{1,0:T(8,128)S(1)}, f32[8,384]{1,0:T(8,128)S(1)}, u32[]{:S(2)}, u32[]{:S(2)}) %collective-permute-start.12) | collective-permute-done | bytes 12320 | tf_op jit(solution)/shard_map/ppermute | solution.py:51
  72.9 2.0 %collective-permute-done.10 = bf16[1024,256]{0,1:T(8,128)(2,1)} collective-permute-done((bf16[1024,256]{0,1:T(8,128)(2,1)}, bf16[1024,256]{0,1:T(8,128)(2,1)}, u32[]{:S(2)}, u32[]{:S(2)}) %collective-permute-start.10) | collective-permute-done | bytes 524320 | tf_op jit(solution)/shard_map/ppermute | solution.py:48
  82.0 2.0 %fusion.17 = f32[3,256,256]{2,1,0:T(8,128)S(1)} fusion(bf16[1,1024,256]{1,2,0:T(8,128)(2,1)} %bitcast.66, bf16[1,1024,256]{1,2,0:T(8,128)(2,1)} %bitcast.64, bf16[1,1024,256]{1,2,0:T(8,128)(2,1)S(1)} %bitcast.62, bf16[1024,256]{0,1:T(8,128)(2,1)} %collective-permute-done.10), kind=kOutput, calls=%fused_computation.24 | convolution fusion | flops 407371776 | bytes 2883584 | tf_op jit(solution)/shard_map/dot_general | solution.py:62
  83.9 2.3 %fusion.3 = f32[4,256,256]{2,1,0:T(8,128)S(1)} fusion(bf16[1,1024,256]{1,2,0:T(8,128)(2,1)} %bitcast.8, bf16[1,1024,256]{1,2,0:T(8,128)(2,1)} %bitcast.67, bf16[1,1024,256]{1,2,0:T(8,128)(2,1)} %bitcast.65, bf16[1,1024,256]{1,2,0:T(8,128)(2,1)S(1)} %bitcast.63, bf16[1024,256]{0,1:T(8,128)(2,1)} %collective-permute-done.10), kind=kOutput, calls=%fused_computation.10 | convolution fusion | flops 540016640 | bytes 3670016 | tf_op jit(solution)/shard_map/dot_general | solution.py:58
  87.4 3.7 %fusion.1 = f32[32,144,256]{2,1,0:T(8,128)S(1)} fusion(s32[]{:T(128)S(6)} %select_n.52, f32[32,128,256]{2,1,0:T(8,128)S(1)} %bitcast.60, f32[32,16,256]{2,1,0:T(8,128)} %pad.4), kind=kLoop, calls=%fused_computation.5 | loop fusion | flops 3538944 | bytes 9437188 | tf_op jit(solution)/shard_map/concatenate | solution.py:78
  91.1 2.1 %copy-done = f32[32,144,256]{2,1,0:T(8,128)} copy-done((f32[32,144,256]{2,1,0:T(8,128)}, f32[32,144,256]{2,1,0:T(8,128)S(1)}, u32[]{:S(2)}) %copy-start) | copy-done | bytes 4718616
  94.8 6.6 %collective-permute-start.13 = (f32[16,144,256]{2,1,0:T(8,128)}, f32[16,144,256]{2,1,0:T(8,128)S(1)}, u32[]{:S(2)}, u32[]{:S(2)}) collective-permute-start(f32[16,144,256]{2,1,0:T(8,128)} %dynamic-slice_bitcast_fusion), channel_id=1, source_target_pairs={{0,16},{16,0},{32,48},{48,32},{64,80},{80,64},{96,112},{112,96},{1... | collective-permute-start | bytes 7077896 | tf_op jit(solution)/shard_map/ppermute | solution.py:87
  101.4 4.3 %collective-permute-done.13 = f32[16,144,256]{2,1,0:T(8,128)S(1)} collective-permute-done((f32[16,144,256]{2,1,0:T(8,128)}, f32[16,144,256]{2,1,0:T(8,128)S(1)}, u32[]{:S(2)}, u32[]{:S(2)}) %collective-permute-start.13) | collective-permute-done | bytes 2359328 | tf_op jit(solution)/shard_map/ppermute | solution.py:87
  105.8 3.4 %bitcast_add_fusion = f32[16,144,256]{2,1,0:T(8,128)} fusion(f32[16,144,256]{2,1,0:T(8,128)S(1)} %collective-permute-done.13, f32[16,2,144,256]{3,2,1,0:T(8,128)} %bitcast.59, s32[]{:T(128)S(6)} %select_n.53), kind=kLoop, calls=%fused_computation.8 | loop fusion | flops 589824 | bytes 7077892 | tf_op jit(solution)/shard_map/add | solution.py:87
  109.2 7.4 %all-to-all-start = ((f32[32,72,256]{2,1,0:T(8,128)}), f32[32,72,256]{2,1,0:T(8,128)S(1)}, u32[]{:S(2)}, u32[]{:S(2)}) async-start(f32[32,72,256]{2,1,0:T(8,128)} %bitcast.19), calls=%async_computation | async-start | bytes 4718592 | tf_op jit(solution)/shard_map/all_to_all | solution.py:89
  116.6 30.8 %all-to-all-done = f32[32,72,256]{2,1,0:T(8,128)S(1)} async-done(((f32[32,72,256]{2,1,0:T(8,128)}), f32[32,72,256]{2,1,0:T(8,128)S(1)}, u32[]{:S(2)}, u32[]{:S(2)}) %all-to-all-start) | async-done | bytes 2359328 | tf_op jit(solution)/shard_map/all_to_all | solution.py:89
  147.6 2.3 %collective-permute-start.14 = (f32[72,256]{1,0:T(8,128)S(1)}, f32[72,256]{1,0:T(8,128)S(1)}, u32[]{:S(2)}, u32[]{:S(2)}) collective-permute-start(f32[72,256]{1,0:T(8,128)S(1)} %get-tuple-element.31), channel_id=1, source_target_pairs={{0,16},{16,0},{32,48},{48,32},{64,80},{80,64},{96,112},{112,96},{1... | collective-permute-start | bytes 221192 | tf_op jit(solution)/shard_map/ppermute | solution.py:93
  150.8 4.6 %collective-permute-start.15 = (f32[144,256]{1,0:T(8,128)S(1)}, f32[144,256]{1,0:T(8,128)S(1)}, u32[]{:S(2)}, u32[]{:S(2)}) collective-permute-start(f32[144,256]{1,0:T(8,128)S(1)} %maximum_select_fusion), channel_id=1, source_target_pairs={{5,40},{6,72},{7,104},{8,388},{9,389},{10,390},{11,391},{21,56},{2... | collective-permute-start | bytes 442376 | tf_op jit(solution)/shard_map/ppermute | solution.py:110
  156.1 16.0 %collective-permute-done.15 = f32[144,256]{1,0:T(8,128)S(1)} collective-permute-done((f32[144,256]{1,0:T(8,128)S(1)}, f32[144,256]{1,0:T(8,128)S(1)}, u32[]{:S(2)}, u32[]{:S(2)}) %collective-permute-start.15) | collective-permute-done | bytes 147488 | tf_op jit(solution)/shard_map/ppermute | solution.py:110
  (61 shorter events, 19.3 us)
Async XLA Ops:
  1.9 24.8 %collective-permute-start = (bf16[1024,256]{0,1:T(8,128)(2,1)S(1)}, bf16[1024,256]{0,1:T(8,128)(2,1)S(1)}, u32[]{:S(2)}, u32[]{:S(2)}) collective-permute-start(bf16[1024,256]{0,1:T(8,128)(2,1)S(1)} %copy.33), channel_id=1, source_target_pairs={{0,1},{1,2},{2,3},{3,4},{4,5},{5,6},{6,7},{7,8},{8,9},{9,10},{10,1... | collective-permute-start | bytes 1572872 | tf_op jit(solution)/shard_map/ppermute | solution.py:48
  5.4 21.3 %collective-permute-start.1 = (bf16[1024,256]{0,1:T(8,128)(2,1)S(1)}, bf16[1024,256]{0,1:T(8,128)(2,1)S(1)}, u32[]{:S(2)}, u32[]{:S(2)}) collective-permute-start(bf16[1024,256]{0,1:T(8,128)(2,1)S(1)} %copy.33), channel_id=1, source_target_pairs={{0,15},{1,0},{2,1},{3,2},{4,3},{5,4},{6,5},{7,6},{8,7},{9,8},{10,9... | collective-permute-start | bytes 1572872 | tf_op jit(solution)/shard_map/ppermute | solution.py:49
  17.1 3.7 %collective-permute-start.2 = (f32[8,384]{1,0:T(8,128)S(1)}, f32[8,384]{1,0:T(8,128)S(1)}, u32[]{:S(2)}, u32[]{:S(2)}) collective-permute-start(f32[8,384]{1,0:T(8,128)S(1)} %pad_maximum_fusion.2), channel_id=1, source_target_pairs={{0,16},{16,0},{32,48},{48,32},{64,80},{80,64},{96,112},{112,96},{1... | collective-permute-start | bytes 36872 | tf_op jit(solution)/shard_map/ppermute | solution.py:51
  20.8 5.9 %collective-permute-start.3 = (f32[8,384]{1,0:T(8,128)S(1)}, f32[8,384]{1,0:T(8,128)S(1)}, u32[]{:S(2)}, u32[]{:S(2)}) collective-permute-start(f32[8,384]{1,0:T(8,128)S(1)} %fusion.34), channel_id=1, source_target_pairs={{0,256},{16,272},{32,288},{48,304},{64,320},{80,336},{96,352},{112... | collective-permute-start | bytes 36872 | tf_op jit(solution)/shard_map/ppermute | solution.py:51
  26.7 52.4 %copy-start.2 = (bf16[1024,256]{0,1:T(8,128)(2,1)}, bf16[1024,256]{0,1:T(8,128)(2,1)S(1)}, u32[]{:S(2)}) copy-start(bf16[1024,256]{0,1:T(8,128)(2,1)S(1)} %collective-permute-done.1) | copy-start | bytes 1572868
  26.7 13.9 %collective-permute-start.5 = (bf16[1024,256]{0,1:T(8,128)(2,1)S(1)}, bf16[1024,256]{0,1:T(8,128)(2,1)S(1)}, u32[]{:S(2)}, u32[]{:S(2)}) collective-permute-start(bf16[1024,256]{0,1:T(8,128)(2,1)S(1)} %collective-permute-done.1), channel_id=1, source_target_pairs={{0,15},{1,0},{2,1},{3,2},{4,3},{5,4},{6,5},{7,6},{8,7},{9,8},{10,9... | collective-permute-start | bytes 1572872 | tf_op jit(solution)/shard_map/ppermute | solution.py:49
  30.8 14.8 %collective-permute-start.4 = (bf16[1024,256]{0,1:T(8,128)(2,1)S(1)}, bf16[1024,256]{0,1:T(8,128)(2,1)S(1)}, u32[]{:S(2)}, u32[]{:S(2)}) collective-permute-start(bf16[1024,256]{0,1:T(8,128)(2,1)S(1)} %collective-permute-done), channel_id=1, source_target_pairs={{0,1},{1,2},{2,3},{3,4},{4,5},{5,6},{6,7},{7,8},{8,9},{9,10},{10,1... | collective-permute-start | bytes 1572872 | tf_op jit(solution)/shard_map/ppermute | solution.py:48
  32.8 4.7 %collective-permute-start.6 = (f32[8,384]{1,0:T(8,128)S(1)}, f32[8,384]{1,0:T(8,128)S(1)}, u32[]{:S(2)}, u32[]{:S(2)}) collective-permute-start(f32[8,384]{1,0:T(8,128)S(1)} %add.48), channel_id=1, source_target_pairs={{0,32},{16,48},{32,0},{48,16},{64,96},{80,112},{96,64},{112,80},{1... | collective-permute-start | bytes 36872 | tf_op jit(solution)/shard_map/ppermute | solution.py:51
  40.6 39.8 %copy-start.4 = (bf16[1024,256]{0,1:T(8,128)(2,1)}, bf16[1024,256]{0,1:T(8,128)(2,1)S(1)}, u32[]{:S(2)}) copy-start(bf16[1024,256]{0,1:T(8,128)(2,1)S(1)} %collective-permute-done.5) | copy-start | bytes 1572868
  45.6 12.8 %collective-permute-start.8 = (bf16[1024,256]{0,1:T(8,128)(2,1)S(1)}, bf16[1024,256]{0,1:T(8,128)(2,1)S(1)}, u32[]{:S(2)}, u32[]{:S(2)}) collective-permute-start(bf16[1024,256]{0,1:T(8,128)(2,1)S(1)} %collective-permute-done.5), channel_id=1, source_target_pairs={{0,15},{1,0},{2,1},{3,2},{4,3},{5,4},{6,5},{7,6},{8,7},{9,8},{10,9... | collective-permute-start | bytes 1572872 | tf_op jit(solution)/shard_map/ppermute | solution.py:49
  47.5 14.0 %collective-permute-start.7 = (bf16[1024,256]{0,1:T(8,128)(2,1)S(1)}, bf16[1024,256]{0,1:T(8,128)(2,1)}, u32[]{:S(2)}, u32[]{:S(2)}) collective-permute-start(bf16[1024,256]{0,1:T(8,128)(2,1)S(1)} %collective-permute-done.4), channel_id=1, source_target_pairs={{0,1},{1,2},{2,3},{3,4},{4,5},{5,6},{6,7},{7,8},{8,9},{9,10},{10,1... | collective-permute-start | bytes 1572872 | tf_op jit(solution)/shard_map/ppermute | solution.py:48
  50.9 5.9 %collective-permute-start.9 = (f32[8,384]{1,0:T(8,128)S(1)}, f32[8,384]{1,0:T(8,128)S(1)}, u32[]{:S(2)}, u32[]{:S(2)}) collective-permute-start(f32[8,384]{1,0:T(8,128)S(1)} %add.49), channel_id=1, source_target_pairs={{0,64},{16,80},{32,96},{48,112},{64,0},{80,16},{96,32},{112,48},{1... | collective-permute-start | bytes 36872 | tf_op jit(solution)/shard_map/ppermute | solution.py:51
  58.4 22.0 %copy-start.5 = (bf16[1024,256]{0,1:T(8,128)(2,1)}, bf16[1024,256]{0,1:T(8,128)(2,1)S(1)}, u32[]{:S(2)}) copy-start(bf16[1024,256]{0,1:T(8,128)(2,1)S(1)} %collective-permute-done.8) | copy-start | bytes 1572868
  61.6 13.4 %collective-permute-start.10 = (bf16[1024,256]{0,1:T(8,128)(2,1)}, bf16[1024,256]{0,1:T(8,128)(2,1)}, u32[]{:S(2)}, u32[]{:S(2)}) collective-permute-start(bf16[1024,256]{0,1:T(8,128)(2,1)} %collective-permute-done.7), channel_id=1, source_target_pairs={{0,1},{1,2},{2,3},{3,4},{4,5},{5,6},{6,7},{7,8},{8,9},{9,10},{10,1... | collective-permute-start | bytes 1572872 | tf_op jit(solution)/shard_map/ppermute | solution.py:48
  63.5 12.0 %collective-permute-start.11 = (bf16[1024,256]{0,1:T(8,128)(2,1)S(1)}, bf16[1024,256]{0,1:T(8,128)(2,1)}, u32[]{:S(2)}, u32[]{:S(2)}) collective-permute-start(bf16[1024,256]{0,1:T(8,128)(2,1)S(1)} %collective-permute-done.8), channel_id=1, source_target_pairs={{0,15},{1,0},{2,1},{3,2},{4,3},{5,4},{6,5},{7,6},{8,7},{9,8},{10,9... | collective-permute-start | bytes 1572872 | tf_op jit(solution)/shard_map/ppermute | solution.py:49
  68.1 4.8 %collective-permute-start.12 = (f32[8,384]{1,0:T(8,128)S(1)}, f32[8,384]{1,0:T(8,128)S(1)}, u32[]{:S(2)}, u32[]{:S(2)}) collective-permute-start(f32[8,384]{1,0:T(8,128)S(1)} %add.50), channel_id=1, source_target_pairs={{0,128},{16,144},{32,160},{48,176},{64,192},{80,208},{96,224},{112... | collective-permute-start | bytes 36872 | tf_op jit(solution)/shard_map/ppermute | solution.py:51
  77.8 2.6 %copy-start.1 = (bf16[1024,256]{1,0:T(8,128)(2,1)S(1)}, bf16[1024,256]{1,0:T(8,128)(2,1)}, u32[]{:S(2)}) copy-start(bf16[1024,256]{1,0:T(8,128)(2,1)} %param.2) | copy-start | bytes 1572868
  80.5 1.5 copy-start.3
  91.1 2.1 %copy-start = (f32[32,144,256]{2,1,0:T(8,128)}, f32[32,144,256]{2,1,0:T(8,128)S(1)}, u32[]{:S(2)}) copy-start(f32[32,144,256]{2,1,0:T(8,128)S(1)} %fusion.1) | copy-start | bytes 14155780
  94.8 10.9 %collective-permute-start.13 = (f32[16,144,256]{2,1,0:T(8,128)}, f32[16,144,256]{2,1,0:T(8,128)S(1)}, u32[]{:S(2)}, u32[]{:S(2)}) collective-permute-start(f32[16,144,256]{2,1,0:T(8,128)} %dynamic-slice_bitcast_fusion), channel_id=1, source_target_pairs={{0,16},{16,0},{32,48},{48,32},{64,80},{80,64},{96,112},{112,96},{1... | collective-permute-start | bytes 7077896 | tf_op jit(solution)/shard_map/ppermute | solution.py:87
  109.2 38.3 %all-to-all-start = ((f32[32,72,256]{2,1,0:T(8,128)}), f32[32,72,256]{2,1,0:T(8,128)S(1)}, u32[]{:S(2)}, u32[]{:S(2)}) async-start(f32[32,72,256]{2,1,0:T(8,128)} %bitcast.19), calls=%async_computation | async-start | bytes 4718592 | tf_op jit(solution)/shard_map/all_to_all | solution.py:89
  147.6 3.2 %collective-permute-start.14 = (f32[72,256]{1,0:T(8,128)S(1)}, f32[72,256]{1,0:T(8,128)S(1)}, u32[]{:S(2)}, u32[]{:S(2)}) collective-permute-start(f32[72,256]{1,0:T(8,128)S(1)} %get-tuple-element.31), channel_id=1, source_target_pairs={{0,16},{16,0},{32,48},{48,32},{64,80},{80,64},{96,112},{112,96},{1... | collective-permute-start | bytes 221192 | tf_op jit(solution)/shard_map/ppermute | solution.py:93
  150.8 21.3 %collective-permute-start.15 = (f32[144,256]{1,0:T(8,128)S(1)}, f32[144,256]{1,0:T(8,128)S(1)}, u32[]{:S(2)}, u32[]{:S(2)}) collective-permute-start(f32[144,256]{1,0:T(8,128)S(1)} %maximum_select_fusion), channel_id=1, source_target_pairs={{5,40},{6,72},{7,104},{8,388},{9,389},{10,390},{11,391},{21,56},{2... | collective-permute-start | bytes 442376 | tf_op jit(solution)/shard_map/ppermute | solution.py:110

commit v11 on v10

--- a/solution.py
+++ b/solution.py
@@ -44,29 +44,46 @@
     down = [(i, (i - 1) % n_t) for i in range(n_t)]
     bfly = [1 << b for b in range(n_dp.bit_length() - 1)]
     per_step = [bfly[i::win] for i in range(win)]
+    contract = (((0,), (0,)), ((), ()))
+    ones = jnp.ones((tok_rows, 8), jnp.bfloat16)
+
+    def near_of(b):
+        pr = lax.dot_general(b, activations, contract, preferred_element_type=jnp.float32)
+        cs = lax.dot_general(b, ones, contract, preferred_element_type=jnp.float32)[:, 0]
+        return pr, cs
+
+    near = [None] * (2 * win + 1)
+    colsums = [None] * (2 * win + 1)
+    near[win], colsums[win] = near_of(activations)
     for step in range(1, win + 1):
         fwd = lax.ppermute(fwd, "tensor", up)
         bwd = lax.ppermute(bwd, "tensor", down)
         for k in per_step[step - 1]:
             stats = stats + lax.ppermute(stats, "dp", [(i, i ^ k) for i in range(n_dp)])
-        fwd, bwd, stats = lax.optimization_barrier((fwd, bwd, stats))
+        ready = []
+        if step > 1:
+            for idx in (win - step + 1, win + step - 1):
+                near[idx], colsums[idx] = near_of(blocks[idx])
+                ready += [near[idx], colsums[idx]]
+        fwd, bwd, stats, ready = lax.optimization_barrier((fwd, bwd, stats, ready))
+        if step > 1:
+            near[win - step + 1], colsums[win - step + 1] = ready[0], ready[1]
+            near[win + step - 1], colsums[win + step - 1] = ready[2], ready[3]
         blocks[win - step] = fwd
         blocks[win + step] = bwd
-    wst = jnp.stack(blocks)
-    contract = (((1,), (0,)), ((), ()))
-    near = lax.dot_general(wst, activations, contract, preferred_element_type=jnp.float32)
-    far_a = lax.dot_general(
-        wst[win + 1:], wst[0], contract, preferred_element_type=jnp.float32
-    )
+    for idx in (0, 2 * win):
+        near[idx], colsums[idx] = near_of(blocks[idx])
     n_b = n_t - 3 * win - 1
-    far_b = lax.dot_general(
-        wst[0], wst[win + 1:win + 1 + n_b], (((0,), (1,)), ((), ())),
-        preferred_element_type=jnp.float32,
-    ).transpose(1, 0, 2)
-    prod = jnp.concatenate([near, far_a, far_b], axis=0).reshape(n_dp, col_width, slice_width)
-    ones = jnp.ones((8, tok_rows), jnp.bfloat16)
-    cs = lax.dot_general(wst, ones, (((1,), (1,)), ((), ())), preferred_element_type=jnp.float32)[..., 0]
-    cs_off = jnp.concatenate([cs, cs[win + 1:], jnp.broadcast_to(cs[0], (n_b, slice_width))], axis=0)
+    far_a = [
+        lax.dot_general(blocks[k], blocks[0], contract, preferred_element_type=jnp.float32)
+        for k in range(win + 1, 2 * win + 1)
+    ]
+    far_b = [
+        lax.dot_general(blocks[0], blocks[k], contract, preferred_element_type=jnp.float32)
+        for k in range(win + 1, win + 1 + n_b)
+    ]
+    prod = jnp.stack(near + far_a + far_b).reshape(n_dp, col_width, slice_width)
+    cs_off = jnp.stack(colsums + colsums[win + 1:] + [colsums[0]] * n_b)
     extra = jnp.pad(
         cs_off.reshape(n_dp, 1, col_width),
         ((0, 0), (0, EXTRA_ROWS - 1), (0, slice_width - col_width)),

time: 174 us -> 180 us (1.034)
  matrix products: 8.17 us -> 18.6 us
  waiting for transfers between devices: 76.9 us -> 73.2 us
    dot_general x4 -> x25, matrix products: 6.94 us -> 17.4 us  [the longest x9 7.22 us: near_of(): lax.dot_general(b, activations, contract, preferred_element_type=jnp.floa...]
    ppermute x5, waiting for transfers between devices: 9.55 us -> 6.16 us  [body(): stats = stats + lax.ppermute(stats, 'dp', [(i, i ^ k) for i in range(n_dp)])]
    unnamed x24 -> x11, local copies, waits for them, and re-layouts: 6.52 us -> 7.21 us
  transfers between devices with their start and end apart: 17 -> 17, of which waited for: 15 -> 13; matrix products, arithmetic and copies ran while one was open for 2% -> 5% of each run, Pallas kernels for 0% -> 0%
where the time goes in v11:
time: 180 us; the launch traced here: 179 us
  waiting for transfers between devices  73.2 us (41%)
  starting transfers between devices  66.7 us (37%)
  matrix products  18.6 us (10%)
  other arithmetic  10.3 us (6%)
  local copies, waits for them, and re-layouts  9.14 us (5%)
    all_to_all x1, waiting for transfers between devices, body(): recv = lax.all_to_all(halves, 'dp', 0, 0, tiled=True)  30.8 us
    ppermute x4, starting transfers between devices, body(): bwd = lax.ppermute(bwd, 'tensor', down)  19.9 us
    ppermute x1, waiting for transfers between devices, body(): moved = lax.ppermute(total, ('dp', 'tensor'), perm)  16.1 us
    ppermute x5, starting transfers between devices, body(): stats = stats + lax.ppermute(stats, 'dp', [(i, i ^ k) for i in range(n_dp)])  15.3 us
    ppermute x4, starting transfers between devices, body(): fwd = lax.ppermute(fwd, 'tensor', up)  10.9 us
    ppermute x4, waiting for transfers between devices, body(): fwd = lax.ppermute(fwd, 'tensor', up)  10.8 us
    all_to_all x1, starting transfers between devices, body(): recv = lax.all_to_all(halves, 'dp', 0, 0, tiled=True)  7.41 us
    dot_general x9, matrix products, near_of(): lax.dot_general(b, activations, contract, preferred_element_type=jnp.floa...  7.22 us
  transfers between devices with their start and end apart: 17, of which 13 were waited for; matrix products, arithmetic and copies ran while one was open for 5% of the time, Pallas kernels for 0%

profile of v11, /device:TPU:17, one launch (start us, length us, event | category | flops | bytes accessed | tf_op | source)
XLA Modules:
  0.0 179.0 jit_solution(17598497709280430783)
XLA Ops:
  0.6 3.7 %collective-permute-start = (bf16[1024,256]{1,0:T(8,128)(2,1)}, bf16[1024,256]{1,0:T(8,128)(2,1)S(1)}, u32[]{:S(2)}, u32[]{:S(2)}) collective-permute-start(bf16[1024,256]{1,0:T(8,128)(2,1)} %param.2), channel_id=1, source_target_pairs={{0,1},{1,2},{2,3},{3,4},{4,5},{5,6},{6,7},{7,8},{8,9},{9,10},{10,1... | collective-permute-start | bytes 1572872 | tf_op jit(solution)/shard_map/ppermute | solution.py:59
  4.3 9.5 %collective-permute-start.1 = (bf16[1024,256]{1,0:T(8,128)(2,1)}, bf16[1024,256]{1,0:T(8,128)(2,1)S(1)}, u32[]{:S(2)}, u32[]{:S(2)}) collective-permute-start(bf16[1024,256]{1,0:T(8,128)(2,1)} %param.2), channel_id=1, source_target_pairs={{0,15},{1,0},{2,1},{3,2},{4,3},{5,4},{6,5},{7,6},{8,7},{9,8},{10,9... | collective-permute-start | bytes 1572872 | tf_op jit(solution)/shard_map/ppermute | solution.py:60
  16.0 2.9 %collective-permute-start.2 = (f32[8,384]{1,0:T(8,128)S(1)}, f32[8,384]{1,0:T(8,128)S(1)}, u32[]{:S(2)}, u32[]{:S(2)}) collective-permute-start(f32[8,384]{1,0:T(8,128)S(1)} %pad_maximum_fusion), channel_id=1, source_target_pairs={{0,16},{16,0},{32,48},{48,32},{64,80},{80,64},{96,112},{112,96},{1... | collective-permute-start | bytes 36872 | tf_op jit(solution)/shard_map/ppermute | solution.py:62
  20.1 2.0 %collective-permute-start.3 = (f32[8,384]{1,0:T(8,128)S(1)}, f32[8,384]{1,0:T(8,128)S(1)}, u32[]{:S(2)}, u32[]{:S(2)}) collective-permute-start(f32[8,384]{1,0:T(8,128)S(1)} %fusion.42), channel_id=1, source_target_pairs={{0,256},{16,272},{32,288},{48,304},{64,320},{80,336},{96,352},{112... | collective-permute-start | bytes 36872 | tf_op jit(solution)/shard_map/ppermute | solution.py:62
  22.2 3.9 %collective-permute-done.3 = f32[8,384]{1,0:T(8,128)S(1)} collective-permute-done((f32[8,384]{1,0:T(8,128)S(1)}, f32[8,384]{1,0:T(8,128)S(1)}, u32[]{:S(2)}, u32[]{:S(2)}) %collective-permute-start.3) | collective-permute-done | bytes 12320 | tf_op jit(solution)/shard_map/ppermute | solution.py:62
  26.1 3.9 %collective-permute-start.5 = (bf16[1024,256]{1,0:T(8,128)(2,1)S(1)}, bf16[1024,256]{1,0:T(8,128)(2,1)S(1)}, u32[]{:S(2)}, u32[]{:S(2)}) collective-permute-start(bf16[1024,256]{1,0:T(8,128)(2,1)S(1)} %collective-permute-done.1), channel_id=1, source_target_pairs={{0,15},{1,0},{2,1},{3,2},{4,3},{5,4},{6,5},{7,6},{8,7},{9,8},{10,9... | collective-permute-start | bytes 1572872 | tf_op jit(solution)/shard_map/ppermute | solution.py:60
  30.0 1.4 fusion.44
  31.4 1.9 %collective-permute-start.4 = (bf16[1024,256]{1,0:T(8,128)(2,1)S(1)}, bf16[1024,256]{1,0:T(8,128)(2,1)S(1)}, u32[]{:S(2)}, u32[]{:S(2)}) collective-permute-start(bf16[1024,256]{1,0:T(8,128)(2,1)S(1)} %collective-permute-done), channel_id=1, source_target_pairs={{0,1},{1,2},{2,3},{3,4},{4,5},{5,6},{6,7},{7,8},{8,9},{9,10},{10,1... | collective-permute-start | bytes 1572872 | tf_op jit(solution)/shard_map/ppermute | solution.py:59
  33.6 3.1 %collective-permute-start.6 = (f32[8,384]{1,0:T(8,128)S(1)}, f32[8,384]{1,0:T(8,128)S(1)}, u32[]{:S(2)}, u32[]{:S(2)}) collective-permute-start(f32[8,384]{1,0:T(8,128)S(1)} %add.48), channel_id=1, source_target_pairs={{0,32},{16,48},{32,0},{48,16},{64,96},{80,112},{96,64},{112,80},{1... | collective-permute-start | bytes 36872 | tf_op jit(solution)/shard_map/ppermute | solution.py:62
  36.7 1.4 fusion.43
  38.3 2.0 %collective-permute-done.5 = bf16[1024,256]{1,0:T(8,128)(2,1)S(1)} collective-permute-done((bf16[1024,256]{1,0:T(8,128)(2,1)S(1)}, bf16[1024,256]{1,0:T(8,128)(2,1)S(1)}, u32[]{:S(2)}, u32[]{:S(2)}) %collective-permute-start.5) | collective-permute-done | bytes 524320 | tf_op jit(solution)/shard_map/ppermute | solution.py:60
  40.3 6.0 %collective-permute-done.4 = bf16[1024,256]{1,0:T(8,128)(2,1)S(1)} collective-permute-done((bf16[1024,256]{1,0:T(8,128)(2,1)S(1)}, bf16[1024,256]{1,0:T(8,128)(2,1)S(1)}, u32[]{:S(2)}, u32[]{:S(2)}) %collective-permute-start.4) | collective-permute-done | bytes 524320 | tf_op jit(solution)/shard_map/ppermute | solution.py:59
  46.3 1.9 %collective-permute-start.8 = (bf16[1024,256]{1,0:T(8,128)(2,1)S(1)}, bf16[1024,256]{1,0:T(8,128)(2,1)S(1)}, u32[]{:S(2)}, u32[]{:S(2)}) collective-permute-start(bf16[1024,256]{1,0:T(8,128)(2,1)S(1)} %collective-permute-done.5), channel_id=1, source_target_pairs={{0,15},{1,0},{2,1},{3,2},{4,3},{5,4},{6,5},{7,6},{8,7},{9,8},{10,9... | collective-permute-start | bytes 1572872 | tf_op jit(solution)/shard_map/ppermute | solution.py:60
  48.5 3.4 %collective-permute-start.7 = (bf16[1024,256]{1,0:T(8,128)(2,1)S(1)}, bf16[1024,256]{1,0:T(8,128)(2,1)S(1)}, u32[]{:S(2)}, u32[]{:S(2)}) collective-permute-start(bf16[1024,256]{1,0:T(8,128)(2,1)S(1)} %collective-permute-done.4), channel_id=1, source_target_pairs={{0,1},{1,2},{2,3},{3,4},{4,5},{5,6},{6,7},{7,8},{8,9},{9,10},{10,1... | collective-permute-start | bytes 1572872 | tf_op jit(solution)/shard_map/ppermute | solution.py:59
  52.1 4.7 %collective-permute-start.9 = (f32[8,384]{1,0:T(8,128)S(1)}, f32[8,384]{1,0:T(8,128)S(1)}, u32[]{:S(2)}, u32[]{:S(2)}) collective-permute-start(f32[8,384]{1,0:T(8,128)S(1)} %add.49), channel_id=1, source_target_pairs={{0,64},{16,80},{32,96},{48,112},{64,0},{80,16},{96,32},{112,48},{1... | collective-permute-start | bytes 36872 | tf_op jit(solution)/shard_map/ppermute | solution.py:62
  59.0 3.5 %collective-permute-done.7 = bf16[1024,256]{1,0:T(8,128)(2,1)S(1)} collective-permute-done((bf16[1024,256]{1,0:T(8,128)(2,1)S(1)}, bf16[1024,256]{1,0:T(8,128)(2,1)S(1)}, u32[]{:S(2)}, u32[]{:S(2)}) %collective-permute-start.7) | collective-permute-done | bytes 524320 | tf_op jit(solution)/shard_map/ppermute | solution.py:59
  62.5 1.9 %collective-permute-start.10 = (bf16[1024,256]{1,0:T(8,128)(2,1)S(1)}, bf16[1024,256]{1,0:T(8,128)(2,1)S(1)}, u32[]{:S(2)}, u32[]{:S(2)}) collective-permute-start(bf16[1024,256]{1,0:T(8,128)(2,1)S(1)} %collective-permute-done.7), channel_id=1, source_target_pairs={{0,1},{1,2},{2,3},{3,4},{4,5},{5,6},{6,7},{7,8},{8,9},{9,10},{10,1... | collective-permute-start | bytes 1572872 | tf_op jit(solution)/shard_map/ppermute | solution.py:59
  64.8 4.6 %collective-permute-start.11 = (bf16[1024,256]{1,0:T(8,128)(2,1)S(1)}, bf16[1024,256]{1,0:T(8,128)(2,1)S(1)}, u32[]{:S(2)}, u32[]{:S(2)}) collective-permute-start(bf16[1024,256]{1,0:T(8,128)(2,1)S(1)} %collective-permute-done.8), channel_id=1, source_target_pairs={{0,15},{1,0},{2,1},{3,2},{4,3},{5,4},{6,5},{7,6},{8,7},{9,8},{10,9... | collective-permute-start | bytes 1572872 | tf_op jit(solution)/shard_map/ppermute | solution.py:60
  69.6 2.7 %collective-permute-start.12 = (f32[8,384]{1,0:T(8,128)S(1)}, f32[8,384]{1,0:T(8,128)S(1)}, u32[]{:S(2)}, u32[]{:S(2)}) collective-permute-start(f32[8,384]{1,0:T(8,128)S(1)} %add.50), channel_id=1, source_target_pairs={{0,128},{16,144},{32,160},{48,176},{64,192},{80,208},{96,224},{112... | collective-permute-start | bytes 36872 | tf_op jit(solution)/shard_map/ppermute | solution.py:62
  72.8 1.5 collective-permute-done.12
  74.3 1.3 collective-permute-done.10
  92.2 5.1 %fusion.1 = f32[32,144,256]{2,1,0:T(8,128)S(1)} fusion(s32[]{:T(128)S(6)} %select_n.52, f32[32,128,256]{2,1,0:T(8,128)} %bitcast.22, f32[32,16,256]{2,1,0:T(8,128)S(1)} %pad.4), kind=kLoop, calls=%fused_computation.5 | loop fusion | flops 3538944 | bytes 9437188 | tf_op jit(solution)/shard_map/concatenate | solution.py:95
  97.3 2.1 %copy-done.1 = f32[32,144,256]{2,1,0:T(8,128)} copy-done((f32[32,144,256]{2,1,0:T(8,128)}, f32[32,144,256]{2,1,0:T(8,128)S(1)}, u32[]{:S(2)}) %copy-start.1) | copy-done | bytes 4718616
  99.4 1.6 dynamic-slice_bitcast_fusion
  101.0 6.5 %collective-permute-start.13 = (f32[16,144,256]{2,1,0:T(8,128)}, f32[16,144,256]{2,1,0:T(8,128)S(1)}, u32[]{:S(2)}, u32[]{:S(2)}) collective-permute-start(f32[16,144,256]{2,1,0:T(8,128)} %dynamic-slice_bitcast_fusion), channel_id=1, source_target_pairs={{0,16},{16,0},{32,48},{48,32},{64,80},{80,64},{96,112},{112,96},{1... | collective-permute-start | bytes 7077896 | tf_op jit(solution)/shard_map/ppermute | solution.py:104
  107.5 4.3 %collective-permute-done.13 = f32[16,144,256]{2,1,0:T(8,128)S(1)} collective-permute-done((f32[16,144,256]{2,1,0:T(8,128)}, f32[16,144,256]{2,1,0:T(8,128)S(1)}, u32[]{:S(2)}, u32[]{:S(2)}) %collective-permute-start.13) | collective-permute-done | bytes 2359328 | tf_op jit(solution)/shard_map/ppermute | solution.py:104
  111.8 3.4 %bitcast_add_fusion = f32[16,144,256]{2,1,0:T(8,128)} fusion(f32[16,144,256]{2,1,0:T(8,128)S(1)} %collective-permute-done.13, f32[16,2,144,256]{3,2,1,0:T(8,128)} %bitcast.133, s32[]{:T(128)S(6)} %select_n.53), kind=kLoop, calls=%fused_computation.7 | loop fusion | flops 589824 | bytes 7077892 | tf_op jit(solution)/shard_map/add | solution.py:104
  115.2 7.4 %all-to-all-start = ((f32[32,72,256]{2,1,0:T(8,128)}), f32[32,72,256]{2,1,0:T(8,128)S(1)}, u32[]{:S(2)}, u32[]{:S(2)}) async-start(f32[32,72,256]{2,1,0:T(8,128)} %bitcast.36), calls=%async_computation | async-start | bytes 4718592 | tf_op jit(solution)/shard_map/all_to_all | solution.py:106
  122.7 30.8 %all-to-all-done = f32[32,72,256]{2,1,0:T(8,128)S(1)} async-done(((f32[32,72,256]{2,1,0:T(8,128)}), f32[32,72,256]{2,1,0:T(8,128)S(1)}, u32[]{:S(2)}, u32[]{:S(2)}) %all-to-all-start) | async-done | bytes 2359328 | tf_op jit(solution)/shard_map/all_to_all | solution.py:106
  153.7 2.3 %collective-permute-start.14 = (f32[72,256]{1,0:T(8,128)S(1)}, f32[72,256]{1,0:T(8,128)S(1)}, u32[]{:S(2)}, u32[]{:S(2)}) collective-permute-start(f32[72,256]{1,0:T(8,128)S(1)} %get-tuple-element.55), channel_id=1, source_target_pairs={{0,16},{16,0},{32,48},{48,32},{64,80},{80,64},{96,112},{112,96},{1... | collective-permute-start | bytes 221192 | tf_op jit(solution)/shard_map/ppermute | solution.py:110
  156.9 4.4 %collective-permute-start.15 = (f32[144,256]{1,0:T(8,128)S(1)}, f32[144,256]{1,0:T(8,128)S(1)}, u32[]{:S(2)}, u32[]{:S(2)}) collective-permute-start(f32[144,256]{1,0:T(8,128)S(1)} %maximum_select_fusion), channel_id=1, source_target_pairs={{5,40},{6,72},{7,104},{8,388},{9,389},{10,390},{11,391},{21,56},{2... | collective-permute-start | bytes 442376 | tf_op jit(solution)/shard_map/ppermute | solution.py:127
  162.0 16.1 %collective-permute-done.15 = f32[144,256]{1,0:T(8,128)S(1)} collective-permute-done((f32[144,256]{1,0:T(8,128)S(1)}, f32[144,256]{1,0:T(8,128)S(1)}, u32[]{:S(2)}, u32[]{:S(2)}) %collective-permute-start.15) | collective-permute-done | bytes 147488 | tf_op jit(solution)/shard_map/ppermute | solution.py:127
  (64 shorter events, 26.9 us)
Async XLA Ops:
  0.6 47.6 %copy-start = (bf16[1024,256]{1,0:T(8,128)(2,1)S(1)}, bf16[1024,256]{1,0:T(8,128)(2,1)}, u32[]{:S(2)}) copy-start(bf16[1024,256]{1,0:T(8,128)(2,1)} %param.2) | copy-start | bytes 1572868
  0.6 25.4 %collective-permute-start = (bf16[1024,256]{1,0:T(8,128)(2,1)}, bf16[1024,256]{1,0:T(8,128)(2,1)S(1)}, u32[]{:S(2)}, u32[]{:S(2)}) collective-permute-start(bf16[1024,256]{1,0:T(8,128)(2,1)} %param.2), channel_id=1, source_target_pairs={{0,1},{1,2},{2,3},{3,4},{4,5},{5,6},{6,7},{7,8},{8,9},{9,10},{10,1... | collective-permute-start | bytes 1572872 | tf_op jit(solution)/shard_map/ppermute | solution.py:59
  4.3 21.8 %collective-permute-start.1 = (bf16[1024,256]{1,0:T(8,128)(2,1)}, bf16[1024,256]{1,0:T(8,128)(2,1)S(1)}, u32[]{:S(2)}, u32[]{:S(2)}) collective-permute-start(bf16[1024,256]{1,0:T(8,128)(2,1)} %param.2), channel_id=1, source_target_pairs={{0,15},{1,0},{2,1},{3,2},{4,3},{5,4},{6,5},{7,6},{8,7},{9,8},{10,9... | collective-permute-start | bytes 1572872 | tf_op jit(solution)/shard_map/ppermute | solution.py:60
  16.0 4.1 %collective-permute-start.2 = (f32[8,384]{1,0:T(8,128)S(1)}, f32[8,384]{1,0:T(8,128)S(1)}, u32[]{:S(2)}, u32[]{:S(2)}) collective-permute-start(f32[8,384]{1,0:T(8,128)S(1)} %pad_maximum_fusion), channel_id=1, source_target_pairs={{0,16},{16,0},{32,48},{48,32},{64,80},{80,64},{96,112},{112,96},{1... | collective-permute-start | bytes 36872 | tf_op jit(solution)/shard_map/ppermute | solution.py:62
  20.1 5.9 %collective-permute-start.3 = (f32[8,384]{1,0:T(8,128)S(1)}, f32[8,384]{1,0:T(8,128)S(1)}, u32[]{:S(2)}, u32[]{:S(2)}) collective-permute-start(f32[8,384]{1,0:T(8,128)S(1)} %fusion.42), channel_id=1, source_target_pairs={{0,256},{16,272},{32,288},{48,304},{64,320},{80,336},{96,352},{112... | collective-permute-start | bytes 36872 | tf_op jit(solution)/shard_map/ppermute | solution.py:62
  26.1 14.2 %collective-permute-start.5 = (bf16[1024,256]{1,0:T(8,128)(2,1)S(1)}, bf16[1024,256]{1,0:T(8,128)(2,1)S(1)}, u32[]{:S(2)}, u32[]{:S(2)}) collective-permute-start(bf16[1024,256]{1,0:T(8,128)(2,1)S(1)} %collective-permute-done.1), channel_id=1, source_target_pairs={{0,15},{1,0},{2,1},{3,2},{4,3},{5,4},{6,5},{7,6},{8,7},{9,8},{10,9... | collective-permute-start | bytes 1572872 | tf_op jit(solution)/shard_map/ppermute | solution.py:60
  31.4 14.9 %collective-permute-start.4 = (bf16[1024,256]{1,0:T(8,128)(2,1)S(1)}, bf16[1024,256]{1,0:T(8,128)(2,1)S(1)}, u32[]{:S(2)}, u32[]{:S(2)}) collective-permute-start(bf16[1024,256]{1,0:T(8,128)(2,1)S(1)} %collective-permute-done), channel_id=1, source_target_pairs={{0,1},{1,2},{2,3},{3,4},{4,5},{5,6},{6,7},{7,8},{8,9},{9,10},{10,1... | collective-permute-start | bytes 1572872 | tf_op jit(solution)/shard_map/ppermute | solution.py:59
  33.6 4.7 %collective-permute-start.6 = (f32[8,384]{1,0:T(8,128)S(1)}, f32[8,384]{1,0:T(8,128)S(1)}, u32[]{:S(2)}, u32[]{:S(2)}) collective-permute-start(f32[8,384]{1,0:T(8,128)S(1)} %add.48), channel_id=1, source_target_pairs={{0,32},{16,48},{32,0},{48,16},{64,96},{80,112},{96,64},{112,80},{1... | collective-permute-start | bytes 36872 | tf_op jit(solution)/shard_map/ppermute | solution.py:62
  46.3 12.8 %collective-permute-start.8 = (bf16[1024,256]{1,0:T(8,128)(2,1)S(1)}, bf16[1024,256]{1,0:T(8,128)(2,1)S(1)}, u32[]{:S(2)}, u32[]{:S(2)}) collective-permute-start(bf16[1024,256]{1,0:T(8,128)(2,1)S(1)} %collective-permute-done.5), channel_id=1, source_target_pairs={{0,15},{1,0},{2,1},{3,2},{4,3},{5,4},{6,5},{7,6},{8,7},{9,8},{10,9... | collective-permute-start | bytes 1572872 | tf_op jit(solution)/shard_map/ppermute | solution.py:60
  48.5 14.0 %collective-permute-start.7 = (bf16[1024,256]{1,0:T(8,128)(2,1)S(1)}, bf16[1024,256]{1,0:T(8,128)(2,1)S(1)}, u32[]{:S(2)}, u32[]{:S(2)}) collective-permute-start(bf16[1024,256]{1,0:T(8,128)(2,1)S(1)} %collective-permute-done.4), channel_id=1, source_target_pairs={{0,1},{1,2},{2,3},{3,4},{4,5},{5,6},{6,7},{7,8},{8,9},{9,10},{10,1... | collective-permute-start | bytes 1572872 | tf_op jit(solution)/shard_map/ppermute | solution.py:59
  52.1 5.9 %collective-permute-start.9 = (f32[8,384]{1,0:T(8,128)S(1)}, f32[8,384]{1,0:T(8,128)S(1)}, u32[]{:S(2)}, u32[]{:S(2)}) collective-permute-start(f32[8,384]{1,0:T(8,128)S(1)} %add.49), channel_id=1, source_target_pairs={{0,64},{16,80},{32,96},{48,112},{64,0},{80,16},{96,32},{112,48},{1... | collective-permute-start | bytes 36872 | tf_op jit(solution)/shard_map/ppermute | solution.py:62
  62.5 13.1 %collective-permute-start.10 = (bf16[1024,256]{1,0:T(8,128)(2,1)S(1)}, bf16[1024,256]{1,0:T(8,128)(2,1)S(1)}, u32[]{:S(2)}, u32[]{:S(2)}) collective-permute-start(bf16[1024,256]{1,0:T(8,128)(2,1)S(1)} %collective-permute-done.7), channel_id=1, source_target_pairs={{0,1},{1,2},{2,3},{3,4},{4,5},{5,6},{6,7},{7,8},{8,9},{9,10},{10,1... | collective-permute-start | bytes 1572872 | tf_op jit(solution)/shard_map/ppermute | solution.py:59
  64.8 12.1 %collective-permute-start.11 = (bf16[1024,256]{1,0:T(8,128)(2,1)S(1)}, bf16[1024,256]{1,0:T(8,128)(2,1)S(1)}, u32[]{:S(2)}, u32[]{:S(2)}) collective-permute-start(bf16[1024,256]{1,0:T(8,128)(2,1)S(1)} %collective-permute-done.8), channel_id=1, source_target_pairs={{0,15},{1,0},{2,1},{3,2},{4,3},{5,4},{6,5},{7,6},{8,7},{9,8},{10,9... | collective-permute-start | bytes 1572872 | tf_op jit(solution)/shard_map/ppermute | solution.py:60
  69.6 4.7 %collective-permute-start.12 = (f32[8,384]{1,0:T(8,128)S(1)}, f32[8,384]{1,0:T(8,128)S(1)}, u32[]{:S(2)}, u32[]{:S(2)}) collective-permute-start(f32[8,384]{1,0:T(8,128)S(1)} %add.50), channel_id=1, source_target_pairs={{0,128},{16,144},{32,160},{48,176},{64,192},{80,208},{96,224},{112... | collective-permute-start | bytes 36872 | tf_op jit(solution)/shard_map/ppermute | solution.py:62
  97.3 2.1 %copy-start.1 = (f32[32,144,256]{2,1,0:T(8,128)}, f32[32,144,256]{2,1,0:T(8,128)S(1)}, u32[]{:S(2)}) copy-start(f32[32,144,256]{2,1,0:T(8,128)S(1)} %fusion.1) | copy-start | bytes 14155780
  101.0 10.8 %collective-permute-start.13 = (f32[16,144,256]{2,1,0:T(8,128)}, f32[16,144,256]{2,1,0:T(8,128)S(1)}, u32[]{:S(2)}, u32[]{:S(2)}) collective-permute-start(f32[16,144,256]{2,1,0:T(8,128)} %dynamic-slice_bitcast_fusion), channel_id=1, source_target_pairs={{0,16},{16,0},{32,48},{48,32},{64,80},{80,64},{96,112},{112,96},{1... | collective-permute-start | bytes 7077896 | tf_op jit(solution)/shard_map/ppermute | solution.py:104
  115.2 38.3 %all-to-all-start = ((f32[32,72,256]{2,1,0:T(8,128)}), f32[32,72,256]{2,1,0:T(8,128)S(1)}, u32[]{:S(2)}, u32[]{:S(2)}) async-start(f32[32,72,256]{2,1,0:T(8,128)} %bitcast.36), calls=%async_computation | async-start | bytes 4718592 | tf_op jit(solution)/shard_map/all_to_all | solution.py:106
  153.7 3.2 %collective-permute-start.14 = (f32[72,256]{1,0:T(8,128)S(1)}, f32[72,256]{1,0:T(8,128)S(1)}, u32[]{:S(2)}, u32[]{:S(2)}) collective-permute-start(f32[72,256]{1,0:T(8,128)S(1)} %get-tuple-element.55), channel_id=1, source_target_pairs={{0,16},{16,0},{32,48},{48,32},{64,80},{80,64},{96,112},{112,96},{1... | collective-permute-start | bytes 221192 | tf_op jit(solution)/shard_map/ppermute | solution.py:110
  156.9 21.2 %collective-permute-start.15 = (f32[144,256]{1,0:T(8,128)S(1)}, f32[144,256]{1,0:T(8,128)S(1)}, u32[]{:S(2)}, u32[]{:S(2)}) collective-permute-start(f32[144,256]{1,0:T(8,128)S(1)} %maximum_select_fusion), channel_id=1, source_target_pairs={{5,40},{6,72},{7,104},{8,388},{9,389},{10,390},{11,391},{21,56},{2... | collective-permute-start | bytes 442376 | tf_op jit(solution)/shard_map/ppermute | solution.py:127

commit v12 on v10

--- a/solution.py
+++ b/solution.py
@@ -63,28 +63,30 @@
         wst[0], wst[win + 1:win + 1 + n_b], (((0,), (1,)), ((), ())),
         preferred_element_type=jnp.float32,
     ).transpose(1, 0, 2)
-    prod = jnp.concatenate([near, far_a, far_b], axis=0).reshape(n_dp, col_width, slice_width)
+    prod = jnp.concatenate([near, far_a, far_b], axis=0)
     ones = jnp.ones((8, tok_rows), jnp.bfloat16)
     cs = lax.dot_general(wst, ones, (((1,), (1,)), ((), ())), preferred_element_type=jnp.float32)[..., 0]
     cs_off = jnp.concatenate([cs, cs[win + 1:], jnp.broadcast_to(cs[0], (n_b, slice_width))], axis=0)
-    extra = jnp.pad(
-        cs_off.reshape(n_dp, 1, col_width),
-        ((0, 0), (0, EXTRA_ROWS - 1), (0, slice_width - col_width)),
-    )
-    off_payload = jnp.concatenate([prod, extra], axis=1)
     rows = col_width + EXTRA_ROWS
     half_rows = rows // 2
-    shift = (2 * m - 2 * win) % n_dp
-    doubled = jnp.concatenate([off_payload, off_payload], axis=0)
-    payload = lax.dynamic_slice_in_dim(doubled, (n_dp - shift) % n_dp, n_dp, axis=0)
 
     me = lax.axis_index("dp")
     core = me & 1
-    pairs = payload.reshape(n_dp // 2, 2, rows, slice_width)
-    keep = lax.dynamic_index_in_dim(pairs, core, 1, keepdims=False)
-    send = lax.dynamic_index_in_dim(pairs, 1 - core, 1, keepdims=False)
+    p2 = prod.reshape(n_t, 2, col_width, slice_width)
+    c2 = cs_off.reshape(n_t, 2, 1, col_width)
+
+    def half(h):
+        extra = jnp.pad(
+            lax.dynamic_index_in_dim(c2, h, 1, keepdims=False),
+            ((0, 0), (0, EXTRA_ROWS - 1), (0, slice_width - col_width)),
+        )
+        return jnp.concatenate([lax.dynamic_index_in_dim(p2, h, 1, keepdims=False), extra], axis=1)
+
     core_swap = [(i, i ^ 1) for i in range(n_dp)]
-    chip_sum = keep + lax.ppermute(send, "dp", core_swap)
+    summed = half(core) + lax.ppermute(half(1 - core), "dp", core_swap)
+    shift = (m - win) % n_t
+    doubled = jnp.concatenate([summed, summed], axis=0)
+    chip_sum = lax.dynamic_slice_in_dim(doubled, (n_t - shift) % n_t, n_t, axis=0)
     halves = chip_sum.reshape(n_dp, half_rows, slice_width)
     recv = lax.all_to_all(halves, "dp", 0, 0, tiled=True)
     by_core = jnp.sum(recv.reshape(n_dp // 2, 2, half_rows, slice_width), axis=0)

time: 174 us -> 168 us (0.966)
  local copies, waits for them, and re-layouts: 10.3 us -> 6.4 us
    unnamed x24 -> x14, local copies, waits for them, and re-layouts: 6.52 us -> 4.38 us
    concatenate x2 -> x3, other arithmetic: 4.06 us -> 3.9 us  [the longest x1 1.85 us: body(): doubled = jnp.concatenate([summed, summed], axis=0)]
where the time goes in v12:
time: 168 us; the launch traced here: 167 us
  waiting for transfers between devices  77.1 us (46%)
  starting transfers between devices  67.2 us (40%)
  other arithmetic  7.67 us (5%)
  matrix products  7.64 us (5%)
  local copies, waits for them, and re-layouts  6.4 us (4%)
    all_to_all x1, waiting for transfers between devices, body(): recv = lax.all_to_all(halves, 'dp', 0, 0, tiled=True)  30.8 us
    ppermute x4, starting transfers between devices, body(): bwd = lax.ppermute(bwd, 'tensor', down)  20.1 us
    ppermute x1, waiting for transfers between devices, body(): moved = lax.ppermute(total, ('dp', 'tensor'), perm)  16 us
    ppermute x5, starting transfers between devices, body(): stats = stats + lax.ppermute(stats, 'dp', [(i, i ^ k) for i in range(n_dp)])  15.5 us
    ppermute x4, starting transfers between devices, body(): fwd = lax.ppermute(fwd, 'tensor', up)  10.7 us
    ppermute x4, waiting for transfers between devices, body(): fwd = lax.ppermute(fwd, 'tensor', up)  10.2 us
    ppermute x5, waiting for transfers between devices, body(): stats = stats + lax.ppermute(stats, 'dp', [(i, i ^ k) for i in range(n_dp)])  9.59 us
    all_to_all x1, starting transfers between devices, body(): recv = lax.all_to_all(halves, 'dp', 0, 0, tiled=True)  7.4 us
  transfers between devices with their start and end apart: 17, of which 15 were waited for; matrix products, arithmetic and copies ran while one was open for 2% of the time, Pallas kernels for 0%

profile of v12, /device:TPU:17, one launch (start us, length us, event | category | flops | bytes accessed | tf_op | source)
XLA Modules:
  0.0 167.0 jit_solution(2869822405180743552)
XLA Ops:
  1.9 3.5 %collective-permute-start = (bf16[1024,256]{0,1:T(8,128)(2,1)S(1)}, bf16[1024,256]{0,1:T(8,128)(2,1)S(1)}, u32[]{:S(2)}, u32[]{:S(2)}) collective-permute-start(bf16[1024,256]{0,1:T(8,128)(2,1)S(1)} %copy.29), channel_id=1, source_target_pairs={{0,1},{1,2},{2,3},{3,4},{4,5},{5,6},{6,7},{7,8},{8,9},{9,10},{10,1... | collective-permute-start | bytes 1572872 | tf_op jit(solution)/shard_map/ppermute | solution.py:48
  5.4 9.5 %collective-permute-start.1 = (bf16[1024,256]{0,1:T(8,128)(2,1)S(1)}, bf16[1024,256]{0,1:T(8,128)(2,1)S(1)}, u32[]{:S(2)}, u32[]{:S(2)}) collective-permute-start(bf16[1024,256]{0,1:T(8,128)(2,1)S(1)} %copy.29), channel_id=1, source_target_pairs={{0,15},{1,0},{2,1},{3,2},{4,3},{5,4},{6,5},{7,6},{8,7},{9,8},{10,9... | collective-permute-start | bytes 1572872 | tf_op jit(solution)/shard_map/ppermute | solution.py:49
  17.1 2.9 %collective-permute-start.2 = (f32[8,384]{1,0:T(8,128)S(1)}, f32[8,384]{1,0:T(8,128)S(1)}, u32[]{:S(2)}, u32[]{:S(2)}) collective-permute-start(f32[8,384]{1,0:T(8,128)S(1)} %pad_maximum_fusion.2), channel_id=1, source_target_pairs={{0,16},{16,0},{32,48},{48,32},{64,80},{80,64},{96,112},{112,96},{1... | collective-permute-start | bytes 36872 | tf_op jit(solution)/shard_map/ppermute | solution.py:51
  20.8 2.0 %collective-permute-start.3 = (f32[8,384]{1,0:T(8,128)S(1)}, f32[8,384]{1,0:T(8,128)S(1)}, u32[]{:S(2)}, u32[]{:S(2)}) collective-permute-start(f32[8,384]{1,0:T(8,128)S(1)} %fusion.33), channel_id=1, source_target_pairs={{0,256},{16,272},{32,288},{48,304},{64,320},{80,336},{96,352},{112... | collective-permute-start | bytes 36872 | tf_op jit(solution)/shard_map/ppermute | solution.py:51
  22.7 4.0 %collective-permute-done.3 = f32[8,384]{1,0:T(8,128)S(1)} collective-permute-done((f32[8,384]{1,0:T(8,128)S(1)}, f32[8,384]{1,0:T(8,128)S(1)}, u32[]{:S(2)}, u32[]{:S(2)}) %collective-permute-start.3) | collective-permute-done | bytes 12320 | tf_op jit(solution)/shard_map/ppermute | solution.py:51
  26.7 4.1 %collective-permute-start.5 = (bf16[1024,256]{0,1:T(8,128)(2,1)S(1)}, bf16[1024,256]{0,1:T(8,128)(2,1)S(1)}, u32[]{:S(2)}, u32[]{:S(2)}) collective-permute-start(bf16[1024,256]{0,1:T(8,128)(2,1)S(1)} %collective-permute-done.1), channel_id=1, source_target_pairs={{0,15},{1,0},{2,1},{3,2},{4,3},{5,4},{6,5},{7,6},{8,7},{9,8},{10,9... | collective-permute-start | bytes 1572872 | tf_op jit(solution)/shard_map/ppermute | solution.py:49
  30.8 1.9 %collective-permute-start.4 = (bf16[1024,256]{0,1:T(8,128)(2,1)S(1)}, bf16[1024,256]{0,1:T(8,128)(2,1)S(1)}, u32[]{:S(2)}, u32[]{:S(2)}) collective-permute-start(bf16[1024,256]{0,1:T(8,128)(2,1)S(1)} %collective-permute-done), channel_id=1, source_target_pairs={{0,1},{1,2},{2,3},{3,4},{4,5},{5,6},{6,7},{7,8},{8,9},{9,10},{10,1... | collective-permute-start | bytes 1572872 | tf_op jit(solution)/shard_map/ppermute | solution.py:48
  32.8 3.1 %collective-permute-start.6 = (f32[8,384]{1,0:T(8,128)S(1)}, f32[8,384]{1,0:T(8,128)S(1)}, u32[]{:S(2)}, u32[]{:S(2)}) collective-permute-start(f32[8,384]{1,0:T(8,128)S(1)} %add.53), channel_id=1, source_target_pairs={{0,32},{16,48},{32,0},{48,16},{64,96},{80,112},{96,64},{112,80},{1... | collective-permute-start | bytes 36872 | tf_op jit(solution)/shard_map/ppermute | solution.py:51
  35.9 1.6 collective-permute-done.6
  37.5 3.1 %collective-permute-done.5 = bf16[1024,256]{0,1:T(8,128)(2,1)S(1)} collective-permute-done((bf16[1024,256]{0,1:T(8,128)(2,1)S(1)}, bf16[1024,256]{0,1:T(8,128)(2,1)S(1)}, u32[]{:S(2)}, u32[]{:S(2)}) %collective-permute-start.5) | collective-permute-done | bytes 524320 | tf_op jit(solution)/shard_map/ppermute | solution.py:49
  40.6 5.0 %collective-permute-done.4 = bf16[1024,256]{0,1:T(8,128)(2,1)S(1)} collective-permute-done((bf16[1024,256]{0,1:T(8,128)(2,1)S(1)}, bf16[1024,256]{0,1:T(8,128)(2,1)S(1)}, u32[]{:S(2)}, u32[]{:S(2)}) %collective-permute-start.4) | collective-permute-done | bytes 524320 | tf_op jit(solution)/shard_map/ppermute | solution.py:48
  45.6 1.9 %collective-permute-start.8 = (bf16[1024,256]{0,1:T(8,128)(2,1)S(1)}, bf16[1024,256]{0,1:T(8,128)(2,1)S(1)}, u32[]{:S(2)}, u32[]{:S(2)}) collective-permute-start(bf16[1024,256]{0,1:T(8,128)(2,1)S(1)} %collective-permute-done.5), channel_id=1, source_target_pairs={{0,15},{1,0},{2,1},{3,2},{4,3},{5,4},{6,5},{7,6},{8,7},{9,8},{10,9... | collective-permute-start | bytes 1572872 | tf_op jit(solution)/shard_map/ppermute | solution.py:49
  47.5 3.4 %collective-permute-start.7 = (bf16[1024,256]{0,1:T(8,128)(2,1)S(1)}, bf16[1024,256]{0,1:T(8,128)(2,1)}, u32[]{:S(2)}, u32[]{:S(2)}) collective-permute-start(bf16[1024,256]{0,1:T(8,128)(2,1)S(1)} %collective-permute-done.4), channel_id=1, source_target_pairs={{0,1},{1,2},{2,3},{3,4},{4,5},{5,6},{6,7},{7,8},{8,9},{9,10},{10,1... | collective-permute-start | bytes 1572872 | tf_op jit(solution)/shard_map/ppermute | solution.py:48
  50.9 4.7 %collective-permute-start.9 = (f32[8,384]{1,0:T(8,128)S(1)}, f32[8,384]{1,0:T(8,128)S(1)}, u32[]{:S(2)}, u32[]{:S(2)}) collective-permute-start(f32[8,384]{1,0:T(8,128)S(1)} %add.54), channel_id=1, source_target_pairs={{0,64},{16,80},{32,96},{48,112},{64,0},{80,16},{96,32},{112,48},{1... | collective-permute-start | bytes 36872 | tf_op jit(solution)/shard_map/ppermute | solution.py:51
  58.4 3.1 %collective-permute-done.7 = bf16[1024,256]{0,1:T(8,128)(2,1)} collective-permute-done((bf16[1024,256]{0,1:T(8,128)(2,1)S(1)}, bf16[1024,256]{0,1:T(8,128)(2,1)}, u32[]{:S(2)}, u32[]{:S(2)}) %collective-permute-start.7) | collective-permute-done | bytes 524320 | tf_op jit(solution)/shard_map/ppermute | solution.py:48
  61.6 1.9 %collective-permute-start.10 = (bf16[1024,256]{0,1:T(8,128)(2,1)}, bf16[1024,256]{0,1:T(8,128)(2,1)}, u32[]{:S(2)}, u32[]{:S(2)}) collective-permute-start(bf16[1024,256]{0,1:T(8,128)(2,1)} %collective-permute-done.7), channel_id=1, source_target_pairs={{0,1},{1,2},{2,3},{3,4},{4,5},{5,6},{6,7},{7,8},{8,9},{9,10},{10,1... | collective-permute-start | bytes 1572872 | tf_op jit(solution)/shard_map/ppermute | solution.py:48
  63.5 4.6 %collective-permute-start.11 = (bf16[1024,256]{0,1:T(8,128)(2,1)S(1)}, bf16[1024,256]{0,1:T(8,128)(2,1)}, u32[]{:S(2)}, u32[]{:S(2)}) collective-permute-start(bf16[1024,256]{0,1:T(8,128)(2,1)S(1)} %collective-permute-done.8), channel_id=1, source_target_pairs={{0,15},{1,0},{2,1},{3,2},{4,3},{5,4},{6,5},{7,6},{8,7},{9,8},{10,9... | collective-permute-start | bytes 1572872 | tf_op jit(solution)/shard_map/ppermute | solution.py:49
  68.1 2.9 %collective-permute-start.12 = (f32[8,384]{1,0:T(8,128)S(1)}, f32[8,384]{1,0:T(8,128)S(1)}, u32[]{:S(2)}, u32[]{:S(2)}) collective-permute-start(f32[8,384]{1,0:T(8,128)S(1)} %add.55), channel_id=1, source_target_pairs={{0,128},{16,144},{32,160},{48,176},{64,192},{80,208},{96,224},{112... | collective-permute-start | bytes 36872 | tf_op jit(solution)/shard_map/ppermute | solution.py:51
  71.0 1.9 %collective-permute-done.12 = f32[8,384]{1,0:T(8,128)S(1)} collective-permute-done((f32[8,384]{1,0:T(8,128)S(1)}, f32[8,384]{1,0:T(8,128)S(1)}, u32[]{:S(2)}, u32[]{:S(2)}) %collective-permute-start.12) | collective-permute-done | bytes 12320 | tf_op jit(solution)/shard_map/ppermute | solution.py:51
  72.9 2.0 %collective-permute-done.10 = bf16[1024,256]{0,1:T(8,128)(2,1)} collective-permute-done((bf16[1024,256]{0,1:T(8,128)(2,1)}, bf16[1024,256]{0,1:T(8,128)(2,1)}, u32[]{:S(2)}, u32[]{:S(2)}) %collective-permute-start.10) | collective-permute-done | bytes 524320 | tf_op jit(solution)/shard_map/ppermute | solution.py:48
  81.9 1.7 %fusion.16 = f32[3,256,256]{2,1,0:T(8,128)S(1)} fusion(bf16[1,1024,256]{1,2,0:T(8,128)(2,1)S(1)} %bitcast.63, bf16[1,1024,256]{1,2,0:T(8,128)(2,1)S(1)} %bitcast.61, bf16[1,1024,256]{1,2,0:T(8,128)(2,1)S(1)} %bitcast.59, bf16[1024,256]{0,1:T(8,128)(2,1)} %collective-permute-done.10), kind=kOutput, calls=%fused_computation.24 | convolution fusion | flops 407371776 | bytes 2883584 | tf_op jit(solution)/shard_map/dot_general | solution.py:62
  83.6 1.9 %fusion.2 = f32[4,256,256]{2,1,0:T(8,128)S(1)} fusion(bf16[1,1024,256]{1,2,0:T(8,128)(2,1)} %bitcast.8, bf16[1,1024,256]{1,2,0:T(8,128)(2,1)S(1)} %bitcast.64, bf16[1,1024,256]{1,2,0:T(8,128)(2,1)S(1)} %bitcast.62, bf16[1,1024,256]{1,2,0:T(8,128)(2,1)S(1)} %bitcast.60, bf16[1024,256]{0,1:T(8,128)(2,1)} %collective-permute-done.10), kind=kOutput, calls=%fused_computation.8 | convolution fusion | flops 540016640 | bytes 3670016 | tf_op jit(solution)/shard_map/dot_general | solution.py:58
  86.7 1.7 select_maximum_fusion
  88.3 6.6 %collective-permute-start.13 = (f32[16,144,256]{2,1,0:T(8,128)}, f32[16,144,256]{2,1,0:T(8,128)}, u32[]{:S(2)}, u32[]{:S(2)}) collective-permute-start(f32[16,144,256]{2,1,0:T(8,128)} %select_maximum_fusion), channel_id=1, source_target_pairs={{0,16},{16,0},{32,48},{48,32},{64,80},{80,64},{96,112},{112,96},{1... | collective-permute-start | bytes 7077896 | tf_op jit(solution)/shard_map/ppermute | solution.py:86
  94.9 4.4 %collective-permute-done.13 = f32[16,144,256]{2,1,0:T(8,128)} collective-permute-done((f32[16,144,256]{2,1,0:T(8,128)}, f32[16,144,256]{2,1,0:T(8,128)}, u32[]{:S(2)}, u32[]{:S(2)}) %collective-permute-start.13) | collective-permute-done | bytes 2359328 | tf_op jit(solution)/shard_map/ppermute | solution.py:86
  99.4 2.0 %fusion.1 = f32[16,144,256]{2,1,0:T(8,128)S(1)} fusion(f32[16,144,256]{2,1,0:T(8,128)} %collective-permute-done.13, f32[16,1,128]{2,1,0:T(1,128)S(1)} %get-tuple-element.34, f32[16,128,256]{2,1,0:T(8,128)S(1)} %get-tuple-element.30), kind=kLoop, calls=%fused_computation.6 | loop fusion | flops 2359296 | bytes 6823936 | tf_op jit(solution)/shard_map/add | solution.py:86
  101.3 1.9 %fusion = f32[16,144,256]{2,1,0:T(8,128)} fusion(s32[]{:T(128)S(6)} %select_n.57, f32[16,144,256]{2,1,0:T(8,128)S(1)} %fusion.1), kind=kLoop, calls=%fused_computation.3 | loop fusion | flops 589824 | bytes 4718596 | tf_op jit(solution)/shard_map/concatenate | solution.py:88
  103.2 7.4 %all-to-all-start = ((f32[32,72,256]{2,1,0:T(8,128)}), f32[32,72,256]{2,1,0:T(8,128)S(1)}, u32[]{:S(2)}, u32[]{:S(2)}) async-start(f32[32,72,256]{2,1,0:T(8,128)} %bitcast.58), calls=%async_computation | async-start | bytes 4718592 | tf_op jit(solution)/shard_map/all_to_all | solution.py:91
  110.7 30.8 %all-to-all-done = f32[32,72,256]{2,1,0:T(8,128)S(1)} async-done(((f32[32,72,256]{2,1,0:T(8,128)}), f32[32,72,256]{2,1,0:T(8,128)S(1)}, u32[]{:S(2)}, u32[]{:S(2)}) %all-to-all-start) | async-done | bytes 2359328 | tf_op jit(solution)/shard_map/all_to_all | solution.py:91
  141.6 2.3 %collective-permute-start.14 = (f32[72,256]{1,0:T(8,128)S(1)}, f32[72,256]{1,0:T(8,128)S(1)}, u32[]{:S(2)}, u32[]{:S(2)}) collective-permute-start(f32[72,256]{1,0:T(8,128)S(1)} %get-tuple-element.33), channel_id=1, source_target_pairs={{0,16},{16,0},{32,48},{48,32},{64,80},{80,64},{96,112},{112,96},{1... | collective-permute-start | bytes 221192 | tf_op jit(solution)/shard_map/ppermute | solution.py:95
  144.8 4.6 %collective-permute-start.15 = (f32[144,256]{1,0:T(8,128)S(1)}, f32[144,256]{1,0:T(8,128)S(1)}, u32[]{:S(2)}, u32[]{:S(2)}) collective-permute-start(f32[144,256]{1,0:T(8,128)S(1)} %maximum_select_fusion), channel_id=1, source_target_pairs={{5,40},{6,72},{7,104},{8,388},{9,389},{10,390},{11,391},{21,56},{2... | collective-permute-start | bytes 442376 | tf_op jit(solution)/shard_map/ppermute | solution.py:112
  150.1 16.0 %collective-permute-done.15 = f32[144,256]{1,0:T(8,128)S(1)} collective-permute-done((f32[144,256]{1,0:T(8,128)S(1)}, f32[144,256]{1,0:T(8,128)S(1)}, u32[]{:S(2)}, u32[]{:S(2)}) %collective-permute-start.15) | collective-permute-done | bytes 147488 | tf_op jit(solution)/shard_map/ppermute | solution.py:112
  (52 shorter events, 17.6 us)
Async XLA Ops:
  1.9 24.8 %collective-permute-start = (bf16[1024,256]{0,1:T(8,128)(2,1)S(1)}, bf16[1024,256]{0,1:T(8,128)(2,1)S(1)}, u32[]{:S(2)}, u32[]{:S(2)}) collective-permute-start(bf16[1024,256]{0,1:T(8,128)(2,1)S(1)} %copy.29), channel_id=1, source_target_pairs={{0,1},{1,2},{2,3},{3,4},{4,5},{5,6},{6,7},{7,8},{8,9},{9,10},{10,1... | collective-permute-start | bytes 1572872 | tf_op jit(solution)/shard_map/ppermute | solution.py:48
  5.4 21.3 %collective-permute-start.1 = (bf16[1024,256]{0,1:T(8,128)(2,1)S(1)}, bf16[1024,256]{0,1:T(8,128)(2,1)S(1)}, u32[]{:S(2)}, u32[]{:S(2)}) collective-permute-start(bf16[1024,256]{0,1:T(8,128)(2,1)S(1)} %copy.29), channel_id=1, source_target_pairs={{0,15},{1,0},{2,1},{3,2},{4,3},{5,4},{6,5},{7,6},{8,7},{9,8},{10,9... | collective-permute-start | bytes 1572872 | tf_op jit(solution)/shard_map/ppermute | solution.py:49
  17.1 3.7 %collective-permute-start.2 = (f32[8,384]{1,0:T(8,128)S(1)}, f32[8,384]{1,0:T(8,128)S(1)}, u32[]{:S(2)}, u32[]{:S(2)}) collective-permute-start(f32[8,384]{1,0:T(8,128)S(1)} %pad_maximum_fusion.2), channel_id=1, source_target_pairs={{0,16},{16,0},{32,48},{48,32},{64,80},{80,64},{96,112},{112,96},{1... | collective-permute-start | bytes 36872 | tf_op jit(solution)/shard_map/ppermute | solution.py:51
  20.8 5.9 %collective-permute-start.3 = (f32[8,384]{1,0:T(8,128)S(1)}, f32[8,384]{1,0:T(8,128)S(1)}, u32[]{:S(2)}, u32[]{:S(2)}) collective-permute-start(f32[8,384]{1,0:T(8,128)S(1)} %fusion.33), channel_id=1, source_target_pairs={{0,256},{16,272},{32,288},{48,304},{64,320},{80,336},{96,352},{112... | collective-permute-start | bytes 36872 | tf_op jit(solution)/shard_map/ppermute | solution.py:51
  26.7 13.9 %collective-permute-start.5 = (bf16[1024,256]{0,1:T(8,128)(2,1)S(1)}, bf16[1024,256]{0,1:T(8,128)(2,1)S(1)}, u32[]{:S(2)}, u32[]{:S(2)}) collective-permute-start(bf16[1024,256]{0,1:T(8,128)(2,1)S(1)} %collective-permute-done.1), channel_id=1, source_target_pairs={{0,15},{1,0},{2,1},{3,2},{4,3},{5,4},{6,5},{7,6},{8,7},{9,8},{10,9... | collective-permute-start | bytes 1572872 | tf_op jit(solution)/shard_map/ppermute | solution.py:49
  30.8 14.8 %collective-permute-start.4 = (bf16[1024,256]{0,1:T(8,128)(2,1)S(1)}, bf16[1024,256]{0,1:T(8,128)(2,1)S(1)}, u32[]{:S(2)}, u32[]{:S(2)}) collective-permute-start(bf16[1024,256]{0,1:T(8,128)(2,1)S(1)} %collective-permute-done), channel_id=1, source_target_pairs={{0,1},{1,2},{2,3},{3,4},{4,5},{5,6},{6,7},{7,8},{8,9},{9,10},{10,1... | collective-permute-start | bytes 1572872 | tf_op jit(solution)/shard_map/ppermute | solution.py:48
  32.8 4.7 %collective-permute-start.6 = (f32[8,384]{1,0:T(8,128)S(1)}, f32[8,384]{1,0:T(8,128)S(1)}, u32[]{:S(2)}, u32[]{:S(2)}) collective-permute-start(f32[8,384]{1,0:T(8,128)S(1)} %add.53), channel_id=1, source_target_pairs={{0,32},{16,48},{32,0},{48,16},{64,96},{80,112},{96,64},{112,80},{1... | collective-permute-start | bytes 36872 | tf_op jit(solution)/shard_map/ppermute | solution.py:51
  45.6 12.8 %collective-permute-start.8 = (bf16[1024,256]{0,1:T(8,128)(2,1)S(1)}, bf16[1024,256]{0,1:T(8,128)(2,1)S(1)}, u32[]{:S(2)}, u32[]{:S(2)}) collective-permute-start(bf16[1024,256]{0,1:T(8,128)(2,1)S(1)} %collective-permute-done.5), channel_id=1, source_target_pairs={{0,15},{1,0},{2,1},{3,2},{4,3},{5,4},{6,5},{7,6},{8,7},{9,8},{10,9... | collective-permute-start | bytes 1572872 | tf_op jit(solution)/shard_map/ppermute | solution.py:49
  47.5 14.0 %collective-permute-start.7 = (bf16[1024,256]{0,1:T(8,128)(2,1)S(1)}, bf16[1024,256]{0,1:T(8,128)(2,1)}, u32[]{:S(2)}, u32[]{:S(2)}) collective-permute-start(bf16[1024,256]{0,1:T(8,128)(2,1)S(1)} %collective-permute-done.4), channel_id=1, source_target_pairs={{0,1},{1,2},{2,3},{3,4},{4,5},{5,6},{6,7},{7,8},{8,9},{9,10},{10,1... | collective-permute-start | bytes 1572872 | tf_op jit(solution)/shard_map/ppermute | solution.py:48
  50.9 5.9 %collective-permute-start.9 = (f32[8,384]{1,0:T(8,128)S(1)}, f32[8,384]{1,0:T(8,128)S(1)}, u32[]{:S(2)}, u32[]{:S(2)}) collective-permute-start(f32[8,384]{1,0:T(8,128)S(1)} %add.54), channel_id=1, source_target_pairs={{0,64},{16,80},{32,96},{48,112},{64,0},{80,16},{96,32},{112,48},{1... | collective-permute-start | bytes 36872 | tf_op jit(solution)/shard_map/ppermute | solution.py:51
  61.6 13.4 %collective-permute-start.10 = (bf16[1024,256]{0,1:T(8,128)(2,1)}, bf16[1024,256]{0,1:T(8,128)(2,1)}, u32[]{:S(2)}, u32[]{:S(2)}) collective-permute-start(bf16[1024,256]{0,1:T(8,128)(2,1)} %collective-permute-done.7), channel_id=1, source_target_pairs={{0,1},{1,2},{2,3},{3,4},{4,5},{5,6},{6,7},{7,8},{8,9},{9,10},{10,1... | collective-permute-start | bytes 1572872 | tf_op jit(solution)/shard_map/ppermute | solution.py:48
  63.5 12.0 %collective-permute-start.11 = (bf16[1024,256]{0,1:T(8,128)(2,1)S(1)}, bf16[1024,256]{0,1:T(8,128)(2,1)}, u32[]{:S(2)}, u32[]{:S(2)}) collective-permute-start(bf16[1024,256]{0,1:T(8,128)(2,1)S(1)} %collective-permute-done.8), channel_id=1, source_target_pairs={{0,15},{1,0},{2,1},{3,2},{4,3},{5,4},{6,5},{7,6},{8,7},{9,8},{10,9... | collective-permute-start | bytes 1572872 | tf_op jit(solution)/shard_map/ppermute | solution.py:49
  68.1 4.8 %collective-permute-start.12 = (f32[8,384]{1,0:T(8,128)S(1)}, f32[8,384]{1,0:T(8,128)S(1)}, u32[]{:S(2)}, u32[]{:S(2)}) collective-permute-start(f32[8,384]{1,0:T(8,128)S(1)} %add.55), channel_id=1, source_target_pairs={{0,128},{16,144},{32,160},{48,176},{64,192},{80,208},{96,224},{112... | collective-permute-start | bytes 36872 | tf_op jit(solution)/shard_map/ppermute | solution.py:51
  77.7 1.3 copy-start
  81.8 1.7 %copy-start.1 = (f32[9,256,8]{1,2,0:T(8,128)}, f32[9,256,8]{1,2,0:T(8,128)S(1)}, u32[]{:S(2)}) copy-start(f32[9,256,8]{1,2,0:T(8,128)S(1)} %fusion.27) | copy-start | bytes 221188
  85.9 0.7 slice-start
  88.3 11.0 %collective-permute-start.13 = (f32[16,144,256]{2,1,0:T(8,128)}, f32[16,144,256]{2,1,0:T(8,128)}, u32[]{:S(2)}, u32[]{:S(2)}) collective-permute-start(f32[16,144,256]{2,1,0:T(8,128)} %select_maximum_fusion), channel_id=1, source_target_pairs={{0,16},{16,0},{32,48},{48,32},{64,80},{80,64},{96,112},{112,96},{1... | collective-permute-start | bytes 7077896 | tf_op jit(solution)/shard_map/ppermute | solution.py:86
  103.2 38.3 %all-to-all-start = ((f32[32,72,256]{2,1,0:T(8,128)}), f32[32,72,256]{2,1,0:T(8,128)S(1)}, u32[]{:S(2)}, u32[]{:S(2)}) async-start(f32[32,72,256]{2,1,0:T(8,128)} %bitcast.58), calls=%async_computation | async-start | bytes 4718592 | tf_op jit(solution)/shard_map/all_to_all | solution.py:91
  141.6 3.2 %collective-permute-start.14 = (f32[72,256]{1,0:T(8,128)S(1)}, f32[72,256]{1,0:T(8,128)S(1)}, u32[]{:S(2)}, u32[]{:S(2)}) collective-permute-start(f32[72,256]{1,0:T(8,128)S(1)} %get-tuple-element.33), channel_id=1, source_target_pairs={{0,16},{16,0},{32,48},{48,32},{64,80},{80,64},{96,112},{112,96},{1... | collective-permute-start | bytes 221192 | tf_op jit(solution)/shard_map/ppermute | solution.py:95
  144.8 21.3 %collective-permute-start.15 = (f32[144,256]{1,0:T(8,128)S(1)}, f32[144,256]{1,0:T(8,128)S(1)}, u32[]{:S(2)}, u32[]{:S(2)}) collective-permute-start(f32[144,256]{1,0:T(8,128)S(1)} %maximum_select_fusion), channel_id=1, source_target_pairs={{5,40},{6,72},{7,104},{8,388},{9,389},{10,390},{11,391},{21,56},{2... | collective-permute-start | bytes 442376 | tf_op jit(solution)/shard_map/ppermute | solution.py:112

commit v13 on v12

--- a/solution.py
+++ b/solution.py
@@ -43,7 +43,8 @@
     up = [(i, (i + 1) % n_t) for i in range(n_t)]
     down = [(i, (i - 1) % n_t) for i in range(n_t)]
     bfly = [1 << b for b in range(n_dp.bit_length() - 1)]
-    per_step = [bfly[i::win] for i in range(win)]
+    per_step = [[k] for k in bfly[:win]]
+    late_bfly = bfly[win:]
     for step in range(1, win + 1):
         fwd = lax.ppermute(fwd, "tensor", up)
         bwd = lax.ppermute(bwd, "tensor", down)
@@ -83,7 +84,11 @@
         return jnp.concatenate([lax.dynamic_index_in_dim(p2, h, 1, keepdims=False), extra], axis=1)
 
     core_swap = [(i, i ^ 1) for i in range(n_dp)]
-    summed = half(core) + lax.ppermute(half(1 - core), "dp", core_swap)
+    swapped = lax.ppermute(half(1 - core), "dp", core_swap)
+    for k in late_bfly:
+        stats = stats + lax.ppermute(stats, "dp", [(i, i ^ k) for i in range(n_dp)])
+    swapped, stats = lax.optimization_barrier((swapped, stats))
+    summed = half(core) + swapped
     shift = (m - win) % n_t
     doubled = jnp.concatenate([summed, summed], axis=0)
     chip_sum = lax.dynamic_slice_in_dim(doubled, (n_t - shift) % n_t, n_t, axis=0)

time: 168 us -> 172 us (1.024)
  waiting for transfers between devices: 77.1 us -> 80.2 us
    ppermute x4, waiting for transfers between devices: 10.2 us -> 15.4 us  [body(): fwd = lax.ppermute(fwd, 'tensor', up)]
    ppermute x1, waiting for transfers between devices: 4.44 us -> 0.01 us  [body(): swapped = lax.ppermute(half(1 - core), 'dp', core_swap)]
    ppermute x4, waiting for transfers between devices: 5.22 us -> 7.35 us  [body(): bwd = lax.ppermute(bwd, 'tensor', down)]
  transfers between devices with their start and end apart: 17 -> 17, of which waited for: 15 -> 16; matrix products, arithmetic and copies ran while one was open for 2% -> 2% of each run, Pallas kernels for 0% -> 0%
where the time goes in v13:
time: 172 us; the launch traced here: 171 us
  waiting for transfers between devices  80.2 us (47%)
  starting transfers between devices  67.7 us (39%)
  other arithmetic  7.67 us (4%)
  matrix products  7.64 us (4%)
  local copies, waits for them, and re-layouts  6.4 us (4%)
    all_to_all x1, waiting for transfers between devices, body(): recv = lax.all_to_all(halves, 'dp', 0, 0, tiled=True)  30.8 us
    ppermute x4, starting transfers between devices, body(): bwd = lax.ppermute(bwd, 'tensor', down)  18.6 us
    ppermute x1, waiting for transfers between devices, body(): moved = lax.ppermute(total, ('dp', 'tensor'), perm)  16.3 us
    ppermute x5, starting transfers between devices, body(): stats = stats + lax.ppermute(stats, 'dp', [(i, i ^ k) for i in range(n_dp)])  15.5 us
    ppermute x4, waiting for transfers between devices, body(): fwd = lax.ppermute(fwd, 'tensor', up)  15.4 us
    ppermute x4, starting transfers between devices, body(): fwd = lax.ppermute(fwd, 'tensor', up)  12.2 us
    ppermute x5, waiting for transfers between devices, body(): stats = stats + lax.ppermute(stats, 'dp', [(i, i ^ k) for i in range(n_dp)])  9.55 us
    all_to_all x1, starting transfers between devices, body(): recv = lax.all_to_all(halves, 'dp', 0, 0, tiled=True)  8.2 us
  transfers between devices with their start and end apart: 17, of which 16 were waited for; matrix products, arithmetic and copies ran while one was open for 2% of the time, Pallas kernels for 0%

profile of v13, /device:TPU:17, one launch (start us, length us, event | category | flops | bytes accessed | tf_op | source)
XLA Modules:
  0.0 170.7 jit_solution(7816965066186030099)
XLA Ops:
  1.9 3.5 %collective-permute-start = (bf16[1024,256]{0,1:T(8,128)(2,1)S(1)}, bf16[1024,256]{0,1:T(8,128)(2,1)S(1)}, u32[]{:S(2)}, u32[]{:S(2)}) collective-permute-start(bf16[1024,256]{0,1:T(8,128)(2,1)S(1)} %copy.29), channel_id=1, source_target_pairs={{0,1},{1,2},{2,3},{3,4},{4,5},{5,6},{6,7},{7,8},{8,9},{9,10},{10,1... | collective-permute-start | bytes 1572872 | tf_op jit(solution)/shard_map/ppermute | solution.py:49
  5.4 9.5 %collective-permute-start.1 = (bf16[1024,256]{0,1:T(8,128)(2,1)S(1)}, bf16[1024,256]{0,1:T(8,128)(2,1)S(1)}, u32[]{:S(2)}, u32[]{:S(2)}) collective-permute-start(bf16[1024,256]{0,1:T(8,128)(2,1)S(1)} %copy.29), channel_id=1, source_target_pairs={{0,15},{1,0},{2,1},{3,2},{4,3},{5,4},{6,5},{7,6},{8,7},{9,8},{10,9... | collective-permute-start | bytes 1572872 | tf_op jit(solution)/shard_map/ppermute | solution.py:50
  17.1 2.9 %collective-permute-start.2 = (f32[8,384]{1,0:T(8,128)S(1)}, f32[8,384]{1,0:T(8,128)S(1)}, u32[]{:S(2)}, u32[]{:S(2)}) collective-permute-start(f32[8,384]{1,0:T(8,128)S(1)} %pad_maximum_fusion.2), channel_id=1, source_target_pairs={{0,16},{16,0},{32,48},{48,32},{64,80},{80,64},{96,112},{112,96},{1... | collective-permute-start | bytes 36872 | tf_op jit(solution)/shard_map/ppermute | solution.py:52
  20.8 3.9 %collective-permute-done = bf16[1024,256]{0,1:T(8,128)(2,1)S(1)} collective-permute-done((bf16[1024,256]{0,1:T(8,128)(2,1)S(1)}, bf16[1024,256]{0,1:T(8,128)(2,1)S(1)}, u32[]{:S(2)}, u32[]{:S(2)}) %collective-permute-start) | collective-permute-done | bytes 524320 | tf_op jit(solution)/shard_map/ppermute | solution.py:49
  25.5 5.3 %collective-permute-start.4 = (bf16[1024,256]{0,1:T(8,128)(2,1)S(1)}, bf16[1024,256]{0,1:T(8,128)(2,1)S(1)}, u32[]{:S(2)}, u32[]{:S(2)}) collective-permute-start(bf16[1024,256]{0,1:T(8,128)(2,1)S(1)} %collective-permute-done.1), channel_id=1, source_target_pairs={{0,15},{1,0},{2,1},{3,2},{4,3},{5,4},{6,5},{7,6},{8,7},{9,8},{10,9... | collective-permute-start | bytes 1572872 | tf_op jit(solution)/shard_map/ppermute | solution.py:50
  30.8 1.9 %collective-permute-start.3 = (bf16[1024,256]{0,1:T(8,128)(2,1)S(1)}, bf16[1024,256]{0,1:T(8,128)(2,1)S(1)}, u32[]{:S(2)}, u32[]{:S(2)}) collective-permute-start(bf16[1024,256]{0,1:T(8,128)(2,1)S(1)} %collective-permute-done), channel_id=1, source_target_pairs={{0,1},{1,2},{2,3},{3,4},{4,5},{5,6},{6,7},{7,8},{8,9},{9,10},{10,1... | collective-permute-start | bytes 1572872 | tf_op jit(solution)/shard_map/ppermute | solution.py:49
  32.8 3.1 %collective-permute-start.5 = (f32[8,384]{1,0:T(8,128)S(1)}, f32[8,384]{1,0:T(8,128)S(1)}, u32[]{:S(2)}, u32[]{:S(2)}) collective-permute-start(f32[8,384]{1,0:T(8,128)S(1)} %fusion.33), channel_id=1, source_target_pairs={{0,32},{16,48},{32,0},{48,16},{64,96},{80,112},{96,64},{112,80},{1... | collective-permute-start | bytes 36872 | tf_op jit(solution)/shard_map/ppermute | solution.py:52
  37.5 3.1 %collective-permute-done.4 = bf16[1024,256]{0,1:T(8,128)(2,1)S(1)} collective-permute-done((bf16[1024,256]{0,1:T(8,128)(2,1)S(1)}, bf16[1024,256]{0,1:T(8,128)(2,1)S(1)}, u32[]{:S(2)}, u32[]{:S(2)}) %collective-permute-start.4) | collective-permute-done | bytes 524320 | tf_op jit(solution)/shard_map/ppermute | solution.py:50
  40.6 5.0 %collective-permute-done.3 = bf16[1024,256]{0,1:T(8,128)(2,1)S(1)} collective-permute-done((bf16[1024,256]{0,1:T(8,128)(2,1)S(1)}, bf16[1024,256]{0,1:T(8,128)(2,1)S(1)}, u32[]{:S(2)}, u32[]{:S(2)}) %collective-permute-start.3) | collective-permute-done | bytes 524320 | tf_op jit(solution)/shard_map/ppermute | solution.py:49
  45.6 1.9 %collective-permute-start.7 = (bf16[1024,256]{0,1:T(8,128)(2,1)S(1)}, bf16[1024,256]{0,1:T(8,128)(2,1)S(1)}, u32[]{:S(2)}, u32[]{:S(2)}) collective-permute-start(bf16[1024,256]{0,1:T(8,128)(2,1)S(1)} %collective-permute-done.4), channel_id=1, source_target_pairs={{0,15},{1,0},{2,1},{3,2},{4,3},{5,4},{6,5},{7,6},{8,7},{9,8},{10,9... | collective-permute-start | bytes 1572872 | tf_op jit(solution)/shard_map/ppermute | solution.py:50
  47.5 3.4 %collective-permute-start.6 = (bf16[1024,256]{0,1:T(8,128)(2,1)S(1)}, bf16[1024,256]{0,1:T(8,128)(2,1)}, u32[]{:S(2)}, u32[]{:S(2)}) collective-permute-start(bf16[1024,256]{0,1:T(8,128)(2,1)S(1)} %collective-permute-done.3), channel_id=1, source_target_pairs={{0,1},{1,2},{2,3},{3,4},{4,5},{5,6},{6,7},{7,8},{8,9},{9,10},{10,1... | collective-permute-start | bytes 1572872 | tf_op jit(solution)/shard_map/ppermute | solution.py:49
  50.9 4.7 %collective-permute-start.8 = (f32[8,384]{1,0:T(8,128)S(1)}, f32[8,384]{1,0:T(8,128)S(1)}, u32[]{:S(2)}, u32[]{:S(2)}) collective-permute-start(f32[8,384]{1,0:T(8,128)S(1)} %add.53), channel_id=1, source_target_pairs={{0,64},{16,80},{32,96},{48,112},{64,0},{80,16},{96,32},{112,48},{1... | collective-permute-start | bytes 36872 | tf_op jit(solution)/shard_map/ppermute | solution.py:52
  58.4 3.1 %collective-permute-done.6 = bf16[1024,256]{0,1:T(8,128)(2,1)} collective-permute-done((bf16[1024,256]{0,1:T(8,128)(2,1)S(1)}, bf16[1024,256]{0,1:T(8,128)(2,1)}, u32[]{:S(2)}, u32[]{:S(2)}) %collective-permute-start.6) | collective-permute-done | bytes 524320 | tf_op jit(solution)/shard_map/ppermute | solution.py:49
  61.6 1.9 %collective-permute-start.10 = (bf16[1024,256]{0,1:T(8,128)(2,1)S(1)}, bf16[1024,256]{0,1:T(8,128)(2,1)}, u32[]{:S(2)}, u32[]{:S(2)}) collective-permute-start(bf16[1024,256]{0,1:T(8,128)(2,1)S(1)} %collective-permute-done.7), channel_id=1, source_target_pairs={{0,15},{1,0},{2,1},{3,2},{4,3},{5,4},{6,5},{7,6},{8,7},{9,8},{10,9... | collective-permute-start | bytes 1572872 | tf_op jit(solution)/shard_map/ppermute | solution.py:50
  63.5 3.4 %collective-permute-start.9 = (bf16[1024,256]{0,1:T(8,128)(2,1)}, bf16[1024,256]{0,1:T(8,128)(2,1)}, u32[]{:S(2)}, u32[]{:S(2)}) collective-permute-start(bf16[1024,256]{0,1:T(8,128)(2,1)} %collective-permute-done.6), channel_id=1, source_target_pairs={{0,1},{1,2},{2,3},{3,4},{4,5},{5,6},{6,7},{7,8},{8,9},{9,10},{10,1... | collective-permute-start | bytes 1572872 | tf_op jit(solution)/shard_map/ppermute | solution.py:49
  66.9 2.9 %collective-permute-start.11 = (f32[8,384]{1,0:T(8,128)S(1)}, f32[8,384]{1,0:T(8,128)S(1)}, u32[]{:S(2)}, u32[]{:S(2)}) collective-permute-start(f32[8,384]{1,0:T(8,128)S(1)} %add.54), channel_id=1, source_target_pairs={{0,128},{16,144},{32,160},{48,176},{64,192},{80,208},{96,224},{112... | collective-permute-start | bytes 36872 | tf_op jit(solution)/shard_map/ppermute | solution.py:52
  69.8 1.9 %collective-permute-done.11 = f32[8,384]{1,0:T(8,128)S(1)} collective-permute-done((f32[8,384]{1,0:T(8,128)S(1)}, f32[8,384]{1,0:T(8,128)S(1)}, u32[]{:S(2)}, u32[]{:S(2)}) %collective-permute-start.11) | collective-permute-done | bytes 12320 | tf_op jit(solution)/shard_map/ppermute | solution.py:52
  71.7 1.8 %collective-permute-done.10 = bf16[1024,256]{0,1:T(8,128)(2,1)} collective-permute-done((bf16[1024,256]{0,1:T(8,128)(2,1)S(1)}, bf16[1024,256]{0,1:T(8,128)(2,1)}, u32[]{:S(2)}, u32[]{:S(2)}) %collective-permute-start.10) | collective-permute-done | bytes 524320 | tf_op jit(solution)/shard_map/ppermute | solution.py:50
  73.5 3.4 %collective-permute-done.9 = bf16[1024,256]{0,1:T(8,128)(2,1)} collective-permute-done((bf16[1024,256]{0,1:T(8,128)(2,1)}, bf16[1024,256]{0,1:T(8,128)(2,1)}, u32[]{:S(2)}, u32[]{:S(2)}) %collective-permute-start.9) | collective-permute-done | bytes 524320 | tf_op jit(solution)/shard_map/ppermute | solution.py:49
  83.2 1.7 fusion.16
  84.9 1.9 %fusion.2 = f32[4,256,256]{2,1,0:T(8,128)S(1)} fusion(bf16[1,1024,256]{1,2,0:T(8,128)(2,1)} %bitcast.8, bf16[1,1024,256]{1,2,0:T(8,128)(2,1)S(1)} %bitcast.64, bf16[1,1024,256]{1,2,0:T(8,128)(2,1)S(1)} %bitcast.62, bf16[1,1024,256]{1,2,0:T(8,128)(2,1)S(1)} %bitcast.60, bf16[1024,256]{0,1:T(8,128)(2,1)} %collective-permute-done.9), kind=kOutput, calls=%fused_computation.8 | convolution fusion | flops 540016640 | bytes 3670016 | tf_op jit(solution)/shard_map/dot_general | solution.py:59
  88.0 1.7 select_maximum_fusion
  89.7 6.3 %collective-permute-start.12 = (f32[16,144,256]{2,1,0:T(8,128)}, f32[16,144,256]{2,1,0:T(8,128)}, u32[]{:S(2)}, u32[]{:S(2)}) collective-permute-start(f32[16,144,256]{2,1,0:T(8,128)} %select_maximum_fusion), channel_id=1, source_target_pairs={{0,16},{16,0},{32,48},{48,32},{64,80},{80,64},{96,112},{112,96},{1... | collective-permute-start | bytes 7077896 | tf_op jit(solution)/shard_map/ppermute | solution.py:87
  95.9 2.0 %collective-permute-start.13 = (f32[8,384]{1,0:T(8,128)S(1)}, f32[8,384]{1,0:T(8,128)S(1)}, u32[]{:S(2)}, u32[]{:S(2)}) collective-permute-start(f32[8,384]{1,0:T(8,128)S(1)} %add.55), channel_id=1, source_target_pairs={{0,256},{16,272},{32,288},{48,304},{64,320},{80,336},{96,352},{112... | collective-permute-start | bytes 36872 | tf_op jit(solution)/shard_map/ppermute | solution.py:89
  98.0 3.9 %collective-permute-done.13 = f32[8,384]{1,0:T(8,128)S(1)} collective-permute-done((f32[8,384]{1,0:T(8,128)S(1)}, f32[8,384]{1,0:T(8,128)S(1)}, u32[]{:S(2)}, u32[]{:S(2)}) %collective-permute-start.13) | collective-permute-done | bytes 12320 | tf_op jit(solution)/shard_map/ppermute | solution.py:89
  101.9 2.0 %fusion.1 = f32[16,144,256]{2,1,0:T(8,128)S(1)} fusion(f32[16,144,256]{2,1,0:T(8,128)} %collective-permute-done.12, f32[16,1,128]{2,1,0:T(1,128)S(1)} %get-tuple-element.38, f32[16,128,256]{2,1,0:T(8,128)S(1)} %get-tuple-element.34), kind=kLoop, calls=%fused_computation.6 | loop fusion | flops 2359296 | bytes 6823936 | tf_op jit(solution)/shard_map/add | solution.py:91
  103.9 1.9 %fusion = f32[16,144,256]{2,1,0:T(8,128)} fusion(s32[]{:T(128)S(6)} %select_n.57, f32[16,144,256]{2,1,0:T(8,128)S(1)} %fusion.1), kind=kLoop, calls=%fused_computation.3 | loop fusion | flops 589824 | bytes 4718596 | tf_op jit(solution)/shard_map/concatenate | solution.py:93
  105.7 8.2 %all-to-all-start = ((f32[32,72,256]{2,1,0:T(8,128)}), f32[32,72,256]{2,1,0:T(8,128)S(1)}, u32[]{:S(2)}, u32[]{:S(2)}) async-start(f32[32,72,256]{2,1,0:T(8,128)} %bitcast.58), calls=%async_computation | async-start | bytes 4718592 | tf_op jit(solution)/shard_map/all_to_all | solution.py:96
  114.0 30.8 %all-to-all-done = f32[32,72,256]{2,1,0:T(8,128)S(1)} async-done(((f32[32,72,256]{2,1,0:T(8,128)}), f32[32,72,256]{2,1,0:T(8,128)S(1)}, u32[]{:S(2)}, u32[]{:S(2)}) %all-to-all-start) | async-done | bytes 2359328 | tf_op jit(solution)/shard_map/all_to_all | solution.py:96
  145.0 2.3 %collective-permute-start.14 = (f32[72,256]{1,0:T(8,128)S(1)}, f32[72,256]{1,0:T(8,128)S(1)}, u32[]{:S(2)}, u32[]{:S(2)}) collective-permute-start(f32[72,256]{1,0:T(8,128)S(1)} %get-tuple-element.37), channel_id=1, source_target_pairs={{0,16},{16,0},{32,48},{48,32},{64,80},{80,64},{96,112},{112,96},{1... | collective-permute-start | bytes 221192 | tf_op jit(solution)/shard_map/ppermute | solution.py:100
  148.2 4.6 %collective-permute-start.15 = (f32[144,256]{1,0:T(8,128)S(1)}, f32[144,256]{1,0:T(8,128)S(1)}, u32[]{:S(2)}, u32[]{:S(2)}) collective-permute-start(f32[144,256]{1,0:T(8,128)S(1)} %maximum_select_fusion), channel_id=1, source_target_pairs={{5,40},{6,72},{7,104},{8,388},{9,389},{10,390},{11,391},{21,56},{2... | collective-permute-start | bytes 442376 | tf_op jit(solution)/shard_map/ppermute | solution.py:117
  153.5 16.3 %collective-permute-done.15 = f32[144,256]{1,0:T(8,128)S(1)} collective-permute-done((f32[144,256]{1,0:T(8,128)S(1)}, f32[144,256]{1,0:T(8,128)S(1)}, u32[]{:S(2)}, u32[]{:S(2)}) %collective-permute-start.15) | collective-permute-done | bytes 147488 | tf_op jit(solution)/shard_map/ppermute | solution.py:117
  (52 shorter events, 19.6 us)
Async XLA Ops:
  1.9 22.7 %collective-permute-start = (bf16[1024,256]{0,1:T(8,128)(2,1)S(1)}, bf16[1024,256]{0,1:T(8,128)(2,1)S(1)}, u32[]{:S(2)}, u32[]{:S(2)}) collective-permute-start(bf16[1024,256]{0,1:T(8,128)(2,1)S(1)} %copy.29), channel_id=1, source_target_pairs={{0,1},{1,2},{2,3},{3,4},{4,5},{5,6},{6,7},{7,8},{8,9},{9,10},{10,1... | collective-permute-start | bytes 1572872 | tf_op jit(solution)/shard_map/ppermute | solution.py:49
  5.4 20.1 %collective-permute-start.1 = (bf16[1024,256]{0,1:T(8,128)(2,1)S(1)}, bf16[1024,256]{0,1:T(8,128)(2,1)S(1)}, u32[]{:S(2)}, u32[]{:S(2)}) collective-permute-start(bf16[1024,256]{0,1:T(8,128)(2,1)S(1)} %copy.29), channel_id=1, source_target_pairs={{0,15},{1,0},{2,1},{3,2},{4,3},{5,4},{6,5},{7,6},{8,7},{9,8},{10,9... | collective-permute-start | bytes 1572872 | tf_op jit(solution)/shard_map/ppermute | solution.py:50
  17.1 3.7 %collective-permute-start.2 = (f32[8,384]{1,0:T(8,128)S(1)}, f32[8,384]{1,0:T(8,128)S(1)}, u32[]{:S(2)}, u32[]{:S(2)}) collective-permute-start(f32[8,384]{1,0:T(8,128)S(1)} %pad_maximum_fusion.2), channel_id=1, source_target_pairs={{0,16},{16,0},{32,48},{48,32},{64,80},{80,64},{96,112},{112,96},{1... | collective-permute-start | bytes 36872 | tf_op jit(solution)/shard_map/ppermute | solution.py:52
  25.5 15.0 %collective-permute-start.4 = (bf16[1024,256]{0,1:T(8,128)(2,1)S(1)}, bf16[1024,256]{0,1:T(8,128)(2,1)S(1)}, u32[]{:S(2)}, u32[]{:S(2)}) collective-permute-start(bf16[1024,256]{0,1:T(8,128)(2,1)S(1)} %collective-permute-done.1), channel_id=1, source_target_pairs={{0,15},{1,0},{2,1},{3,2},{4,3},{5,4},{6,5},{7,6},{8,7},{9,8},{10,9... | collective-permute-start | bytes 1572872 | tf_op jit(solution)/shard_map/ppermute | solution.py:50
  30.8 14.8 %collective-permute-start.3 = (bf16[1024,256]{0,1:T(8,128)(2,1)S(1)}, bf16[1024,256]{0,1:T(8,128)(2,1)S(1)}, u32[]{:S(2)}, u32[]{:S(2)}) collective-permute-start(bf16[1024,256]{0,1:T(8,128)(2,1)S(1)} %collective-permute-done), channel_id=1, source_target_pairs={{0,1},{1,2},{2,3},{3,4},{4,5},{5,6},{6,7},{7,8},{8,9},{9,10},{10,1... | collective-permute-start | bytes 1572872 | tf_op jit(solution)/shard_map/ppermute | solution.py:49
  32.8 4.7 %collective-permute-start.5 = (f32[8,384]{1,0:T(8,128)S(1)}, f32[8,384]{1,0:T(8,128)S(1)}, u32[]{:S(2)}, u32[]{:S(2)}) collective-permute-start(f32[8,384]{1,0:T(8,128)S(1)} %fusion.33), channel_id=1, source_target_pairs={{0,32},{16,48},{32,0},{48,16},{64,96},{80,112},{96,64},{112,80},{1... | collective-permute-start | bytes 36872 | tf_op jit(solution)/shard_map/ppermute | solution.py:52
  45.6 12.8 %collective-permute-start.7 = (bf16[1024,256]{0,1:T(8,128)(2,1)S(1)}, bf16[1024,256]{0,1:T(8,128)(2,1)S(1)}, u32[]{:S(2)}, u32[]{:S(2)}) collective-permute-start(bf16[1024,256]{0,1:T(8,128)(2,1)S(1)} %collective-permute-done.4), channel_id=1, source_target_pairs={{0,15},{1,0},{2,1},{3,2},{4,3},{5,4},{6,5},{7,6},{8,7},{9,8},{10,9... | collective-permute-start | bytes 1572872 | tf_op jit(solution)/shard_map/ppermute | solution.py:50
  47.5 14.0 %collective-permute-start.6 = (bf16[1024,256]{0,1:T(8,128)(2,1)S(1)}, bf16[1024,256]{0,1:T(8,128)(2,1)}, u32[]{:S(2)}, u32[]{:S(2)}) collective-permute-start(bf16[1024,256]{0,1:T(8,128)(2,1)S(1)} %collective-permute-done.3), channel_id=1, source_target_pairs={{0,1},{1,2},{2,3},{3,4},{4,5},{5,6},{6,7},{7,8},{8,9},{9,10},{10,1... | collective-permute-start | bytes 1572872 | tf_op jit(solution)/shard_map/ppermute | solution.py:49
  50.9 5.9 %collective-permute-start.8 = (f32[8,384]{1,0:T(8,128)S(1)}, f32[8,384]{1,0:T(8,128)S(1)}, u32[]{:S(2)}, u32[]{:S(2)}) collective-permute-start(f32[8,384]{1,0:T(8,128)S(1)} %add.53), channel_id=1, source_target_pairs={{0,64},{16,80},{32,96},{48,112},{64,0},{80,16},{96,32},{112,48},{1... | collective-permute-start | bytes 36872 | tf_op jit(solution)/shard_map/ppermute | solution.py:52
  61.6 11.9 %collective-permute-start.10 = (bf16[1024,256]{0,1:T(8,128)(2,1)S(1)}, bf16[1024,256]{0,1:T(8,128)(2,1)}, u32[]{:S(2)}, u32[]{:S(2)}) collective-permute-start(bf16[1024,256]{0,1:T(8,128)(2,1)S(1)} %collective-permute-done.7), channel_id=1, source_target_pairs={{0,15},{1,0},{2,1},{3,2},{4,3},{5,4},{6,5},{7,6},{8,7},{9,8},{10,9... | collective-permute-start | bytes 1572872 | tf_op jit(solution)/shard_map/ppermute | solution.py:50
  63.5 13.4 %collective-permute-start.9 = (bf16[1024,256]{0,1:T(8,128)(2,1)}, bf16[1024,256]{0,1:T(8,128)(2,1)}, u32[]{:S(2)}, u32[]{:S(2)}) collective-permute-start(bf16[1024,256]{0,1:T(8,128)(2,1)} %collective-permute-done.6), channel_id=1, source_target_pairs={{0,1},{1,2},{2,3},{3,4},{4,5},{5,6},{6,7},{7,8},{8,9},{9,10},{10,1... | collective-permute-start | bytes 1572872 | tf_op jit(solution)/shard_map/ppermute | solution.py:49
  66.9 4.8 %collective-permute-start.11 = (f32[8,384]{1,0:T(8,128)S(1)}, f32[8,384]{1,0:T(8,128)S(1)}, u32[]{:S(2)}, u32[]{:S(2)}) collective-permute-start(f32[8,384]{1,0:T(8,128)S(1)} %add.54), channel_id=1, source_target_pairs={{0,128},{16,144},{32,160},{48,176},{64,192},{80,208},{96,224},{112... | collective-permute-start | bytes 36872 | tf_op jit(solution)/shard_map/ppermute | solution.py:52
  79.1 1.3 copy-start
  83.2 1.7 %copy-start.1 = (f32[9,256,8]{1,2,0:T(8,128)}, f32[9,256,8]{1,2,0:T(8,128)S(1)}, u32[]{:S(2)}) copy-start(f32[9,256,8]{1,2,0:T(8,128)S(1)} %fusion.27) | copy-start | bytes 221188
  87.3 0.7 slice-start
  89.7 12.2 %collective-permute-start.12 = (f32[16,144,256]{2,1,0:T(8,128)}, f32[16,144,256]{2,1,0:T(8,128)}, u32[]{:S(2)}, u32[]{:S(2)}) collective-permute-start(f32[16,144,256]{2,1,0:T(8,128)} %select_maximum_fusion), channel_id=1, source_target_pairs={{0,16},{16,0},{32,48},{48,32},{64,80},{80,64},{96,112},{112,96},{1... | collective-permute-start | bytes 7077896 | tf_op jit(solution)/shard_map/ppermute | solution.py:87
  95.9 5.9 %collective-permute-start.13 = (f32[8,384]{1,0:T(8,128)S(1)}, f32[8,384]{1,0:T(8,128)S(1)}, u32[]{:S(2)}, u32[]{:S(2)}) collective-permute-start(f32[8,384]{1,0:T(8,128)S(1)} %add.55), channel_id=1, source_target_pairs={{0,256},{16,272},{32,288},{48,304},{64,320},{80,336},{96,352},{112... | collective-permute-start | bytes 36872 | tf_op jit(solution)/shard_map/ppermute | solution.py:89
  105.7 39.1 %all-to-all-start = ((f32[32,72,256]{2,1,0:T(8,128)}), f32[32,72,256]{2,1,0:T(8,128)S(1)}, u32[]{:S(2)}, u32[]{:S(2)}) async-start(f32[32,72,256]{2,1,0:T(8,128)} %bitcast.58), calls=%async_computation | async-start | bytes 4718592 | tf_op jit(solution)/shard_map/all_to_all | solution.py:96
  145.0 3.2 %collective-permute-start.14 = (f32[72,256]{1,0:T(8,128)S(1)}, f32[72,256]{1,0:T(8,128)S(1)}, u32[]{:S(2)}, u32[]{:S(2)}) collective-permute-start(f32[72,256]{1,0:T(8,128)S(1)} %get-tuple-element.37), channel_id=1, source_target_pairs={{0,16},{16,0},{32,48},{48,32},{64,80},{80,64},{96,112},{112,96},{1... | collective-permute-start | bytes 221192 | tf_op jit(solution)/shard_map/ppermute | solution.py:100
  148.2 21.6 %collective-permute-start.15 = (f32[144,256]{1,0:T(8,128)S(1)}, f32[144,256]{1,0:T(8,128)S(1)}, u32[]{:S(2)}, u32[]{:S(2)}) collective-permute-start(f32[144,256]{1,0:T(8,128)S(1)} %maximum_select_fusion), channel_id=1, source_target_pairs={{5,40},{6,72},{7,104},{8,388},{9,389},{10,390},{11,391},{21,56},{2... | collective-permute-start | bytes 442376 | tf_op jit(solution)/shard_map/ppermute | solution.py:117

commit v14 on v12

--- a/solution.py
+++ b/solution.py
@@ -43,7 +43,7 @@
     up = [(i, (i + 1) % n_t) for i in range(n_t)]
     down = [(i, (i - 1) % n_t) for i in range(n_t)]
     bfly = [1 << b for b in range(n_dp.bit_length() - 1)]
-    per_step = [bfly[i::win] for i in range(win)]
+    per_step = [bfly[:1], bfly[1:2] + bfly[win:], bfly[2:3], bfly[3:win]]
     for step in range(1, win + 1):
         fwd = lax.ppermute(fwd, "tensor", up)
         bwd = lax.ppermute(bwd, "tensor", down)

time: 168 us -> 168 us (level)
  starting transfers between devices: 67.2 us -> 69.2 us
  waiting for transfers between devices: 77.1 us -> 75.1 us
    ppermute x4, waiting for transfers between devices: 10.2 us -> 8.28 us  [body(): fwd = lax.ppermute(fwd, 'tensor', up)]
  transfers between devices with their start and end apart: 17 -> 17, of which waited for: 15 -> 16; matrix products, arithmetic and copies ran while one was open for 2% -> 2% of each run, Pallas kernels for 0% -> 0%
where the time goes in v14:
time: 168 us; the launch traced here: 167 us
  waiting for transfers between devices  75.1 us (45%)
  starting transfers between devices  69.2 us (41%)
  other arithmetic  7.67 us (5%)
  matrix products  7.64 us (5%)
  local copies, waits for them, and re-layouts  6.4 us (4%)
    all_to_all x1, waiting for transfers between devices, body(): recv = lax.all_to_all(halves, 'dp', 0, 0, tiled=True)  30.8 us
    ppermute x4, starting transfers between devices, body(): bwd = lax.ppermute(bwd, 'tensor', down)  20.8 us
    ppermute x1, waiting for transfers between devices, body(): moved = lax.ppermute(total, ('dp', 'tensor'), perm)  16.3 us
    ppermute x5, starting transfers between devices, body(): stats = stats + lax.ppermute(stats, 'dp', [(i, i ^ k) for i in range(n_dp)])  15.5 us
    ppermute x4, starting transfers between devices, body(): fwd = lax.ppermute(fwd, 'tensor', up)  11.2 us
    ppermute x5, waiting for transfers between devices, body(): stats = stats + lax.ppermute(stats, 'dp', [(i, i ^ k) for i in range(n_dp)])  9.48 us
    ppermute x4, waiting for transfers between devices, body(): fwd = lax.ppermute(fwd, 'tensor', up)  8.28 us
    all_to_all x1, starting transfers between devices, body(): recv = lax.all_to_all(halves, 'dp', 0, 0, tiled=True)  7.41 us
  transfers between devices with their start and end apart: 17, of which 16 were waited for; matrix products, arithmetic and copies ran while one was open for 2% of the time, Pallas kernels for 0%

profile of v14, /device:TPU:17, one launch (start us, length us, event | category | flops | bytes accessed | tf_op | source)
XLA Modules:
  0.0 167.0 jit_solution(789047743251544881)
XLA Ops:
  1.9 3.5 %collective-permute-start = (bf16[1024,256]{0,1:T(8,128)(2,1)S(1)}, bf16[1024,256]{0,1:T(8,128)(2,1)S(1)}, u32[]{:S(2)}, u32[]{:S(2)}) collective-permute-start(bf16[1024,256]{0,1:T(8,128)(2,1)S(1)} %copy.29), channel_id=1, source_target_pairs={{0,1},{1,2},{2,3},{3,4},{4,5},{5,6},{6,7},{7,8},{8,9},{9,10},{10,1... | collective-permute-start | bytes 1572872 | tf_op jit(solution)/shard_map/ppermute | solution.py:48
  5.4 9.5 %collective-permute-start.1 = (bf16[1024,256]{0,1:T(8,128)(2,1)S(1)}, bf16[1024,256]{0,1:T(8,128)(2,1)S(1)}, u32[]{:S(2)}, u32[]{:S(2)}) collective-permute-start(bf16[1024,256]{0,1:T(8,128)(2,1)S(1)} %copy.29), channel_id=1, source_target_pairs={{0,15},{1,0},{2,1},{3,2},{4,3},{5,4},{6,5},{7,6},{8,7},{9,8},{10,9... | collective-permute-start | bytes 1572872 | tf_op jit(solution)/shard_map/ppermute | solution.py:49
  17.1 2.9 %collective-permute-start.2 = (f32[8,384]{1,0:T(8,128)S(1)}, f32[8,384]{1,0:T(8,128)S(1)}, u32[]{:S(2)}, u32[]{:S(2)}) collective-permute-start(f32[8,384]{1,0:T(8,128)S(1)} %pad_maximum_fusion.2), channel_id=1, source_target_pairs={{0,16},{16,0},{32,48},{48,32},{64,80},{80,64},{96,112},{112,96},{1... | collective-permute-start | bytes 36872 | tf_op jit(solution)/shard_map/ppermute | solution.py:51
  20.8 3.9 %collective-permute-done = bf16[1024,256]{0,1:T(8,128)(2,1)S(1)} collective-permute-done((bf16[1024,256]{0,1:T(8,128)(2,1)S(1)}, bf16[1024,256]{0,1:T(8,128)(2,1)S(1)}, u32[]{:S(2)}, u32[]{:S(2)}) %collective-permute-start) | collective-permute-done | bytes 524320 | tf_op jit(solution)/shard_map/ppermute | solution.py:48
  25.5 5.3 %collective-permute-start.4 = (bf16[1024,256]{0,1:T(8,128)(2,1)S(1)}, bf16[1024,256]{0,1:T(8,128)(2,1)S(1)}, u32[]{:S(2)}, u32[]{:S(2)}) collective-permute-start(bf16[1024,256]{0,1:T(8,128)(2,1)S(1)} %collective-permute-done.1), channel_id=1, source_target_pairs={{0,15},{1,0},{2,1},{3,2},{4,3},{5,4},{6,5},{7,6},{8,7},{9,8},{10,9... | collective-permute-start | bytes 1572872 | tf_op jit(solution)/shard_map/ppermute | solution.py:49
  30.8 1.9 %collective-permute-start.3 = (bf16[1024,256]{0,1:T(8,128)(2,1)S(1)}, bf16[1024,256]{0,1:T(8,128)(2,1)S(1)}, u32[]{:S(2)}, u32[]{:S(2)}) collective-permute-start(bf16[1024,256]{0,1:T(8,128)(2,1)S(1)} %collective-permute-done), channel_id=1, source_target_pairs={{0,1},{1,2},{2,3},{3,4},{4,5},{5,6},{6,7},{7,8},{8,9},{9,10},{10,1... | collective-permute-start | bytes 1572872 | tf_op jit(solution)/shard_map/ppermute | solution.py:48
  32.8 3.1 %collective-permute-start.5 = (f32[8,384]{1,0:T(8,128)S(1)}, f32[8,384]{1,0:T(8,128)S(1)}, u32[]{:S(2)}, u32[]{:S(2)}) collective-permute-start(f32[8,384]{1,0:T(8,128)S(1)} %fusion.33), channel_id=1, source_target_pairs={{0,32},{16,48},{32,0},{48,16},{64,96},{80,112},{96,64},{112,80},{1... | collective-permute-start | bytes 36872 | tf_op jit(solution)/shard_map/ppermute | solution.py:51
  35.9 1.6 collective-permute-done.5
  37.5 2.0 %collective-permute-start.6 = (f32[8,384]{1,0:T(8,128)S(1)}, f32[8,384]{1,0:T(8,128)S(1)}, u32[]{:S(2)}, u32[]{:S(2)}) collective-permute-start(f32[8,384]{1,0:T(8,128)S(1)} %add.53), channel_id=1, source_target_pairs={{0,256},{16,272},{32,288},{48,304},{64,320},{80,336},{96,352},{112... | collective-permute-start | bytes 36872 | tf_op jit(solution)/shard_map/ppermute | solution.py:51
  39.5 4.3 %collective-permute-done.6 = f32[8,384]{1,0:T(8,128)S(1)} collective-permute-done((f32[8,384]{1,0:T(8,128)S(1)}, f32[8,384]{1,0:T(8,128)S(1)}, u32[]{:S(2)}, u32[]{:S(2)}) %collective-permute-start.6) | collective-permute-done | bytes 12320 | tf_op jit(solution)/shard_map/ppermute | solution.py:51
  43.7 1.9 %collective-permute-done.3 = bf16[1024,256]{0,1:T(8,128)(2,1)S(1)} collective-permute-done((bf16[1024,256]{0,1:T(8,128)(2,1)S(1)}, bf16[1024,256]{0,1:T(8,128)(2,1)S(1)}, u32[]{:S(2)}, u32[]{:S(2)}) %collective-permute-start.3) | collective-permute-done | bytes 524320 | tf_op jit(solution)/shard_map/ppermute | solution.py:48
  45.6 2.4 %collective-permute-start.8 = (bf16[1024,256]{0,1:T(8,128)(2,1)S(1)}, bf16[1024,256]{0,1:T(8,128)(2,1)S(1)}, u32[]{:S(2)}, u32[]{:S(2)}) collective-permute-start(bf16[1024,256]{0,1:T(8,128)(2,1)S(1)} %collective-permute-done.4), channel_id=1, source_target_pairs={{0,15},{1,0},{2,1},{3,2},{4,3},{5,4},{6,5},{7,6},{8,7},{9,8},{10,9... | collective-permute-start | bytes 1572872 | tf_op jit(solution)/shard_map/ppermute | solution.py:49
  48.0 2.9 %collective-permute-start.7 = (bf16[1024,256]{0,1:T(8,128)(2,1)S(1)}, bf16[1024,256]{0,1:T(8,128)(2,1)}, u32[]{:S(2)}, u32[]{:S(2)}) collective-permute-start(bf16[1024,256]{0,1:T(8,128)(2,1)S(1)} %collective-permute-done.3), channel_id=1, source_target_pairs={{0,1},{1,2},{2,3},{3,4},{4,5},{5,6},{6,7},{7,8},{8,9},{9,10},{10,1... | collective-permute-start | bytes 1572872 | tf_op jit(solution)/shard_map/ppermute | solution.py:48
  50.9 4.7 %collective-permute-start.9 = (f32[8,384]{1,0:T(8,128)S(1)}, f32[8,384]{1,0:T(8,128)S(1)}, u32[]{:S(2)}, u32[]{:S(2)}) collective-permute-start(f32[8,384]{1,0:T(8,128)S(1)} %add.54), channel_id=1, source_target_pairs={{0,64},{16,80},{32,96},{48,112},{64,0},{80,16},{96,32},{112,48},{1... | collective-permute-start | bytes 36872 | tf_op jit(solution)/shard_map/ppermute | solution.py:51
  58.3 2.0 %collective-permute-done.7 = bf16[1024,256]{0,1:T(8,128)(2,1)} collective-permute-done((bf16[1024,256]{0,1:T(8,128)(2,1)S(1)}, bf16[1024,256]{0,1:T(8,128)(2,1)}, u32[]{:S(2)}, u32[]{:S(2)}) %collective-permute-start.7) | collective-permute-done | bytes 524320 | tf_op jit(solution)/shard_map/ppermute | solution.py:48
  60.4 2.9 %collective-permute-start.10 = (bf16[1024,256]{0,1:T(8,128)(2,1)}, bf16[1024,256]{0,1:T(8,128)(2,1)}, u32[]{:S(2)}, u32[]{:S(2)}) collective-permute-start(bf16[1024,256]{0,1:T(8,128)(2,1)} %collective-permute-done.7), channel_id=1, source_target_pairs={{0,1},{1,2},{2,3},{3,4},{4,5},{5,6},{6,7},{7,8},{8,9},{9,10},{10,1... | collective-permute-start | bytes 1572872 | tf_op jit(solution)/shard_map/ppermute | solution.py:48
  63.2 3.6 %collective-permute-start.11 = (bf16[1024,256]{0,1:T(8,128)(2,1)S(1)}, bf16[1024,256]{0,1:T(8,128)(2,1)}, u32[]{:S(2)}, u32[]{:S(2)}) collective-permute-start(bf16[1024,256]{0,1:T(8,128)(2,1)S(1)} %collective-permute-done.8), channel_id=1, source_target_pairs={{0,15},{1,0},{2,1},{3,2},{4,3},{5,4},{6,5},{7,6},{8,7},{9,8},{10,9... | collective-permute-start | bytes 1572872 | tf_op jit(solution)/shard_map/ppermute | solution.py:49
  66.9 2.9 %collective-permute-start.12 = (f32[8,384]{1,0:T(8,128)S(1)}, f32[8,384]{1,0:T(8,128)S(1)}, u32[]{:S(2)}, u32[]{:S(2)}) collective-permute-start(f32[8,384]{1,0:T(8,128)S(1)} %add.55), channel_id=1, source_target_pairs={{0,128},{16,144},{32,160},{48,176},{64,192},{80,208},{96,224},{112... | collective-permute-start | bytes 36872 | tf_op jit(solution)/shard_map/ppermute | solution.py:51
  69.8 1.5 collective-permute-done.12
  71.8 2.6 %collective-permute-done.11 = bf16[1024,256]{0,1:T(8,128)(2,1)} collective-permute-done((bf16[1024,256]{0,1:T(8,128)(2,1)S(1)}, bf16[1024,256]{0,1:T(8,128)(2,1)}, u32[]{:S(2)}, u32[]{:S(2)}) %collective-permute-start.11) | collective-permute-done | bytes 524320 | tf_op jit(solution)/shard_map/ppermute | solution.py:49
  80.8 1.7 %fusion.16 = f32[3,256,256]{2,1,0:T(8,128)S(1)} fusion(bf16[1,1024,256]{1,2,0:T(8,128)(2,1)S(1)} %bitcast.63, bf16[1,1024,256]{1,2,0:T(8,128)(2,1)S(1)} %bitcast.61, bf16[1,1024,256]{1,2,0:T(8,128)(2,1)S(1)} %bitcast.59, bf16[1024,256]{0,1:T(8,128)(2,1)} %collective-permute-done.10), kind=kOutput, calls=%fused_computation.24 | convolution fusion | flops 407371776 | bytes 2883584 | tf_op jit(solution)/shard_map/dot_general | solution.py:62
  82.5 1.9 %fusion.2 = f32[4,256,256]{2,1,0:T(8,128)S(1)} fusion(bf16[1,1024,256]{1,2,0:T(8,128)(2,1)} %bitcast.8, bf16[1,1024,256]{1,2,0:T(8,128)(2,1)S(1)} %bitcast.64, bf16[1,1024,256]{1,2,0:T(8,128)(2,1)S(1)} %bitcast.62, bf16[1,1024,256]{1,2,0:T(8,128)(2,1)S(1)} %bitcast.60, bf16[1024,256]{0,1:T(8,128)(2,1)} %collective-permute-done.10), kind=kOutput, calls=%fused_computation.8 | convolution fusion | flops 540016640 | bytes 3670016 | tf_op jit(solution)/shard_map/dot_general | solution.py:58
  85.6 1.7 select_maximum_fusion
  87.2 7.0 %collective-permute-start.13 = (f32[16,144,256]{2,1,0:T(8,128)}, f32[16,144,256]{2,1,0:T(8,128)}, u32[]{:S(2)}, u32[]{:S(2)}) collective-permute-start(f32[16,144,256]{2,1,0:T(8,128)} %select_maximum_fusion), channel_id=1, source_target_pairs={{0,16},{16,0},{32,48},{48,32},{64,80},{80,64},{96,112},{112,96},{1... | collective-permute-start | bytes 7077896 | tf_op jit(solution)/shard_map/ppermute | solution.py:86
  94.3 4.4 %collective-permute-done.13 = f32[16,144,256]{2,1,0:T(8,128)} collective-permute-done((f32[16,144,256]{2,1,0:T(8,128)}, f32[16,144,256]{2,1,0:T(8,128)}, u32[]{:S(2)}, u32[]{:S(2)}) %collective-permute-start.13) | collective-permute-done | bytes 2359328 | tf_op jit(solution)/shard_map/ppermute | solution.py:86
  98.8 2.0 %fusion.1 = f32[16,144,256]{2,1,0:T(8,128)S(1)} fusion(f32[16,144,256]{2,1,0:T(8,128)} %collective-permute-done.13, f32[16,1,128]{2,1,0:T(1,128)S(1)} %get-tuple-element.34, f32[16,128,256]{2,1,0:T(8,128)S(1)} %get-tuple-element.30), kind=kLoop, calls=%fused_computation.6 | loop fusion | flops 2359296 | bytes 6823936 | tf_op jit(solution)/shard_map/add | solution.py:86
  100.7 1.9 %fusion = f32[16,144,256]{2,1,0:T(8,128)} fusion(s32[]{:T(128)S(6)} %select_n.57, f32[16,144,256]{2,1,0:T(8,128)S(1)} %fusion.1), kind=kLoop, calls=%fused_computation.3 | loop fusion | flops 589824 | bytes 4718596 | tf_op jit(solution)/shard_map/concatenate | solution.py:88
  102.6 7.4 %all-to-all-start = ((f32[32,72,256]{2,1,0:T(8,128)}), f32[32,72,256]{2,1,0:T(8,128)S(1)}, u32[]{:S(2)}, u32[]{:S(2)}) async-start(f32[32,72,256]{2,1,0:T(8,128)} %bitcast.58), calls=%async_computation | async-start | bytes 4718592 | tf_op jit(solution)/shard_map/all_to_all | solution.py:91
  110.0 30.8 %all-to-all-done = f32[32,72,256]{2,1,0:T(8,128)S(1)} async-done(((f32[32,72,256]{2,1,0:T(8,128)}), f32[32,72,256]{2,1,0:T(8,128)S(1)}, u32[]{:S(2)}, u32[]{:S(2)}) %all-to-all-start) | async-done | bytes 2359328 | tf_op jit(solution)/shard_map/all_to_all | solution.py:91
  141.0 2.3 %collective-permute-start.14 = (f32[72,256]{1,0:T(8,128)S(1)}, f32[72,256]{1,0:T(8,128)S(1)}, u32[]{:S(2)}, u32[]{:S(2)}) collective-permute-start(f32[72,256]{1,0:T(8,128)S(1)} %get-tuple-element.33), channel_id=1, source_target_pairs={{0,16},{16,0},{32,48},{48,32},{64,80},{80,64},{96,112},{112,96},{1... | collective-permute-start | bytes 221192 | tf_op jit(solution)/shard_map/ppermute | solution.py:95
  144.2 4.9 %collective-permute-start.15 = (f32[144,256]{1,0:T(8,128)S(1)}, f32[144,256]{1,0:T(8,128)S(1)}, u32[]{:S(2)}, u32[]{:S(2)}) collective-permute-start(f32[144,256]{1,0:T(8,128)S(1)} %maximum_select_fusion), channel_id=1, source_target_pairs={{5,40},{6,72},{7,104},{8,388},{9,389},{10,390},{11,391},{21,56},{2... | collective-permute-start | bytes 442376 | tf_op jit(solution)/shard_map/ppermute | solution.py:112
  149.8 16.3 %collective-permute-done.15 = f32[144,256]{1,0:T(8,128)S(1)} collective-permute-done((f32[144,256]{1,0:T(8,128)S(1)}, f32[144,256]{1,0:T(8,128)S(1)}, u32[]{:S(2)}, u32[]{:S(2)}) %collective-permute-start.15) | collective-permute-done | bytes 147488 | tf_op jit(solution)/shard_map/ppermute | solution.py:112
  (52 shorter events, 18.3 us)
Async XLA Ops:
  1.9 22.7 %collective-permute-start = (bf16[1024,256]{0,1:T(8,128)(2,1)S(1)}, bf16[1024,256]{0,1:T(8,128)(2,1)S(1)}, u32[]{:S(2)}, u32[]{:S(2)}) collective-permute-start(bf16[1024,256]{0,1:T(8,128)(2,1)S(1)} %copy.29), channel_id=1, source_target_pairs={{0,1},{1,2},{2,3},{3,4},{4,5},{5,6},{6,7},{7,8},{8,9},{9,10},{10,1... | collective-permute-start | bytes 1572872 | tf_op jit(solution)/shard_map/ppermute | solution.py:48
  5.4 20.1 %collective-permute-start.1 = (bf16[1024,256]{0,1:T(8,128)(2,1)S(1)}, bf16[1024,256]{0,1:T(8,128)(2,1)S(1)}, u32[]{:S(2)}, u32[]{:S(2)}) collective-permute-start(bf16[1024,256]{0,1:T(8,128)(2,1)S(1)} %copy.29), channel_id=1, source_target_pairs={{0,15},{1,0},{2,1},{3,2},{4,3},{5,4},{6,5},{7,6},{8,7},{9,8},{10,9... | collective-permute-start | bytes 1572872 | tf_op jit(solution)/shard_map/ppermute | solution.py:49
  17.1 3.7 %collective-permute-start.2 = (f32[8,384]{1,0:T(8,128)S(1)}, f32[8,384]{1,0:T(8,128)S(1)}, u32[]{:S(2)}, u32[]{:S(2)}) collective-permute-start(f32[8,384]{1,0:T(8,128)S(1)} %pad_maximum_fusion.2), channel_id=1, source_target_pairs={{0,16},{16,0},{32,48},{48,32},{64,80},{80,64},{96,112},{112,96},{1... | collective-permute-start | bytes 36872 | tf_op jit(solution)/shard_map/ppermute | solution.py:51
  25.5 18.2 %collective-permute-start.4 = (bf16[1024,256]{0,1:T(8,128)(2,1)S(1)}, bf16[1024,256]{0,1:T(8,128)(2,1)S(1)}, u32[]{:S(2)}, u32[]{:S(2)}) collective-permute-start(bf16[1024,256]{0,1:T(8,128)(2,1)S(1)} %collective-permute-done.1), channel_id=1, source_target_pairs={{0,15},{1,0},{2,1},{3,2},{4,3},{5,4},{6,5},{7,6},{8,7},{9,8},{10,9... | collective-permute-start | bytes 1572872 | tf_op jit(solution)/shard_map/ppermute | solution.py:49
  30.8 14.8 %collective-permute-start.3 = (bf16[1024,256]{0,1:T(8,128)(2,1)S(1)}, bf16[1024,256]{0,1:T(8,128)(2,1)S(1)}, u32[]{:S(2)}, u32[]{:S(2)}) collective-permute-start(bf16[1024,256]{0,1:T(8,128)(2,1)S(1)} %collective-permute-done), channel_id=1, source_target_pairs={{0,1},{1,2},{2,3},{3,4},{4,5},{5,6},{6,7},{7,8},{8,9},{9,10},{10,1... | collective-permute-start | bytes 1572872 | tf_op jit(solution)/shard_map/ppermute | solution.py:48
  32.8 4.7 %collective-permute-start.5 = (f32[8,384]{1,0:T(8,128)S(1)}, f32[8,384]{1,0:T(8,128)S(1)}, u32[]{:S(2)}, u32[]{:S(2)}) collective-permute-start(f32[8,384]{1,0:T(8,128)S(1)} %fusion.33), channel_id=1, source_target_pairs={{0,32},{16,48},{32,0},{48,16},{64,96},{80,112},{96,64},{112,80},{1... | collective-permute-start | bytes 36872 | tf_op jit(solution)/shard_map/ppermute | solution.py:51
  37.5 6.2 %collective-permute-start.6 = (f32[8,384]{1,0:T(8,128)S(1)}, f32[8,384]{1,0:T(8,128)S(1)}, u32[]{:S(2)}, u32[]{:S(2)}) collective-permute-start(f32[8,384]{1,0:T(8,128)S(1)} %add.53), channel_id=1, source_target_pairs={{0,256},{16,272},{32,288},{48,304},{64,320},{80,336},{96,352},{112... | collective-permute-start | bytes 36872 | tf_op jit(solution)/shard_map/ppermute | solution.py:51
  45.6 12.7 %collective-permute-start.8 = (bf16[1024,256]{0,1:T(8,128)(2,1)S(1)}, bf16[1024,256]{0,1:T(8,128)(2,1)S(1)}, u32[]{:S(2)}, u32[]{:S(2)}) collective-permute-start(bf16[1024,256]{0,1:T(8,128)(2,1)S(1)} %collective-permute-done.4), channel_id=1, source_target_pairs={{0,15},{1,0},{2,1},{3,2},{4,3},{5,4},{6,5},{7,6},{8,7},{9,8},{10,9... | collective-permute-start | bytes 1572872 | tf_op jit(solution)/shard_map/ppermute | solution.py:49
  48.0 12.3 %collective-permute-start.7 = (bf16[1024,256]{0,1:T(8,128)(2,1)S(1)}, bf16[1024,256]{0,1:T(8,128)(2,1)}, u32[]{:S(2)}, u32[]{:S(2)}) collective-permute-start(bf16[1024,256]{0,1:T(8,128)(2,1)S(1)} %collective-permute-done.3), channel_id=1, source_target_pairs={{0,1},{1,2},{2,3},{3,4},{4,5},{5,6},{6,7},{7,8},{8,9},{9,10},{10,1... | collective-permute-start | bytes 1572872 | tf_op jit(solution)/shard_map/ppermute | solution.py:48
  50.9 5.9 %collective-permute-start.9 = (f32[8,384]{1,0:T(8,128)S(1)}, f32[8,384]{1,0:T(8,128)S(1)}, u32[]{:S(2)}, u32[]{:S(2)}) collective-permute-start(f32[8,384]{1,0:T(8,128)S(1)} %add.54), channel_id=1, source_target_pairs={{0,64},{16,80},{32,96},{48,112},{64,0},{80,16},{96,32},{112,48},{1... | collective-permute-start | bytes 36872 | tf_op jit(solution)/shard_map/ppermute | solution.py:51
  60.4 11.4 %collective-permute-start.10 = (bf16[1024,256]{0,1:T(8,128)(2,1)}, bf16[1024,256]{0,1:T(8,128)(2,1)}, u32[]{:S(2)}, u32[]{:S(2)}) collective-permute-start(bf16[1024,256]{0,1:T(8,128)(2,1)} %collective-permute-done.7), channel_id=1, source_target_pairs={{0,1},{1,2},{2,3},{3,4},{4,5},{5,6},{6,7},{7,8},{8,9},{9,10},{10,1... | collective-permute-start | bytes 1572872 | tf_op jit(solution)/shard_map/ppermute | solution.py:48
  63.2 11.2 %collective-permute-start.11 = (bf16[1024,256]{0,1:T(8,128)(2,1)S(1)}, bf16[1024,256]{0,1:T(8,128)(2,1)}, u32[]{:S(2)}, u32[]{:S(2)}) collective-permute-start(bf16[1024,256]{0,1:T(8,128)(2,1)S(1)} %collective-permute-done.8), channel_id=1, source_target_pairs={{0,15},{1,0},{2,1},{3,2},{4,3},{5,4},{6,5},{7,6},{8,7},{9,8},{10,9... | collective-permute-start | bytes 1572872 | tf_op jit(solution)/shard_map/ppermute | solution.py:49
  66.9 4.4 %collective-permute-start.12 = (f32[8,384]{1,0:T(8,128)S(1)}, f32[8,384]{1,0:T(8,128)S(1)}, u32[]{:S(2)}, u32[]{:S(2)}) collective-permute-start(f32[8,384]{1,0:T(8,128)S(1)} %add.55), channel_id=1, source_target_pairs={{0,128},{16,144},{32,160},{48,176},{64,192},{80,208},{96,224},{112... | collective-permute-start | bytes 36872 | tf_op jit(solution)/shard_map/ppermute | solution.py:51
  76.6 1.3 copy-start
  80.7 1.7 %copy-start.1 = (f32[9,256,8]{1,2,0:T(8,128)}, f32[9,256,8]{1,2,0:T(8,128)S(1)}, u32[]{:S(2)}) copy-start(f32[9,256,8]{1,2,0:T(8,128)S(1)} %fusion.27) | copy-start | bytes 221188
  84.8 0.7 slice-start
  87.2 11.5 %collective-permute-start.13 = (f32[16,144,256]{2,1,0:T(8,128)}, f32[16,144,256]{2,1,0:T(8,128)}, u32[]{:S(2)}, u32[]{:S(2)}) collective-permute-start(f32[16,144,256]{2,1,0:T(8,128)} %select_maximum_fusion), channel_id=1, source_target_pairs={{0,16},{16,0},{32,48},{48,32},{64,80},{80,64},{96,112},{112,96},{1... | collective-permute-start | bytes 7077896 | tf_op jit(solution)/shard_map/ppermute | solution.py:86
  102.6 38.3 %all-to-all-start = ((f32[32,72,256]{2,1,0:T(8,128)}), f32[32,72,256]{2,1,0:T(8,128)S(1)}, u32[]{:S(2)}, u32[]{:S(2)}) async-start(f32[32,72,256]{2,1,0:T(8,128)} %bitcast.58), calls=%async_computation | async-start | bytes 4718592 | tf_op jit(solution)/shard_map/all_to_all | solution.py:91
  141.0 3.2 %collective-permute-start.14 = (f32[72,256]{1,0:T(8,128)S(1)}, f32[72,256]{1,0:T(8,128)S(1)}, u32[]{:S(2)}, u32[]{:S(2)}) collective-permute-start(f32[72,256]{1,0:T(8,128)S(1)} %get-tuple-element.33), channel_id=1, source_target_pairs={{0,16},{16,0},{32,48},{48,32},{64,80},{80,64},{96,112},{112,96},{1... | collective-permute-start | bytes 221192 | tf_op jit(solution)/shard_map/ppermute | solution.py:95
  144.2 21.9 %collective-permute-start.15 = (f32[144,256]{1,0:T(8,128)S(1)}, f32[144,256]{1,0:T(8,128)S(1)}, u32[]{:S(2)}, u32[]{:S(2)}) collective-permute-start(f32[144,256]{1,0:T(8,128)S(1)} %maximum_select_fusion), channel_id=1, source_target_pairs={{5,40},{6,72},{7,104},{8,388},{9,389},{10,390},{11,391},{21,56},{2... | collective-permute-start | bytes 442376 | tf_op jit(solution)/shard_map/ppermute | solution.py:112

commit v15 on v12

--- a/solution.py
+++ b/solution.py
@@ -89,10 +89,10 @@
     chip_sum = lax.dynamic_slice_in_dim(doubled, (n_t - shift) % n_t, n_t, axis=0)
     halves = chip_sum.reshape(n_dp, half_rows, slice_width)
     recv = lax.all_to_all(halves, "dp", 0, 0, tiled=True)
-    by_core = jnp.sum(recv.reshape(n_dp // 2, 2, half_rows, slice_width), axis=0)
-    mine = lax.dynamic_index_in_dim(by_core, core, 0, keepdims=False)
-    other = lax.dynamic_index_in_dim(by_core, 1 - core, 0, keepdims=False)
+    by_sender = recv.reshape(n_dp // 2, 2, half_rows, slice_width)
+    other = jnp.sum(lax.dynamic_index_in_dim(by_sender, 1 - core, 1, keepdims=False), axis=0)
     got = lax.ppermute(other, "dp", core_swap)
+    mine = jnp.sum(lax.dynamic_index_in_dim(by_sender, core, 1, keepdims=False), axis=0)
     total = jnp.where(
         core == 0, jnp.concatenate([mine, got], axis=0), jnp.concatenate([got, mine], axis=0)
     )

time: 168 us -> 168 us (level)
  no operation moved by 1% of the time
where the time goes in v15:
time: 168 us; the launch traced here: 167 us
  waiting for transfers between devices  77.1 us (46%)
  starting transfers between devices  67.2 us (40%)
  other arithmetic  7.73 us (5%)
  matrix products  7.65 us (5%)
  local copies, waits for them, and re-layouts  6.4 us (4%)
    all_to_all x1, waiting for transfers between devices, body(): recv = lax.all_to_all(halves, 'dp', 0, 0, tiled=True)  30.8 us
    ppermute x4, starting transfers between devices, body(): bwd = lax.ppermute(bwd, 'tensor', down)  20.1 us
    ppermute x1, waiting for transfers between devices, body(): moved = lax.ppermute(total, ('dp', 'tensor'), perm)  16 us
    ppermute x5, starting transfers between devices, body(): stats = stats + lax.ppermute(stats, 'dp', [(i, i ^ k) for i in range(n_dp)])  15.5 us
    ppermute x4, starting transfers between devices, body(): fwd = lax.ppermute(fwd, 'tensor', up)  10.7 us
    ppermute x4, waiting for transfers between devices, body(): fwd = lax.ppermute(fwd, 'tensor', up)  10.2 us
    ppermute x5, waiting for transfers between devices, body(): stats = stats + lax.ppermute(stats, 'dp', [(i, i ^ k) for i in range(n_dp)])  9.59 us
    all_to_all x1, starting transfers between devices, body(): recv = lax.all_to_all(halves, 'dp', 0, 0, tiled=True)  7.4 us
  transfers between devices with their start and end apart: 17, of which 15 were waited for; matrix products, arithmetic and copies ran while one was open for 2% of the time, Pallas kernels for 0%

profile of v15, /device:TPU:17, one launch (start us, length us, event | category | flops | bytes accessed | tf_op | source)
XLA Modules:
  0.0 167.1 jit_solution(9211906096636097354)
XLA Ops:
  1.9 3.5 %collective-permute-start = (bf16[1024,256]{0,1:T(8,128)(2,1)S(1)}, bf16[1024,256]{0,1:T(8,128)(2,1)S(1)}, u32[]{:S(2)}, u32[]{:S(2)}) collective-permute-start(bf16[1024,256]{0,1:T(8,128)(2,1)S(1)} %copy.23), channel_id=1, source_target_pairs={{0,1},{1,2},{2,3},{3,4},{4,5},{5,6},{6,7},{7,8},{8,9},{9,10},{10,1... | collective-permute-start | bytes 1572872 | tf_op jit(solution)/shard_map/ppermute | solution.py:48
  5.4 9.5 %collective-permute-start.1 = (bf16[1024,256]{0,1:T(8,128)(2,1)S(1)}, bf16[1024,256]{0,1:T(8,128)(2,1)S(1)}, u32[]{:S(2)}, u32[]{:S(2)}) collective-permute-start(bf16[1024,256]{0,1:T(8,128)(2,1)S(1)} %copy.23), channel_id=1, source_target_pairs={{0,15},{1,0},{2,1},{3,2},{4,3},{5,4},{6,5},{7,6},{8,7},{9,8},{10,9... | collective-permute-start | bytes 1572872 | tf_op jit(solution)/shard_map/ppermute | solution.py:49
  17.1 2.9 %collective-permute-start.2 = (f32[8,384]{1,0:T(8,128)S(1)}, f32[8,384]{1,0:T(8,128)S(1)}, u32[]{:S(2)}, u32[]{:S(2)}) collective-permute-start(f32[8,384]{1,0:T(8,128)S(1)} %pad_maximum_fusion.2), channel_id=1, source_target_pairs={{0,16},{16,0},{32,48},{48,32},{64,80},{80,64},{96,112},{112,96},{1... | collective-permute-start | bytes 36872 | tf_op jit(solution)/shard_map/ppermute | solution.py:51
  20.8 2.0 %collective-permute-start.3 = (f32[8,384]{1,0:T(8,128)S(1)}, f32[8,384]{1,0:T(8,128)S(1)}, u32[]{:S(2)}, u32[]{:S(2)}) collective-permute-start(f32[8,384]{1,0:T(8,128)S(1)} %fusion.33), channel_id=1, source_target_pairs={{0,256},{16,272},{32,288},{48,304},{64,320},{80,336},{96,352},{112... | collective-permute-start | bytes 36872 | tf_op jit(solution)/shard_map/ppermute | solution.py:51
  22.7 4.0 %collective-permute-done.3 = f32[8,384]{1,0:T(8,128)S(1)} collective-permute-done((f32[8,384]{1,0:T(8,128)S(1)}, f32[8,384]{1,0:T(8,128)S(1)}, u32[]{:S(2)}, u32[]{:S(2)}) %collective-permute-start.3) | collective-permute-done | bytes 12320 | tf_op jit(solution)/shard_map/ppermute | solution.py:51
  26.7 4.1 %collective-permute-start.5 = (bf16[1024,256]{0,1:T(8,128)(2,1)S(1)}, bf16[1024,256]{0,1:T(8,128)(2,1)S(1)}, u32[]{:S(2)}, u32[]{:S(2)}) collective-permute-start(bf16[1024,256]{0,1:T(8,128)(2,1)S(1)} %collective-permute-done.1), channel_id=1, source_target_pairs={{0,15},{1,0},{2,1},{3,2},{4,3},{5,4},{6,5},{7,6},{8,7},{9,8},{10,9... | collective-permute-start | bytes 1572872 | tf_op jit(solution)/shard_map/ppermute | solution.py:49
  30.8 1.9 %collective-permute-start.4 = (bf16[1024,256]{0,1:T(8,128)(2,1)S(1)}, bf16[1024,256]{0,1:T(8,128)(2,1)S(1)}, u32[]{:S(2)}, u32[]{:S(2)}) collective-permute-start(bf16[1024,256]{0,1:T(8,128)(2,1)S(1)} %collective-permute-done), channel_id=1, source_target_pairs={{0,1},{1,2},{2,3},{3,4},{4,5},{5,6},{6,7},{7,8},{8,9},{9,10},{10,1... | collective-permute-start | bytes 1572872 | tf_op jit(solution)/shard_map/ppermute | solution.py:48
  32.8 3.1 %collective-permute-start.6 = (f32[8,384]{1,0:T(8,128)S(1)}, f32[8,384]{1,0:T(8,128)S(1)}, u32[]{:S(2)}, u32[]{:S(2)}) collective-permute-start(f32[8,384]{1,0:T(8,128)S(1)} %add.53), channel_id=1, source_target_pairs={{0,32},{16,48},{32,0},{48,16},{64,96},{80,112},{96,64},{112,80},{1... | collective-permute-start | bytes 36872 | tf_op jit(solution)/shard_map/ppermute | solution.py:51
  35.9 1.6 collective-permute-done.6
  37.5 3.1 %collective-permute-done.5 = bf16[1024,256]{0,1:T(8,128)(2,1)S(1)} collective-permute-done((bf16[1024,256]{0,1:T(8,128)(2,1)S(1)}, bf16[1024,256]{0,1:T(8,128)(2,1)S(1)}, u32[]{:S(2)}, u32[]{:S(2)}) %collective-permute-start.5) | collective-permute-done | bytes 524320 | tf_op jit(solution)/shard_map/ppermute | solution.py:49
  40.6 5.0 %collective-permute-done.4 = bf16[1024,256]{0,1:T(8,128)(2,1)S(1)} collective-permute-done((bf16[1024,256]{0,1:T(8,128)(2,1)S(1)}, bf16[1024,256]{0,1:T(8,128)(2,1)S(1)}, u32[]{:S(2)}, u32[]{:S(2)}) %collective-permute-start.4) | collective-permute-done | bytes 524320 | tf_op jit(solution)/shard_map/ppermute | solution.py:48
  45.6 1.9 %collective-permute-start.8 = (bf16[1024,256]{0,1:T(8,128)(2,1)S(1)}, bf16[1024,256]{0,1:T(8,128)(2,1)S(1)}, u32[]{:S(2)}, u32[]{:S(2)}) collective-permute-start(bf16[1024,256]{0,1:T(8,128)(2,1)S(1)} %collective-permute-done.5), channel_id=1, source_target_pairs={{0,15},{1,0},{2,1},{3,2},{4,3},{5,4},{6,5},{7,6},{8,7},{9,8},{10,9... | collective-permute-start | bytes 1572872 | tf_op jit(solution)/shard_map/ppermute | solution.py:49
  47.5 3.4 %collective-permute-start.7 = (bf16[1024,256]{0,1:T(8,128)(2,1)S(1)}, bf16[1024,256]{0,1:T(8,128)(2,1)}, u32[]{:S(2)}, u32[]{:S(2)}) collective-permute-start(bf16[1024,256]{0,1:T(8,128)(2,1)S(1)} %collective-permute-done.4), channel_id=1, source_target_pairs={{0,1},{1,2},{2,3},{3,4},{4,5},{5,6},{6,7},{7,8},{8,9},{9,10},{10,1... | collective-permute-start | bytes 1572872 | tf_op jit(solution)/shard_map/ppermute | solution.py:48
  50.9 4.7 %collective-permute-start.9 = (f32[8,384]{1,0:T(8,128)S(1)}, f32[8,384]{1,0:T(8,128)S(1)}, u32[]{:S(2)}, u32[]{:S(2)}) collective-permute-start(f32[8,384]{1,0:T(8,128)S(1)} %add.54), channel_id=1, source_target_pairs={{0,64},{16,80},{32,96},{48,112},{64,0},{80,16},{96,32},{112,48},{1... | collective-permute-start | bytes 36872 | tf_op jit(solution)/shard_map/ppermute | solution.py:51
  58.4 3.1 %collective-permute-done.7 = bf16[1024,256]{0,1:T(8,128)(2,1)} collective-permute-done((bf16[1024,256]{0,1:T(8,128)(2,1)S(1)}, bf16[1024,256]{0,1:T(8,128)(2,1)}, u32[]{:S(2)}, u32[]{:S(2)}) %collective-permute-start.7) | collective-permute-done | bytes 524320 | tf_op jit(solution)/shard_map/ppermute | solution.py:48
  61.6 1.9 %collective-permute-start.10 = (bf16[1024,256]{0,1:T(8,128)(2,1)}, bf16[1024,256]{0,1:T(8,128)(2,1)}, u32[]{:S(2)}, u32[]{:S(2)}) collective-permute-start(bf16[1024,256]{0,1:T(8,128)(2,1)} %collective-permute-done.7), channel_id=1, source_target_pairs={{0,1},{1,2},{2,3},{3,4},{4,5},{5,6},{6,7},{7,8},{8,9},{9,10},{10,1... | collective-permute-start | bytes 1572872 | tf_op jit(solution)/shard_map/ppermute | solution.py:48
  63.5 4.6 %collective-permute-start.11 = (bf16[1024,256]{0,1:T(8,128)(2,1)S(1)}, bf16[1024,256]{0,1:T(8,128)(2,1)}, u32[]{:S(2)}, u32[]{:S(2)}) collective-permute-start(bf16[1024,256]{0,1:T(8,128)(2,1)S(1)} %collective-permute-done.8), channel_id=1, source_target_pairs={{0,15},{1,0},{2,1},{3,2},{4,3},{5,4},{6,5},{7,6},{8,7},{9,8},{10,9... | collective-permute-start | bytes 1572872 | tf_op jit(solution)/shard_map/ppermute | solution.py:49
  68.1 2.9 %collective-permute-start.12 = (f32[8,384]{1,0:T(8,128)S(1)}, f32[8,384]{1,0:T(8,128)S(1)}, u32[]{:S(2)}, u32[]{:S(2)}) collective-permute-start(f32[8,384]{1,0:T(8,128)S(1)} %add.55), channel_id=1, source_target_pairs={{0,128},{16,144},{32,160},{48,176},{64,192},{80,208},{96,224},{112... | collective-permute-start | bytes 36872 | tf_op jit(solution)/shard_map/ppermute | solution.py:51
  71.0 1.9 %collective-permute-done.12 = f32[8,384]{1,0:T(8,128)S(1)} collective-permute-done((f32[8,384]{1,0:T(8,128)S(1)}, f32[8,384]{1,0:T(8,128)S(1)}, u32[]{:S(2)}, u32[]{:S(2)}) %collective-permute-start.12) | collective-permute-done | bytes 12320 | tf_op jit(solution)/shard_map/ppermute | solution.py:51
  72.9 2.0 %collective-permute-done.10 = bf16[1024,256]{0,1:T(8,128)(2,1)} collective-permute-done((bf16[1024,256]{0,1:T(8,128)(2,1)}, bf16[1024,256]{0,1:T(8,128)(2,1)}, u32[]{:S(2)}, u32[]{:S(2)}) %collective-permute-start.10) | collective-permute-done | bytes 524320 | tf_op jit(solution)/shard_map/ppermute | solution.py:48
  81.9 1.7 %fusion.16 = f32[3,256,256]{2,1,0:T(8,128)S(1)} fusion(bf16[1,1024,256]{1,2,0:T(8,128)(2,1)S(1)} %bitcast.59, bf16[1,1024,256]{1,2,0:T(8,128)(2,1)S(1)} %bitcast.57, bf16[1,1024,256]{1,2,0:T(8,128)(2,1)S(1)} %bitcast.55, bf16[1024,256]{0,1:T(8,128)(2,1)} %collective-permute-done.10), kind=kOutput, calls=%fused_computation.24 | convolution fusion | flops 407371776 | bytes 2883584 | tf_op jit(solution)/shard_map/dot_general | solution.py:62
  83.6 2.0 %fusion.2 = f32[4,256,256]{2,1,0:T(8,128)S(1)} fusion(bf16[1,1024,256]{1,2,0:T(8,128)(2,1)} %bitcast.8, bf16[1,1024,256]{1,2,0:T(8,128)(2,1)S(1)} %bitcast.60, bf16[1,1024,256]{1,2,0:T(8,128)(2,1)S(1)} %bitcast.58, bf16[1,1024,256]{1,2,0:T(8,128)(2,1)S(1)} %bitcast.56, bf16[1024,256]{0,1:T(8,128)(2,1)} %collective-permute-done.10), kind=kOutput, calls=%fused_computation.8 | convolution fusion | flops 540016640 | bytes 3670016 | tf_op jit(solution)/shard_map/dot_general | solution.py:58
  86.7 1.7 select_maximum_fusion
  88.4 6.6 %collective-permute-start.13 = (f32[16,144,256]{2,1,0:T(8,128)}, f32[16,144,256]{2,1,0:T(8,128)}, u32[]{:S(2)}, u32[]{:S(2)}) collective-permute-start(f32[16,144,256]{2,1,0:T(8,128)} %select_maximum_fusion), channel_id=1, source_target_pairs={{0,16},{16,0},{32,48},{48,32},{64,80},{80,64},{96,112},{112,96},{1... | collective-permute-start | bytes 7077896 | tf_op jit(solution)/shard_map/ppermute | solution.py:86
  95.0 4.4 %collective-permute-done.13 = f32[16,144,256]{2,1,0:T(8,128)} collective-permute-done((f32[16,144,256]{2,1,0:T(8,128)}, f32[16,144,256]{2,1,0:T(8,128)}, u32[]{:S(2)}, u32[]{:S(2)}) %collective-permute-start.13) | collective-permute-done | bytes 2359328 | tf_op jit(solution)/shard_map/ppermute | solution.py:86
  99.4 2.0 %fusion.1 = f32[16,144,256]{2,1,0:T(8,128)S(1)} fusion(f32[16,144,256]{2,1,0:T(8,128)} %collective-permute-done.13, f32[16,1,128]{2,1,0:T(1,128)S(1)} %get-tuple-element.34, f32[16,128,256]{2,1,0:T(8,128)S(1)} %get-tuple-element.32), kind=kLoop, calls=%fused_computation.6 | loop fusion | flops 2359296 | bytes 6823936 | tf_op jit(solution)/shard_map/add | solution.py:86
  101.4 1.8 %fusion = f32[16,144,256]{2,1,0:T(8,128)} fusion(s32[]{:T(128)S(6)} %select_n.57, f32[16,144,256]{2,1,0:T(8,128)S(1)} %fusion.1), kind=kLoop, calls=%fused_computation.3 | loop fusion | flops 589824 | bytes 4718596 | tf_op jit(solution)/shard_map/concatenate | solution.py:88
  103.2 7.4 %all-to-all-start = ((f32[32,72,256]{2,1,0:T(8,128)}), f32[32,72,256]{2,1,0:T(8,128)S(1)}, u32[]{:S(2)}, u32[]{:S(2)}) async-start(f32[32,72,256]{2,1,0:T(8,128)} %bitcast.54), calls=%async_computation | async-start | bytes 4718592 | tf_op jit(solution)/shard_map/all_to_all | solution.py:91
  110.7 30.8 %all-to-all-done = f32[32,72,256]{2,1,0:T(8,128)S(1)} async-done(((f32[32,72,256]{2,1,0:T(8,128)}), f32[32,72,256]{2,1,0:T(8,128)S(1)}, u32[]{:S(2)}, u32[]{:S(2)}) %all-to-all-start) | async-done | bytes 2359328 | tf_op jit(solution)/shard_map/all_to_all | solution.py:91
  141.7 2.3 %collective-permute-start.14 = (f32[72,256]{1,0:T(8,128)S(1)}, f32[72,256]{1,0:T(8,128)S(1)}, u32[]{:S(2)}, u32[]{:S(2)}) collective-permute-start(f32[72,256]{1,0:T(8,128)S(1)} %get-tuple-element.31), channel_id=1, source_target_pairs={{0,16},{16,0},{32,48},{48,32},{64,80},{80,64},{96,112},{112,96},{1... | collective-permute-start | bytes 221192 | tf_op jit(solution)/shard_map/ppermute | solution.py:94
  144.9 4.6 %collective-permute-start.15 = (f32[144,256]{1,0:T(8,128)S(1)}, f32[144,256]{1,0:T(8,128)S(1)}, u32[]{:S(2)}, u32[]{:S(2)}) collective-permute-start(f32[144,256]{1,0:T(8,128)S(1)} %maximum_select_fusion), channel_id=1, source_target_pairs={{5,40},{6,72},{7,104},{8,388},{9,389},{10,390},{11,391},{21,56},{2... | collective-permute-start | bytes 442376 | tf_op jit(solution)/shard_map/ppermute | solution.py:112
  150.2 16.0 %collective-permute-done.15 = f32[144,256]{1,0:T(8,128)S(1)} collective-permute-done((f32[144,256]{1,0:T(8,128)S(1)}, f32[144,256]{1,0:T(8,128)S(1)}, u32[]{:S(2)}, u32[]{:S(2)}) %collective-permute-start.15) | collective-permute-done | bytes 147488 | tf_op jit(solution)/shard_map/ppermute | solution.py:112
  (51 shorter events, 17.7 us)
Async XLA Ops:
  1.9 24.8 %collective-permute-start = (bf16[1024,256]{0,1:T(8,128)(2,1)S(1)}, bf16[1024,256]{0,1:T(8,128)(2,1)S(1)}, u32[]{:S(2)}, u32[]{:S(2)}) collective-permute-start(bf16[1024,256]{0,1:T(8,128)(2,1)S(1)} %copy.23), channel_id=1, source_target_pairs={{0,1},{1,2},{2,3},{3,4},{4,5},{5,6},{6,7},{7,8},{8,9},{9,10},{10,1... | collective-permute-start | bytes 1572872 | tf_op jit(solution)/shard_map/ppermute | solution.py:48
  5.4 21.3 %collective-permute-start.1 = (bf16[1024,256]{0,1:T(8,128)(2,1)S(1)}, bf16[1024,256]{0,1:T(8,128)(2,1)S(1)}, u32[]{:S(2)}, u32[]{:S(2)}) collective-permute-start(bf16[1024,256]{0,1:T(8,128)(2,1)S(1)} %copy.23), channel_id=1, source_target_pairs={{0,15},{1,0},{2,1},{3,2},{4,3},{5,4},{6,5},{7,6},{8,7},{9,8},{10,9... | collective-permute-start | bytes 1572872 | tf_op jit(solution)/shard_map/ppermute | solution.py:49
  17.1 3.7 %collective-permute-start.2 = (f32[8,384]{1,0:T(8,128)S(1)}, f32[8,384]{1,0:T(8,128)S(1)}, u32[]{:S(2)}, u32[]{:S(2)}) collective-permute-start(f32[8,384]{1,0:T(8,128)S(1)} %pad_maximum_fusion.2), channel_id=1, source_target_pairs={{0,16},{16,0},{32,48},{48,32},{64,80},{80,64},{96,112},{112,96},{1... | collective-permute-start | bytes 36872 | tf_op jit(solution)/shard_map/ppermute | solution.py:51
  20.8 5.9 %collective-permute-start.3 = (f32[8,384]{1,0:T(8,128)S(1)}, f32[8,384]{1,0:T(8,128)S(1)}, u32[]{:S(2)}, u32[]{:S(2)}) collective-permute-start(f32[8,384]{1,0:T(8,128)S(1)} %fusion.33), channel_id=1, source_target_pairs={{0,256},{16,272},{32,288},{48,304},{64,320},{80,336},{96,352},{112... | collective-permute-start | bytes 36872 | tf_op jit(solution)/shard_map/ppermute | solution.py:51
  26.7 13.9 %collective-permute-start.5 = (bf16[1024,256]{0,1:T(8,128)(2,1)S(1)}, bf16[1024,256]{0,1:T(8,128)(2,1)S(1)}, u32[]{:S(2)}, u32[]{:S(2)}) collective-permute-start(bf16[1024,256]{0,1:T(8,128)(2,1)S(1)} %collective-permute-done.1), channel_id=1, source_target_pairs={{0,15},{1,0},{2,1},{3,2},{4,3},{5,4},{6,5},{7,6},{8,7},{9,8},{10,9... | collective-permute-start | bytes 1572872 | tf_op jit(solution)/shard_map/ppermute | solution.py:49
  30.8 14.8 %collective-permute-start.4 = (bf16[1024,256]{0,1:T(8,128)(2,1)S(1)}, bf16[1024,256]{0,1:T(8,128)(2,1)S(1)}, u32[]{:S(2)}, u32[]{:S(2)}) collective-permute-start(bf16[1024,256]{0,1:T(8,128)(2,1)S(1)} %collective-permute-done), channel_id=1, source_target_pairs={{0,1},{1,2},{2,3},{3,4},{4,5},{5,6},{6,7},{7,8},{8,9},{9,10},{10,1... | collective-permute-start | bytes 1572872 | tf_op jit(solution)/shard_map/ppermute | solution.py:48
  32.8 4.7 %collective-permute-start.6 = (f32[8,384]{1,0:T(8,128)S(1)}, f32[8,384]{1,0:T(8,128)S(1)}, u32[]{:S(2)}, u32[]{:S(2)}) collective-permute-start(f32[8,384]{1,0:T(8,128)S(1)} %add.53), channel_id=1, source_target_pairs={{0,32},{16,48},{32,0},{48,16},{64,96},{80,112},{96,64},{112,80},{1... | collective-permute-start | bytes 36872 | tf_op jit(solution)/shard_map/ppermute | solution.py:51
  45.6 12.8 %collective-permute-start.8 = (bf16[1024,256]{0,1:T(8,128)(2,1)S(1)}, bf16[1024,256]{0,1:T(8,128)(2,1)S(1)}, u32[]{:S(2)}, u32[]{:S(2)}) collective-permute-start(bf16[1024,256]{0,1:T(8,128)(2,1)S(1)} %collective-permute-done.5), channel_id=1, source_target_pairs={{0,15},{1,0},{2,1},{3,2},{4,3},{5,4},{6,5},{7,6},{8,7},{9,8},{10,9... | collective-permute-start | bytes 1572872 | tf_op jit(solution)/shard_map/ppermute | solution.py:49
  47.5 14.0 %collective-permute-start.7 = (bf16[1024,256]{0,1:T(8,128)(2,1)S(1)}, bf16[1024,256]{0,1:T(8,128)(2,1)}, u32[]{:S(2)}, u32[]{:S(2)}) collective-permute-start(bf16[1024,256]{0,1:T(8,128)(2,1)S(1)} %collective-permute-done.4), channel_id=1, source_target_pairs={{0,1},{1,2},{2,3},{3,4},{4,5},{5,6},{6,7},{7,8},{8,9},{9,10},{10,1... | collective-permute-start | bytes 1572872 | tf_op jit(solution)/shard_map/ppermute | solution.py:48
  50.9 5.9 %collective-permute-start.9 = (f32[8,384]{1,0:T(8,128)S(1)}, f32[8,384]{1,0:T(8,128)S(1)}, u32[]{:S(2)}, u32[]{:S(2)}) collective-permute-start(f32[8,384]{1,0:T(8,128)S(1)} %add.54), channel_id=1, source_target_pairs={{0,64},{16,80},{32,96},{48,112},{64,0},{80,16},{96,32},{112,48},{1... | collective-permute-start | bytes 36872 | tf_op jit(solution)/shard_map/ppermute | solution.py:51
  61.6 13.4 %collective-permute-start.10 = (bf16[1024,256]{0,1:T(8,128)(2,1)}, bf16[1024,256]{0,1:T(8,128)(2,1)}, u32[]{:S(2)}, u32[]{:S(2)}) collective-permute-start(bf16[1024,256]{0,1:T(8,128)(2,1)} %collective-permute-done.7), channel_id=1, source_target_pairs={{0,1},{1,2},{2,3},{3,4},{4,5},{5,6},{6,7},{7,8},{8,9},{9,10},{10,1... | collective-permute-start | bytes 1572872 | tf_op jit(solution)/shard_map/ppermute | solution.py:48
  63.5 12.0 %collective-permute-start.11 = (bf16[1024,256]{0,1:T(8,128)(2,1)S(1)}, bf16[1024,256]{0,1:T(8,128)(2,1)}, u32[]{:S(2)}, u32[]{:S(2)}) collective-permute-start(bf16[1024,256]{0,1:T(8,128)(2,1)S(1)} %collective-permute-done.8), channel_id=1, source_target_pairs={{0,15},{1,0},{2,1},{3,2},{4,3},{5,4},{6,5},{7,6},{8,7},{9,8},{10,9... | collective-permute-start | bytes 1572872 | tf_op jit(solution)/shard_map/ppermute | solution.py:49
  68.1 4.8 %collective-permute-start.12 = (f32[8,384]{1,0:T(8,128)S(1)}, f32[8,384]{1,0:T(8,128)S(1)}, u32[]{:S(2)}, u32[]{:S(2)}) collective-permute-start(f32[8,384]{1,0:T(8,128)S(1)} %add.55), channel_id=1, source_target_pairs={{0,128},{16,144},{32,160},{48,176},{64,192},{80,208},{96,224},{112... | collective-permute-start | bytes 36872 | tf_op jit(solution)/shard_map/ppermute | solution.py:51
  77.8 1.3 copy-start
  81.9 1.7 %copy-start.1 = (f32[9,256,8]{1,2,0:T(8,128)}, f32[9,256,8]{1,2,0:T(8,128)S(1)}, u32[]{:S(2)}) copy-start(f32[9,256,8]{1,2,0:T(8,128)S(1)} %fusion.27) | copy-start | bytes 221188
  86.0 0.7 slice-start
  88.4 11.0 %collective-permute-start.13 = (f32[16,144,256]{2,1,0:T(8,128)}, f32[16,144,256]{2,1,0:T(8,128)}, u32[]{:S(2)}, u32[]{:S(2)}) collective-permute-start(f32[16,144,256]{2,1,0:T(8,128)} %select_maximum_fusion), channel_id=1, source_target_pairs={{0,16},{16,0},{32,48},{48,32},{64,80},{80,64},{96,112},{112,96},{1... | collective-permute-start | bytes 7077896 | tf_op jit(solution)/shard_map/ppermute | solution.py:86
  103.2 38.3 %all-to-all-start = ((f32[32,72,256]{2,1,0:T(8,128)}), f32[32,72,256]{2,1,0:T(8,128)S(1)}, u32[]{:S(2)}, u32[]{:S(2)}) async-start(f32[32,72,256]{2,1,0:T(8,128)} %bitcast.54), calls=%async_computation | async-start | bytes 4718592 | tf_op jit(solution)/shard_map/all_to_all | solution.py:91
  141.7 3.2 %collective-permute-start.14 = (f32[72,256]{1,0:T(8,128)S(1)}, f32[72,256]{1,0:T(8,128)S(1)}, u32[]{:S(2)}, u32[]{:S(2)}) collective-permute-start(f32[72,256]{1,0:T(8,128)S(1)} %get-tuple-element.31), channel_id=1, source_target_pairs={{0,16},{16,0},{32,48},{48,32},{64,80},{80,64},{96,112},{112,96},{1... | collective-permute-start | bytes 221192 | tf_op jit(solution)/shard_map/ppermute | solution.py:94
  144.9 21.3 %collective-permute-start.15 = (f32[144,256]{1,0:T(8,128)S(1)}, f32[144,256]{1,0:T(8,128)S(1)}, u32[]{:S(2)}, u32[]{:S(2)}) collective-permute-start(f32[144,256]{1,0:T(8,128)S(1)} %maximum_select_fusion), channel_id=1, source_target_pairs={{5,40},{6,72},{7,104},{8,388},{9,389},{10,390},{11,391},{21,56},{2... | collective-permute-start | bytes 442376 | tf_op jit(solution)/shard_map/ppermute | solution.py:112
